TPU v7x, 32 devices: a whole 2x2x4 slice. The times are simulated.
32 devices in a mesh: ctx: 16 (over z, y, core), grp: 2 (over x).
Axes of the slice: x: 2, y: 2, z: 4, core: 2. Of those that a mesh axis runs over, the one named last changes fastest.
Arguments:
- projected: bfloat16 [4096, 6144], P(('ctx', 'grp')), may hold values from -6 to 6
- conv_weight: float32 [3, 6144], replicated, may hold values from -2.5 to 2.5
- skip_gain: float32 [2048], replicated, may hold values from 0.5 to 1.5
- spectrum_real: bfloat16 [32, 256, 2048], P('ctx', None, 'grp'), may hold values from -6 to 6
- spectrum_imag: bfloat16 [32, 256, 2048], P('ctx', None, 'grp'), may hold values from -6 to 6
Outputs:
- mixer_out: bfloat16 [4096, 2048], P(('ctx', 'grp'))
All inputs are finite; a program needn't handle non-finite values.
Results may differ from a plain program's by a relative error of at most 0.0065.
Values may be sent and summed in bfloat16 or wider, within the bound.
No kernel may reach another device: no remote copies, remote signals or barrier semaphores. Data moves between devices by JAX's collectives and lax.ppermute only.
A program may use at most 64 MiB of HBM per device.

v0:
```python
import math

import jax
import jax.numpy as jnp
from jax import lax
from jax.sharding import PartitionSpec as P

TWO_PI = 2.0 * math.pi


def shifted(shard, axis, by):
    devices = lax.axis_size(axis)
    pairs = [(i, i + by) for i in range(devices) if 0 <= i + by < devices]
    return lax.ppermute(shard, axis, pairs)


def rotation(rows_index, cols_index, length, direction):
    product = rows_index[:, None] * cols_index[None, :] % length
    angles = product.astype(jnp.float32) * (TWO_PI / length)
    return (jnp.cos(angles), direction * jnp.sin(angles))


def complex_table(cos_part, sin_part):
    return jnp.stack([jnp.stack([cos_part, -sin_part]), jnp.stack([sin_part, cos_part])])


def contract(form, table, data):
    return jnp.einsum(
        form, table, data, precision=lax.Precision.HIGHEST, preferred_element_type=jnp.float32
    )


def twist(data, turn_real, turn_imag):
    return jnp.stack(
        [data[0] * turn_real - data[1] * turn_imag, data[0] * turn_imag + data[1] * turn_real]
    )


def across_forward(blocks, token_index, fft_len):
    block_count = blocks.shape[0]
    frequency = jnp.arange(2 * block_count, dtype=jnp.int32)
    block_order = jnp.arange(block_count, dtype=jnp.int32)
    cos_table, sin_table = rotation(frequency, block_order, 2 * block_count, -1.0)
    accum = contract("pkj,jbc->pkbc", jnp.stack([cos_table, sin_table]), blocks)
    turn_real, turn_imag = rotation(frequency, token_index, fft_len, -1.0)
    return twist(accum, turn_real[:, :, None], turn_imag[:, :, None])


def within_block(data, direction):
    leading, length, lane_count = (data.shape[1], data.shape[2], data.shape[3])
    first_len = math.gcd(length, 256)
    second_len = length // first_len
    data = data.reshape(2, leading, second_len, first_len, lane_count)
    outer_index = jnp.arange(second_len, dtype=jnp.int32)
    inner_index = jnp.arange(first_len, dtype=jnp.int32)
    table_real, table_imag = rotation(outer_index, outer_index, second_len, direction)
    section = contract("pqkj,qxjbc->pxkbc", complex_table(table_real, table_imag), data)
    turn_real, turn_imag = rotation(outer_index, inner_index, length, direction)
    twisted = twist(section, turn_real[None, :, :, None], turn_imag[None, :, :, None])
    last_real, last_imag = rotation(inner_index, inner_index, first_len, direction)
    result = contract("pqgb,qxkbc->pxgkc", complex_table(last_real, last_imag), twisted)
    return result.reshape(2, leading, length, lane_count)


def across_inverse(data, fft_len):
    block_count = data.shape[1] // 2
    block_order = jnp.arange(block_count, dtype=jnp.int32)
    frequency = jnp.arange(2 * block_count, dtype=jnp.int32)
    cos_table, sin_table = rotation(block_order, frequency, 2 * block_count, 1.0)
    summed = contract("qjk,qkbc->jbc", jnp.stack([cos_table, -sin_table]), data)
    return summed * (1.0 / fft_len)


def per_device(projected, conv_weight, skip_gain, spectrum_real, spectrum_imag):
    channels = conv_weight.shape[1] // 3
    rim_rows = conv_weight.shape[0] - 1
    row_count = projected.shape[0]
    rim = shifted(projected[row_count - rim_rows :], ("ctx", "grp"), 1)
    extended = jnp.concatenate([rim, projected], axis=0)
    short = jnp.zeros((row_count, 3 * channels), jnp.float32)
    for offset in range(rim_rows + 1):
        short = short + conv_weight[offset] * extended[
            rim_rows - offset : rim_rows - offset + row_count
        ].astype(jnp.float32)
    short = short.astype(jnp.bfloat16)
    query = short[:, :channels]
    gated = short[:, channels : 2 * channels].astype(jnp.float32) * short[:, 2 * channels :].astype(
        jnp.float32
    )
    block_count = lax.axis_size("ctx")
    group_count = lax.axis_size("grp")
    block_len = row_count * group_count
    fft_len = 2 * block_len * block_count
    block_index = lax.axis_index("ctx")
    sliver = lax.all_to_all(gated, "grp", split_axis=1, concat_axis=0, tiled=True)
    piece_len = block_len // block_count
    token_index = block_index * piece_len + jnp.arange(piece_len, dtype=jnp.int32)
    front = across_forward(
        lax.all_to_all(sliver[None], "ctx", split_axis=1, concat_axis=0, tiled=True),
        token_index,
        fft_len,
    )
    spectra = within_block(
        lax.all_to_all(front, "ctx", split_axis=1, concat_axis=2, tiled=True), -1.0
    )
    filtered = twist(spectra, spectrum_real.astype(jnp.float32), spectrum_imag.astype(jnp.float32))
    restored = within_block(filtered, 1.0)
    local_freq = spectra.shape[1]
    frequency = block_index * local_freq + jnp.arange(local_freq, dtype=jnp.int32)
    turn_real, turn_imag = rotation(frequency, jnp.arange(block_len, dtype=jnp.int32), fft_len, 1.0)
    restored = twist(restored, turn_real[:, :, None], turn_imag[:, :, None])
    long_blocks = across_inverse(
        lax.all_to_all(restored, "ctx", split_axis=2, concat_axis=1, tiled=True), fft_len
    )
    long_sliver = lax.all_to_all(long_blocks, "ctx", split_axis=0, concat_axis=1, tiled=True)[0]
    long_tokens = lax.all_to_all(long_sliver, "grp", split_axis=0, concat_axis=1, tiled=True)
    mixed = query.astype(jnp.float32) * (long_tokens + skip_gain * gated)
    return mixed.astype(jnp.bfloat16)


def short_convolution(projected, conv_weight):
    channels = conv_weight.shape[1] // 3
    rim_rows = conv_weight.shape[0] - 1
    row_count = projected.shape[0]
    rim = shifted(projected[row_count - rim_rows :], ("ctx", "grp"), 1)
    extended = jnp.concatenate([rim, projected], axis=0)
    short = jnp.zeros((row_count, 3 * channels), jnp.float32)
    for offset in range(rim_rows + 1):
        short = short + conv_weight[offset] * extended[
            rim_rows - offset : rim_rows - offset + row_count
        ].astype(jnp.float32)
    short = short.astype(jnp.bfloat16)
    query = short[:, :channels]
    gated = short[:, channels : 2 * channels].astype(jnp.float32) * short[:, 2 * channels :].astype(
        jnp.float32
    )
    return query, gated


def angle_table(rows_index, cols_index, length):
    product = rows_index[:, None] * cols_index[None, :] % length
    angles = product.astype(jnp.float32) * (TWO_PI / length)
    return jnp.cos(angles), jnp.sin(angles)


def channel_parallel(projected, conv_weight, skip_gain, spectrum_real, spectrum_imag):
    query, gated = short_convolution(projected, conv_weight)
    row_count, channels = gated.shape
    block_count = lax.axis_size("ctx")
    group_count = lax.axis_size("grp")
    devices = block_count * group_count
    block_len = row_count * group_count
    residues = 2 * block_count
    fft_len = residues * block_len
    width = channels // devices
    everyone = ("ctx", "grp")

    outgoing = gated.reshape(row_count, group_count, block_count, width).transpose(0, 2, 1, 3)
    outgoing = outgoing.reshape(row_count, devices, width)
    outgoing = outgoing.astype(jnp.bfloat16)
    tokens = lax.all_to_all(outgoing, everyone, split_axis=1, concat_axis=0, tiled=True)
    tokens = tokens.reshape(block_count, block_len, width).astype(jnp.float32)

    tokens, spectrum = lax.optimization_barrier((tokens, jnp.stack([spectrum_real, spectrum_imag])))
    spectrum = lax.all_to_all(spectrum, "ctx", split_axis=3, concat_axis=1, tiled=True)
    spectrum = spectrum.transpose(0, 2, 3, 1).astype(jnp.float32)
    filter_real, filter_imag = spectrum[0], spectrum[1]

    residue = jnp.arange(residues, dtype=jnp.int32)
    block_order = jnp.arange(block_count, dtype=jnp.int32)
    position = jnp.arange(block_len, dtype=jnp.int32)

    across_cos, across_sin = angle_table(block_order, residue, residues)
    folded_real = contract("jpc,ja->pca", tokens, across_cos)
    folded_imag = -contract("jpc,ja->pca", tokens, across_sin)
    turn_cos, turn_sin = angle_table(position, residue, fft_len)
    turn_cos, turn_sin = turn_cos[:, None, :], turn_sin[:, None, :]
    twisted_real = folded_real * turn_cos + folded_imag * turn_sin
    twisted_imag = folded_imag * turn_cos - folded_real * turn_sin

    within_cos, within_sin = angle_table(position, position, block_len)
    lanes = width * residues

    def times(table_part, data, precision=lax.Precision.HIGH):
        return lax.dot_general(
            table_part,
            data.reshape(block_len, lanes),
            (((1,), (0,)), ((), ())),
            precision=precision,
            preferred_element_type=jnp.float32,
        ).reshape(block_len, width, residues)

    def inverse(table_part, data):
        return times(table_part, data, lax.Precision.DEFAULT)

    spectra_real = times(within_cos, twisted_real) + times(within_sin, twisted_imag)
    spectra_imag = times(within_cos, twisted_imag) - times(within_sin, twisted_real)
    product_real = spectra_real * filter_real - spectra_imag * filter_imag
    product_imag = spectra_real * filter_imag + spectra_imag * filter_real
    restored_real = inverse(within_cos, product_real) - inverse(within_sin, product_imag)
    restored_imag = inverse(within_cos, product_imag) + inverse(within_sin, product_real)
    unturned_real = restored_real * turn_cos - restored_imag * turn_sin
    unturned_imag = restored_real * turn_sin + restored_imag * turn_cos
    long_blocks = contract("ja,pca->jpc", across_cos, unturned_real) - contract(
        "ja,pca->jpc", across_sin, unturned_imag
    )
    long_blocks = (long_blocks * (1.0 / fft_len)).reshape(devices, row_count, width)
    long_blocks = long_blocks.astype(jnp.bfloat16)
    returned = lax.all_to_all(long_blocks, everyone, split_axis=0, concat_axis=0, tiled=True)
    returned = returned.astype(jnp.float32)
    returned = returned.reshape(block_count, group_count, row_count, width).transpose(2, 1, 0, 3)
    long_tokens = returned.reshape(row_count, channels)
    mixed = query.astype(jnp.float32) * (long_tokens + skip_gain * gated)
    return mixed.astype(jnp.bfloat16)


def solution(mesh):
    in_specs = (P(("ctx", "grp"), None), P(), P(), P("ctx", None, "grp"), P("ctx", None, "grp"))
    out_specs = P(("ctx", "grp"), None)
    devices = mesh.shape["ctx"] * mesh.shape["grp"]

    def run(projected, conv_weight, skip_gain, spectrum_real, spectrum_imag):
        channels = conv_weight.shape[1] // 3
        wide = channels % devices == 0 and channels // devices >= 32
        body = channel_parallel if wide else per_device
        return jax.shard_map(
            body, mesh=mesh, in_specs=in_specs, out_specs=out_specs, check_vma=False
        )(projected, conv_weight, skip_gain, spectrum_real, spectrum_imag)

    return run
```

profile of v0, /device:TPU:1, one launch (start us, length us, event | category | flops | bytes accessed | tf_op | source)
XLA Modules:
  0.0 131.4 jit_solution(1473451587891497941)
XLA Ops:
  0.0 0.9 slice.35
  0.9 3.9 %collective-permute-start = (bf16[2,6144]{1,0:T(2,128)(2,1)S(1)}, bf16[2,6144]{1,0:T(2,128)(2,1)S(1)}, u32[]{:S(2)}, u32[]{:S(2)}) collective-permute-start(bf16[2,6144]{1,0:T(2,128)(2,1)S(1)} %slice.35), channel_id=1, source_target_pairs={{0,1},{1,2},{2,3},{3,4},{4,5},{5,6},{6,7},{7,8},{8,9},{9,10},{10,1... | collective-permute-start | bytes 73736 | tf_op jit(solution)/shard_map/ppermute | solution.py:14
  4.9 1.1 fusion.151
  6.0 1.9 %copy.59 = bf16[128,6144]{0,1:T(8,128)(2,1)S(1)} copy(bf16[128,6144]{1,0:T(8,128)(2,1)} %param.5) | data formatting | bytes 3145728 | tf_op args[0]
  7.9 0.0 collective-permute-done
  7.9 0.9 copy.60
  8.8 4.4 %add_convert_fusion = bf16[128,6144]{0,1:T(8,128)(2,1)S(1)} fusion(bf16[128,6144]{0,1:T(8,128)(2,1)S(1)} %copy.59, bf16[2,6144]{0,1:T(8,128)(2,1)S(1)} %copy.60, f32[6144]{0:T(1024)S(1)} %bitcast.118, f32[6144]{0:T(1024)S(1)} %bitcast.119, f32[6144]{0:T(1024)S(1)} %bitcast.117), kind=kLoop, calls=%fused_computation.3 | loop fusion | flops 11796480 | bytes 3244032 | tf_op jit(solution)/shard_map/convert_element_type | solution.py:132
  13.2 0.0 copy-start
  13.2 1.2 copy-done
  14.4 0.0 copy-start.4
  14.4 0.1 fusion.52
  14.5 0.8 copy.62
  15.4 5.8 %all-to-all-start = ((bf16[128,32,64]{0,2,1:T(8,128)(2,1)}), bf16[128,32,64]{0,2,1:T(8,128)(2,1)S(1)}, u32[]{:S(2)}, u32[]{:S(2)}) async-start(bf16[128,32,64]{0,2,1:T(8,128)(2,1)} %bitcast.7), calls=%async_computation | async-start | bytes 1048576 | tf_op jit(solution)/shard_map/all_to_all | solution.py:161
  21.2 0.0 copy-done.4
  21.2 0.9 copy.64
  22.1 2.5 %copy.65 = bf16[2,256,1024]{1,0,2:T(2,128)(2,1)S(1)} copy(bf16[2,256,1024]{2,1,0:T(8,128)(2,1)} %param.9) | data formatting | bytes 2097152 | tf_op args[4]
  24.6 4.0 %pad_maximum_fusion = bf16[2,2,256,1024]{2,1,0,3:T(2,128)(2,1)} fusion(bf16[1,2,256,1024]{2,1,0,3:T(2,128)(2,1)S(1)} %bitcast.114, bf16[1,2,256,1024]{2,1,0,3:T(2,128)(2,1)S(1)} %bitcast.113), kind=kLoop, calls=%fused_computation.6 | loop fusion | flops 1048576 | bytes 4194304 | tf_op jit(solution)/shard_map/stack | solution.py:164
  28.7 8.3 %all-to-all-done = bf16[128,32,64]{0,2,1:T(8,128)(2,1)S(1)} async-done(((bf16[128,32,64]{0,2,1:T(8,128)(2,1)}), bf16[128,32,64]{0,2,1:T(8,128)(2,1)S(1)}, u32[]{:S(2)}, u32[]{:S(2)}) %all-to-all-start) | async-done | bytes 524320 | tf_op jit(solution)/shard_map/all_to_all | solution.py:161
  37.0 0.1 convert_bitcast_fusion.2
  37.1 0.6 copy.63
  37.8 0.3 reshape.100
  38.1 4.5 %all-to-all-start.1 = ((bf16[2,2,256,1024]{2,1,0,3:T(2,128)(2,1)}), bf16[2,2,256,1024]{2,1,0,3:T(2,128)(2,1)}, u32[]{:S(2)}, u32[]{:S(2)}) async-start(bf16[2,2,256,1024]{2,1,0,3:T(2,128)(2,1)} %pad_maximum_fusion), calls=%async_computation.1 | async-start | bytes 4194304 | tf_op jit(solution)/shard_map/all_to_all | solution.py:165
  42.6 0.1 fusion.83
  42.7 1.9 %fusion.89 = f32[256,64,32]{0,2,1:T(8,128)S(1)} fusion(f32[16,256,64]{1,0,2:T(8,128)S(1)} %reshape.100), kind=kOutput, calls=%fused_computation.92 | convolution fusion | flops 100670464 | bytes 3145728 | tf_op jit(solution)/shard_map/jpc,ja->pca/dot_general | solution.py:28
  44.6 2.3 %add_bitcast_fusion.1 = (f32[64,32,256]{2,1,0:T(8,128)S(1)}, f32[64,32,256]{2,1,0:T(8,128)S(1)}) fusion(f32[256,64,32]{0,2,1:T(8,128)S(1)} %fusion.89, f32[256,32]{0,1:T(8,128)S(1)} %get-tuple-element.16, f32[256,32]{0,1:T(8,128)S(1)} %get-tuple-element.17, f32[16,256,64]{1,0,2:T(8,128)S(1)} %reshape.100), kind=kOutput, calls=%fused_computation.18 | convolution fusion | flops 104340480 | bytes 7405568 | tf_op jit(solution)/shard_map/jpc,ja->pca/dot_general | solution.py:28
  46.9 4.3 %fusion.16 = f32[256,64,32]{0,1,2:T(8,128)} fusion(f32[64,32,256]{2,1,0:T(8,128)S(1)} %get-tuple-element.12), kind=kOutput, calls=%fused_computation.27 | convolution fusion | flops 806223872 | bytes 4194304 | tf_op jit(solution)/shard_map/dot_general | solution.py:185
  51.3 3.0 %fusion.18 = f32[256,64,32]{0,1,2:T(8,128)S(1)} fusion(f32[64,32,256]{2,1,0:T(8,128)S(1)} %get-tuple-element.12), kind=kOutput, calls=%fused_computation.29 | convolution fusion | flops 806223872 | bytes 4194304 | tf_op jit(solution)/shard_map/dot_general | solution.py:185
  54.3 4.6 %fusion.24 = f32[256,64,32]{0,1,2:T(8,128)} fusion(f32[256,64,32]{0,1,2:T(8,128)S(1)} %fusion.18, f32[64,32,256]{2,1,0:T(8,128)S(1)} %get-tuple-element.11), kind=kOutput, calls=%fused_computation.35 | convolution fusion | flops 806748160 | bytes 6291456 | tf_op jit(solution)/shard_map/dot_general | solution.py:185
  58.9 24.4 %all-to-all-done.1 = bf16[2,2,256,1024]{2,1,0,3:T(2,128)(2,1)} async-done(((bf16[2,2,256,1024]{2,1,0,3:T(2,128)(2,1)}), bf16[2,2,256,1024]{2,1,0,3:T(2,128)(2,1)}, u32[]{:S(2)}, u32[]{:S(2)}) %all-to-all-start.1) | async-done | bytes 2097184 | tf_op jit(solution)/shard_map/all_to_all | solution.py:165
  83.3 1.9 %copy.68 = bf16[2,2,256,1024]{2,3,1,0:T(8,128)(2,1)S(1)} copy(bf16[2,2,256,1024]{2,1,0,3:T(2,128)(2,1)} %all-to-all-done.1) | data formatting | bytes 4194304 | tf_op jit(solution)/shard_map/all_to_all | solution.py:165
  85.2 0.6 convert_bitcast_fusion
  85.7 0.0 copy-start.2
  85.8 0.0 copy-start.3
  85.8 0.5 copy.69
  86.3 1.1 copy-done.2
  87.3 0.6 copy-done.3
  88.0 3.6 %subtract_bitcast_fusion = (bf16[64,32,256]{2,0,1:T(8,128)(2,1)S(1)}, bf16[64,32,256]{2,0,1:T(8,128)(2,1)S(1)}) fusion(f32[256,64,32]{0,1,2:T(8,128)S(1)} %copy-done.2, f32[2,256,64,32]{1,2,3,0:T(8,128)S(1)} %bitcast.111, f32[256,64,32]{0,1,2:T(8,128)S(1)} %copy-done.3, f32[64,32,256]{2,1,0:T(8,128)S(1)} %get-tuple-element.11), kind=kOutput, calls=%fused_computation.16 | convolution fusion | flops 810942464 | bytes 12582912 | tf_op jit(solution)/shard_map/dot_general | solution.py:185
  91.6 1.7 %fusion.8 = f32[256,64,32]{0,2,1:T(8,128)S(1)} fusion(bf16[64,32,256]{2,0,1:T(8,128)(2,1)S(1)} %get-tuple-element.10), kind=kOutput, calls=%fused_computation.19 | convolution fusion | flops 269352960 | bytes 3145728 | tf_op jit(solution)/shard_map/dot_general | solution.py:185
  93.3 1.7 %fusion.10 = f32[256,64,32]{0,2,1:T(8,128)S(1)} fusion(bf16[64,32,256]{2,0,1:T(8,128)(2,1)S(1)} %get-tuple-element.10), kind=kOutput, calls=%fused_computation.21 | convolution fusion | flops 269352960 | bytes 3145728 | tf_op jit(solution)/shard_map/dot_general | solution.py:185
  95.1 1.9 %fusion.33 = f32[256,64,32]{0,2,1:T(8,128)S(1)} fusion(f32[256,64,32]{0,2,1:T(8,128)S(1)} %fusion.8, bf16[64,32,256]{2,0,1:T(8,128)(2,1)S(1)} %get-tuple-element.9), kind=kOutput, calls=%fused_computation.38 | convolution fusion | flops 269877248 | bytes 5242880 | tf_op jit(solution)/shard_map/dot_general | solution.py:185
  97.0 2.1 %fusion.30 = f32[256,64,32]{0,2,1:T(8,128)S(1)} fusion(f32[256,64,32]{0,2,1:T(8,128)S(1)} %fusion.10, bf16[64,32,256]{2,0,1:T(8,128)(2,1)S(1)} %get-tuple-element.9), kind=kOutput, calls=%fused_computation.37 | convolution fusion | flops 269877248 | bytes 5242880 | tf_op jit(solution)/shard_map/dot_general | solution.py:185
  99.1 1.4 %fusion = f32[16,256,64]{1,0,2:T(8,128)S(1)} fusion(f32[256,64,32]{0,2,1:T(8,128)S(1)} %fusion.33, f32[256,64,32]{0,2,1:T(8,128)S(1)} %fusion.30, f32[256,32]{0,1:T(8,128)S(1)} %get-tuple-element.16, f32[256,32]{0,1:T(8,128)S(1)} %get-tuple-element.17), kind=kOutput, calls=%fused_computation.7 | convolution fusion | flops 102243328 | bytes 5308416 | tf_op jit(solution)/shard_map/ja,pca->jpc/dot_general | solution.py:28
  100.4 1.4 %fusion.43 = bf16[16,256,64]{1,0,2:T(8,128)(2,1)S(1)} fusion(f32[16,256,64]{1,0,2:T(8,128)S(1)} %fusion, f32[256,64,32]{0,2,1:T(8,128)S(1)} %fusion.33, f32[256,64,32]{0,2,1:T(8,128)S(1)} %fusion.30, f32[256,32]{0,1:T(8,128)S(1)} %get-tuple-element.16, f32[256,32]{0,1:T(8,128)S(1)} %get-tuple-element.17), kind=kOutput, calls=%fused_computation.43 | convolution fusion | flops 103029760 | bytes 5832704 | tf_op jit(solution)/shard_map/ja,pca->jpc/dot_general | solution.py:28
  101.9 0.2 convert_element_type.144
  102.0 0.2 copy.82
  102.3 26.4 %all_to_all.23 = bf16[32,128,64]{1,2,0:T(8,128)(2,1)S(1)} all-to-all(bf16[32,128,64]{1,2,0:T(8,128)(2,1)S(1)} %copy.82), channel_id=1, replica_groups=mesh['ctx'=16,'grp'=2] {'ctx','grp'}, dimensions={0} | all-to-all | bytes 1048576 | tf_op jit(solution)/shard_map/all_to_all | solution.py:209
  128.7 0.0 copy-start.1
  128.7 0.0 copy-start.5
  128.7 0.1 convert_bitcast_fusion.1
  128.8 0.1 copy.83
  128.9 1.2 copy-done.1
  130.1 0.0 copy-done.5
  130.1 0.3 fusion.47
  130.4 1.0 copy.84
Async XLA Ops:
  0.9 7.0 %collective-permute-start = (bf16[2,6144]{1,0:T(2,128)(2,1)S(1)}, bf16[2,6144]{1,0:T(2,128)(2,1)S(1)}, u32[]{:S(2)}, u32[]{:S(2)}) collective-permute-start(bf16[2,6144]{1,0:T(2,128)(2,1)S(1)} %slice.35), channel_id=1, source_target_pairs={{0,1},{1,2},{2,3},{3,4},{4,5},{5,6},{6,7},{7,8},{8,9},{9,10},{10,1... | collective-permute-start | bytes 73736 | tf_op jit(solution)/shard_map/ppermute | solution.py:14
  13.2 1.2 copy-start
  14.4 6.8 %copy-start.4 = (bf16[2,256,1024]{2,1,0:T(8,128)(2,1)S(1)}, bf16[2,256,1024]{2,1,0:T(8,128)(2,1)}, u32[]{:S(2)}) copy-start(bf16[2,256,1024]{2,1,0:T(8,128)(2,1)} %param.8) | copy-start | bytes 3145732
  15.4 21.6 %all-to-all-start = ((bf16[128,32,64]{0,2,1:T(8,128)(2,1)}), bf16[128,32,64]{0,2,1:T(8,128)(2,1)S(1)}, u32[]{:S(2)}, u32[]{:S(2)}) async-start(bf16[128,32,64]{0,2,1:T(8,128)(2,1)} %bitcast.7), calls=%async_computation | async-start | bytes 1048576 | tf_op jit(solution)/shard_map/all_to_all | solution.py:161
  38.1 45.2 %all-to-all-start.1 = ((bf16[2,2,256,1024]{2,1,0,3:T(2,128)(2,1)}), bf16[2,2,256,1024]{2,1,0,3:T(2,128)(2,1)}, u32[]{:S(2)}, u32[]{:S(2)}) async-start(bf16[2,2,256,1024]{2,1,0,3:T(2,128)(2,1)} %pad_maximum_fusion), calls=%async_computation.1 | async-start | bytes 4194304 | tf_op jit(solution)/shard_map/all_to_all | solution.py:165
  85.7 1.6 %copy-start.2 = (f32[256,64,32]{0,1,2:T(8,128)S(1)}, f32[256,64,32]{0,1,2:T(8,128)}, u32[]{:S(2)}) copy-start(f32[256,64,32]{0,1,2:T(8,128)} %fusion.24) | copy-start | bytes 6291460
  85.8 2.2 %copy-start.3 = (f32[256,64,32]{0,1,2:T(8,128)S(1)}, f32[256,64,32]{0,1,2:T(8,128)}, u32[]{:S(2)}) copy-start(f32[256,64,32]{0,1,2:T(8,128)} %fusion.16) | copy-start | bytes 6291460
  128.7 1.4 %copy-start.1 = (bf16[128,6144]{0,1:T(8,128)(2,1)S(1)}, bf16[128,6144]{0,1:T(8,128)(2,1)}, u32[]{:S(2)}) copy-start(bf16[128,6144]{0,1:T(8,128)(2,1)} %copy-done) | copy-start | bytes 4718596
  128.7 1.4 %copy-start.5 = (f32[2048]{0:T(1024)S(1)}, f32[2048]{0:T(1024)}, u32[]{:S(2)}) copy-start(f32[2048]{0:T(1024)} %param.7) | copy-start | bytes 24580
where the time goes:
time: 132 us; the launch traced here: 131 us
  waiting for transfers between devices  32.7 us (25%)
  matrix products  30 us (23%)
  blocking collectives  26.4 us (20%)
  local copies, waits for them, and re-layouts  18 us (14%)
  starting transfers between devices  14.3 us (11%)
  other arithmetic  9.81 us (7%)
    all_to_all x1, blocking collectives, channel_parallel(): lax.all_to_all(long_blocks, everyone, split_axis=0, concat_axis=0, tiled=...  26.4 us
    all_to_all x1, waiting for transfers between devices, channel_parallel(): lax.all_to_all(spectrum, 'ctx', split_axis=3, concat_axis=1, tiled=True)  24.4 us
    dot_general x8, matrix products, times(): lax.dot_general(table_part, data.reshape(block_len, lanes), (((1,), (0,))...  23 us
    unnamed x15, local copies, waits for them, and re-layouts  9.49 us
    all_to_all x1, waiting for transfers between devices, channel_parallel(): lax.all_to_all(outgoing, everyone, split_axis=1, concat_axis=0, tiled=True)  8.34 us
    dot_general x4, matrix products, contract(): jnp.einsum(form, table, data, precision=lax.Precision.HIGHEST, preferred_...  6.96 us
    all_to_all x1, starting transfers between devices, channel_parallel(): lax.all_to_all(outgoing, everyone, split_axis=1, concat_axis=0, tiled=True)  5.79 us
    all_to_all x1, starting transfers between devices, channel_parallel(): lax.all_to_all(spectrum, 'ctx', split_axis=3, concat_axis=1, tiled=True)  4.53 us
  transfers between devices with their start and end apart: 3, of which 2 were waited for; matrix products, arithmetic and copies ran while one was open for 20% of the time, Pallas kernels for 0%

commit v1 on v0

--- a/solution.py
+++ b/solution.py
@@ -24,10 +24,12 @@
     return jnp.stack([jnp.stack([cos_part, -sin_part]), jnp.stack([sin_part, cos_part])])
 
 
-def contract(form, table, data):
-    return jnp.einsum(
-        form, table, data, precision=lax.Precision.HIGHEST, preferred_element_type=jnp.float32
-    )
+def contract(form, table, data, precision=lax.Precision.HIGHEST):
+    return jnp.einsum(form, table, data, precision=precision, preferred_element_type=jnp.float32)
+
+
+def contract_high(form, table, data):
+    return contract(form, table, data, lax.Precision.HIGH)
 
 
 def twist(data, turn_real, turn_imag):
@@ -171,8 +173,8 @@
     position = jnp.arange(block_len, dtype=jnp.int32)
 
     across_cos, across_sin = angle_table(block_order, residue, residues)
-    folded_real = contract("jpc,ja->pca", tokens, across_cos)
-    folded_imag = -contract("jpc,ja->pca", tokens, across_sin)
+    folded_real = contract_high("jpc,ja->pca", tokens, across_cos)
+    folded_imag = -contract_high("jpc,ja->pca", tokens, across_sin)
     turn_cos, turn_sin = angle_table(position, residue, fft_len)
     turn_cos, turn_sin = turn_cos[:, None, :], turn_sin[:, None, :]
     twisted_real = folded_real * turn_cos + folded_imag * turn_sin
@@ -201,7 +203,7 @@
     restored_imag = inverse(within_cos, product_imag) + inverse(within_sin, product_real)
     unturned_real = restored_real * turn_cos - restored_imag * turn_sin
     unturned_imag = restored_real * turn_sin + restored_imag * turn_cos
-    long_blocks = contract("ja,pca->jpc", across_cos, unturned_real) - contract(
+    long_blocks = contract_high("ja,pca->jpc", across_cos, unturned_real) - contract_high(
         "ja,pca->jpc", across_sin, unturned_imag
     )
     long_blocks = (long_blocks * (1.0 / fft_len)).reshape(devices, row_count, width)

time: 132 us -> 131 us (level)
  matrix products: 30 us -> 26.8 us
  waiting for transfers between devices: 32.7 us -> 34.6 us
    dot_general x4, matrix products: 6.96 us -> 4.26 us  [contract(): jnp.einsum(form, table, data, precision=precision, preferred_element_type...]
    all_to_all x1, waiting for transfers between devices: 24.4 us -> 26.2 us  [channel_parallel(): lax.all_to_all(spectrum, 'ctx', split_axis=3, concat_axis=1, tiled=True)]
  transfers between devices with their start and end apart: 3 -> 3, of which waited for: 2 -> 2; matrix products, arithmetic and copies ran while one was open for 20% -> 19% of each run, Pallas kernels for 0% -> 0%
where the time goes in v1:
time: 131 us; the launch traced here: 130 us
  waiting for transfers between devices  34.6 us (26%)
  matrix products  26.8 us (20%)
  blocking collectives  26.4 us (20%)
  local copies, waits for them, and re-layouts  18.2 us (14%)
  starting transfers between devices  14.3 us (11%)
  other arithmetic  9.81 us (7%)
    all_to_all x1, blocking collectives, channel_parallel(): lax.all_to_all(long_blocks, everyone, split_axis=0, concat_axis=0, tiled=...  26.4 us
    all_to_all x1, waiting for transfers between devices, channel_parallel(): lax.all_to_all(spectrum, 'ctx', split_axis=3, concat_axis=1, tiled=True)  26.2 us
    dot_general x8, matrix products, times(): lax.dot_general(table_part, data.reshape(block_len, lanes), (((1,), (0,))...  22.6 us
    unnamed x15, local copies, waits for them, and re-layouts  9.49 us
    all_to_all x1, waiting for transfers between devices, channel_parallel(): lax.all_to_all(outgoing, everyone, split_axis=1, concat_axis=0, tiled=True)  8.34 us
    all_to_all x1, starting transfers between devices, channel_parallel(): lax.all_to_all(outgoing, everyone, split_axis=1, concat_axis=0, tiled=True)  5.79 us
    all_to_all x1, starting transfers between devices, channel_parallel(): lax.all_to_all(spectrum, 'ctx', split_axis=3, concat_axis=1, tiled=True)  4.53 us
    convert_element_type x1, other arithmetic, short_convolution(): short = short.astype(jnp.bfloat16)  4.37 us
  transfers between devices with their start and end apart: 3, of which 2 were waited for; matrix products, arithmetic and copies ran while one was open for 19% of the time, Pallas kernels for 0%

profile of v1, /device:TPU:1, one launch (start us, length us, event | category | flops | bytes accessed | tf_op | source)
XLA Modules:
  0.0 130.3 jit_solution(6619790510466767212)
XLA Ops:
  0.0 0.9 slice.35
  0.9 3.9 %collective-permute-start = (bf16[2,6144]{1,0:T(2,128)(2,1)S(1)}, bf16[2,6144]{1,0:T(2,128)(2,1)S(1)}, u32[]{:S(2)}, u32[]{:S(2)}) collective-permute-start(bf16[2,6144]{1,0:T(2,128)(2,1)S(1)} %slice.35), channel_id=1, source_target_pairs={{0,1},{1,2},{2,3},{3,4},{4,5},{5,6},{6,7},{7,8},{8,9},{9,10},{10,1... | collective-permute-start | bytes 73736 | tf_op jit(solution)/shard_map/ppermute | solution.py:14
  4.9 1.1 fusion.151
  6.0 1.9 %copy.59 = bf16[128,6144]{0,1:T(8,128)(2,1)S(1)} copy(bf16[128,6144]{1,0:T(8,128)(2,1)} %param.5) | data formatting | bytes 3145728 | tf_op args[0]
  7.9 0.0 collective-permute-done
  7.9 0.9 copy.60
  8.8 4.4 %add_convert_fusion = bf16[128,6144]{0,1:T(8,128)(2,1)S(1)} fusion(bf16[128,6144]{0,1:T(8,128)(2,1)S(1)} %copy.59, bf16[2,6144]{0,1:T(8,128)(2,1)S(1)} %copy.60, f32[6144]{0:T(1024)S(1)} %bitcast.118, f32[6144]{0:T(1024)S(1)} %bitcast.119, f32[6144]{0:T(1024)S(1)} %bitcast.117), kind=kLoop, calls=%fused_computation.3 | loop fusion | flops 11796480 | bytes 3244032 | tf_op jit(solution)/shard_map/convert_element_type | solution.py:134
  13.2 0.0 copy-start
  13.2 1.2 copy-done
  14.4 0.0 copy-start.4
  14.4 0.1 fusion.52
  14.5 0.8 copy.62
  15.4 5.8 %all-to-all-start = ((bf16[128,32,64]{0,2,1:T(8,128)(2,1)}), bf16[128,32,64]{0,2,1:T(8,128)(2,1)S(1)}, u32[]{:S(2)}, u32[]{:S(2)}) async-start(bf16[128,32,64]{0,2,1:T(8,128)(2,1)} %bitcast.7), calls=%async_computation | async-start | bytes 1048576 | tf_op jit(solution)/shard_map/all_to_all | solution.py:163
  21.2 0.0 copy-done.4
  21.2 0.9 copy.64
  22.1 2.5 %copy.65 = bf16[2,256,1024]{1,0,2:T(2,128)(2,1)S(1)} copy(bf16[2,256,1024]{2,1,0:T(8,128)(2,1)} %param.9) | data formatting | bytes 2097152 | tf_op args[4]
  24.6 4.0 %pad_maximum_fusion = bf16[2,2,256,1024]{2,1,0,3:T(2,128)(2,1)} fusion(bf16[1,2,256,1024]{2,1,0,3:T(2,128)(2,1)S(1)} %bitcast.114, bf16[1,2,256,1024]{2,1,0,3:T(2,128)(2,1)S(1)} %bitcast.113), kind=kLoop, calls=%fused_computation.6 | loop fusion | flops 1048576 | bytes 4194304 | tf_op jit(solution)/shard_map/stack | solution.py:166
  28.7 8.3 %all-to-all-done = bf16[128,32,64]{0,2,1:T(8,128)(2,1)S(1)} async-done(((bf16[128,32,64]{0,2,1:T(8,128)(2,1)}), bf16[128,32,64]{0,2,1:T(8,128)(2,1)S(1)}, u32[]{:S(2)}, u32[]{:S(2)}) %all-to-all-start) | async-done | bytes 524320 | tf_op jit(solution)/shard_map/all_to_all | solution.py:163
  37.0 0.1 convert_bitcast_fusion.2
  37.1 0.6 copy.63
  37.8 0.3 reshape.100
  38.1 4.5 %all-to-all-start.1 = ((bf16[2,2,256,1024]{2,1,0,3:T(2,128)(2,1)}), bf16[2,2,256,1024]{2,1,0,3:T(2,128)(2,1)}, u32[]{:S(2)}, u32[]{:S(2)}) async-start(bf16[2,2,256,1024]{2,1,0,3:T(2,128)(2,1)} %pad_maximum_fusion), calls=%async_computation.1 | async-start | bytes 4194304 | tf_op jit(solution)/shard_map/all_to_all | solution.py:167
  42.6 0.1 fusion.83
  42.7 1.1 fusion.89
  43.8 1.5 %add_bitcast_fusion.1 = (f32[64,32,256]{2,1,0:T(8,128)S(1)}, f32[64,32,256]{2,1,0:T(8,128)S(1)}) fusion(f32[256,64,32]{0,2,1:T(8,128)S(1)} %fusion.89, f32[256,32]{0,1:T(8,128)S(1)} %get-tuple-element.16, f32[256,32]{0,1:T(8,128)S(1)} %get-tuple-element.17, f32[16,256,64]{1,0,2:T(8,128)S(1)} %reshape.100), kind=kOutput, calls=%fused_computation.18 | convolution fusion | flops 54008832 | bytes 7405568 | tf_op jit(solution)/shard_map/jpc,ja->pca/dot_general | solution.py:28
  45.3 4.3 %fusion.16 = f32[256,64,32]{0,1,2:T(8,128)} fusion(f32[64,32,256]{2,1,0:T(8,128)S(1)} %get-tuple-element.12), kind=kOutput, calls=%fused_computation.27 | convolution fusion | flops 806223872 | bytes 4194304 | tf_op jit(solution)/shard_map/dot_general | solution.py:187
  49.7 3.0 %fusion.18 = f32[256,64,32]{0,1,2:T(8,128)S(1)} fusion(f32[64,32,256]{2,1,0:T(8,128)S(1)} %get-tuple-element.12), kind=kOutput, calls=%fused_computation.29 | convolution fusion | flops 806223872 | bytes 4194304 | tf_op jit(solution)/shard_map/dot_general | solution.py:187
  52.7 4.4 %fusion.24 = f32[256,64,32]{0,1,2:T(8,128)} fusion(f32[256,64,32]{0,1,2:T(8,128)S(1)} %fusion.18, f32[64,32,256]{2,1,0:T(8,128)S(1)} %get-tuple-element.11), kind=kOutput, calls=%fused_computation.35 | convolution fusion | flops 806748160 | bytes 6291456 | tf_op jit(solution)/shard_map/dot_general | solution.py:187
  57.1 26.2 %all-to-all-done.1 = bf16[2,2,256,1024]{2,1,0,3:T(2,128)(2,1)} async-done(((bf16[2,2,256,1024]{2,1,0,3:T(2,128)(2,1)}), bf16[2,2,256,1024]{2,1,0,3:T(2,128)(2,1)}, u32[]{:S(2)}, u32[]{:S(2)}) %all-to-all-start.1) | async-done | bytes 2097184 | tf_op jit(solution)/shard_map/all_to_all | solution.py:167
  83.3 2.1 %copy.68 = bf16[2,2,256,1024]{2,3,1,0:T(8,128)(2,1)S(1)} copy(bf16[2,2,256,1024]{2,1,0,3:T(2,128)(2,1)} %all-to-all-done.1) | data formatting | bytes 4194304 | tf_op jit(solution)/shard_map/all_to_all | solution.py:167
  85.4 0.6 convert_bitcast_fusion
  86.0 0.0 copy-start.2
  86.0 0.0 copy-start.3
  86.0 0.5 copy.69
  86.5 1.1 copy-done.2
  87.6 0.6 copy-done.3
  88.2 3.6 %subtract_bitcast_fusion = (bf16[64,32,256]{2,0,1:T(8,128)(2,1)S(1)}, bf16[64,32,256]{2,0,1:T(8,128)(2,1)S(1)}) fusion(f32[256,64,32]{0,1,2:T(8,128)S(1)} %copy-done.2, f32[2,256,64,32]{1,2,3,0:T(8,128)S(1)} %bitcast.111, f32[256,64,32]{0,1,2:T(8,128)S(1)} %copy-done.3, f32[64,32,256]{2,1,0:T(8,128)S(1)} %get-tuple-element.11), kind=kOutput, calls=%fused_computation.16 | convolution fusion | flops 810942464 | bytes 12582912 | tf_op jit(solution)/shard_map/dot_general | solution.py:187
  91.8 1.7 %fusion.8 = f32[256,64,32]{0,2,1:T(8,128)S(1)} fusion(bf16[64,32,256]{2,0,1:T(8,128)(2,1)S(1)} %get-tuple-element.10), kind=kOutput, calls=%fused_computation.19 | convolution fusion | flops 269352960 | bytes 3145728 | tf_op jit(solution)/shard_map/dot_general | solution.py:187
  93.6 1.8 %fusion.10 = f32[256,64,32]{0,2,1:T(8,128)S(1)} fusion(bf16[64,32,256]{2,0,1:T(8,128)(2,1)S(1)} %get-tuple-element.10), kind=kOutput, calls=%fused_computation.21 | convolution fusion | flops 269352960 | bytes 3145728 | tf_op jit(solution)/shard_map/dot_general | solution.py:187
  95.3 1.9 %fusion.33 = f32[256,64,32]{0,2,1:T(8,128)S(1)} fusion(f32[256,64,32]{0,2,1:T(8,128)S(1)} %fusion.8, bf16[64,32,256]{2,0,1:T(8,128)(2,1)S(1)} %get-tuple-element.9), kind=kOutput, calls=%fused_computation.38 | convolution fusion | flops 269877248 | bytes 5242880 | tf_op jit(solution)/shard_map/dot_general | solution.py:187
  97.2 1.9 %fusion.30 = f32[256,64,32]{0,2,1:T(8,128)S(1)} fusion(f32[256,64,32]{0,2,1:T(8,128)S(1)} %fusion.10, bf16[64,32,256]{2,0,1:T(8,128)(2,1)S(1)} %get-tuple-element.9), kind=kOutput, calls=%fused_computation.37 | convolution fusion | flops 269877248 | bytes 5242880 | tf_op jit(solution)/shard_map/dot_general | solution.py:187
  99.0 0.8 fusion
  99.9 0.9 fusion.43
  100.8 0.2 convert_element_type.144
  100.9 0.2 copy.82
  101.1 26.4 %all_to_all.23 = bf16[32,128,64]{1,2,0:T(8,128)(2,1)S(1)} all-to-all(bf16[32,128,64]{1,2,0:T(8,128)(2,1)S(1)} %copy.82), channel_id=1, replica_groups=mesh['ctx'=16,'grp'=2] {'ctx','grp'}, dimensions={0} | all-to-all | bytes 1048576 | tf_op jit(solution)/shard_map/all_to_all | solution.py:211
  127.6 0.0 copy-start.1
  127.6 0.0 copy-start.5
  127.6 0.1 convert_bitcast_fusion.1
  127.7 0.1 copy.83
  127.8 1.2 copy-done.1
  129.0 0.0 copy-done.5
  129.0 0.3 fusion.47
  129.3 1.0 copy.84
Async XLA Ops:
  0.9 7.0 %collective-permute-start = (bf16[2,6144]{1,0:T(2,128)(2,1)S(1)}, bf16[2,6144]{1,0:T(2,128)(2,1)S(1)}, u32[]{:S(2)}, u32[]{:S(2)}) collective-permute-start(bf16[2,6144]{1,0:T(2,128)(2,1)S(1)} %slice.35), channel_id=1, source_target_pairs={{0,1},{1,2},{2,3},{3,4},{4,5},{5,6},{6,7},{7,8},{8,9},{9,10},{10,1... | collective-permute-start | bytes 73736 | tf_op jit(solution)/shard_map/ppermute | solution.py:14
  13.2 1.2 copy-start
  14.4 6.8 %copy-start.4 = (bf16[2,256,1024]{2,1,0:T(8,128)(2,1)S(1)}, bf16[2,256,1024]{2,1,0:T(8,128)(2,1)}, u32[]{:S(2)}) copy-start(bf16[2,256,1024]{2,1,0:T(8,128)(2,1)} %param.8) | copy-start | bytes 3145732
  15.4 21.6 %all-to-all-start = ((bf16[128,32,64]{0,2,1:T(8,128)(2,1)}), bf16[128,32,64]{0,2,1:T(8,128)(2,1)S(1)}, u32[]{:S(2)}, u32[]{:S(2)}) async-start(bf16[128,32,64]{0,2,1:T(8,128)(2,1)} %bitcast.7), calls=%async_computation | async-start | bytes 1048576 | tf_op jit(solution)/shard_map/all_to_all | solution.py:163
  38.1 45.2 %all-to-all-start.1 = ((bf16[2,2,256,1024]{2,1,0,3:T(2,128)(2,1)}), bf16[2,2,256,1024]{2,1,0,3:T(2,128)(2,1)}, u32[]{:S(2)}, u32[]{:S(2)}) async-start(bf16[2,2,256,1024]{2,1,0,3:T(2,128)(2,1)} %pad_maximum_fusion), calls=%async_computation.1 | async-start | bytes 4194304 | tf_op jit(solution)/shard_map/all_to_all | solution.py:167
  86.0 1.6 %copy-start.2 = (f32[256,64,32]{0,1,2:T(8,128)S(1)}, f32[256,64,32]{0,1,2:T(8,128)}, u32[]{:S(2)}) copy-start(f32[256,64,32]{0,1,2:T(8,128)} %fusion.24) | copy-start | bytes 6291460
  86.0 2.2 %copy-start.3 = (f32[256,64,32]{0,1,2:T(8,128)S(1)}, f32[256,64,32]{0,1,2:T(8,128)}, u32[]{:S(2)}) copy-start(f32[256,64,32]{0,1,2:T(8,128)} %fusion.16) | copy-start | bytes 6291460
  127.6 1.4 %copy-start.1 = (bf16[128,6144]{0,1:T(8,128)(2,1)S(1)}, bf16[128,6144]{0,1:T(8,128)(2,1)}, u32[]{:S(2)}) copy-start(bf16[128,6144]{0,1:T(8,128)(2,1)} %copy-done) | copy-start | bytes 4718596
  127.6 1.4 %copy-start.5 = (f32[2048]{0:T(1024)S(1)}, f32[2048]{0:T(1024)}, u32[]{:S(2)}) copy-start(f32[2048]{0:T(1024)} %param.7) | copy-start | bytes 24580

commit v2 on v1

--- a/solution.py
+++ b/solution.py
@@ -146,22 +146,33 @@
 
 
 def channel_parallel(projected, conv_weight, skip_gain, spectrum_real, spectrum_imag):
-    query, gated = short_convolution(projected, conv_weight)
-    row_count, channels = gated.shape
+    row_count = projected.shape[0]
+    taps, all_channels = conv_weight.shape
+    channels = all_channels // 3
     block_count = lax.axis_size("ctx")
     group_count = lax.axis_size("grp")
     devices = block_count * group_count
     block_len = row_count * group_count
+    sequence = block_len * block_count
     residues = 2 * block_count
     fft_len = residues * block_len
     width = channels // devices
     everyone = ("ctx", "grp")
 
-    outgoing = gated.reshape(row_count, group_count, block_count, width).transpose(0, 2, 1, 3)
-    outgoing = outgoing.reshape(row_count, devices, width)
-    outgoing = outgoing.astype(jnp.bfloat16)
-    tokens = lax.all_to_all(outgoing, everyone, split_axis=1, concat_axis=0, tiled=True)
-    tokens = tokens.reshape(block_count, block_len, width).astype(jnp.float32)
+    pairs = projected[:, channels:].reshape(row_count, 2, group_count, block_count, width)
+    pairs = pairs.transpose(0, 3, 2, 1, 4).reshape(row_count, devices, 2, width)
+    pairs = lax.all_to_all(pairs, everyone, split_axis=1, concat_axis=0, tiled=True)
+    pairs = pairs.reshape(sequence, 2, width).astype(jnp.float32)
+    pair_weight = conv_weight[:, channels:].reshape(taps, 2, group_count, block_count, width)
+    pair_weight = lax.dynamic_index_in_dim(pair_weight, lax.axis_index("grp"), 2, keepdims=False)
+    pair_weight = lax.dynamic_index_in_dim(pair_weight, lax.axis_index("ctx"), 2, keepdims=False)
+    padded = jnp.pad(pairs, ((taps - 1, 0), (0, 0), (0, 0)))
+    short = jnp.zeros((sequence, 2, width), jnp.float32)
+    for offset in range(taps):
+        short = short + pair_weight[offset] * padded[taps - 1 - offset : taps - 1 - offset + sequence]
+    short = short.astype(jnp.bfloat16).astype(jnp.float32)
+    tokens = (short[:, 0] * short[:, 1]).reshape(block_count, block_len, width)
+    query, gated = short_convolution(projected, conv_weight)
 
     tokens, spectrum = lax.optimization_barrier((tokens, jnp.stack([spectrum_real, spectrum_imag])))
     spectrum = lax.all_to_all(spectrum, "ctx", split_axis=3, concat_axis=1, tiled=True)

time: 131 us -> 157 us (1.20)
  starting transfers between devices: 14.3 us -> 40.7 us
  blocking collectives: 26.4 us -> 0 us
  waiting for transfers between devices: 34.6 us -> 50.4 us
  local copies, waits for them, and re-layouts: 18.2 us -> 23.5 us
  other arithmetic: 9.81 us -> 13.5 us
    all_to_all x1 -> x2, starting transfers between devices: 5.79 us -> 32.9 us  [the longest x1 25.9 us: channel_parallel(): lax.all_to_all(long_blocks, everyone, split_axis=0, concat_axis=0, tiled=...]
    all_to_all x1 -> x0, blocking collectives: 26.4 us -> none  [channel_parallel(): lax.all_to_all(long_blocks, everyone, split_axis=0, concat_axis=0, tiled=...]
    all_to_all x1 -> x2, waiting for transfers between devices: 8.34 us -> 28.9 us  [the longest x1 18.4 us: channel_parallel(): lax.all_to_all(pairs, everyone, split_axis=1, concat_axis=0, tiled=True)]
    all_to_all x1, waiting for transfers between devices: 26.2 us -> 19.3 us  [channel_parallel(): lax.all_to_all(spectrum, 'ctx', split_axis=3, concat_axis=1, tiled=True)]
    convert_element_type x2, local copies, waits for them, and re-layouts: 0.38 us -> 4.21 us  [channel_parallel(): long_blocks = long_blocks.astype(jnp.bfloat16)]
    convert_element_type x3 -> x2, local copies, waits for them, and re-layouts: 1.74 us -> 4.27 us  [channel_parallel(): pairs = pairs.reshape(sequence, 2, width).astype(jnp.float32)]
    ppermute x1, waiting for transfers between devices: 0.01 us -> 2.22 us  [shifted(): return lax.ppermute(shard, axis, pairs)]
    unnamed x15 -> x22, local copies, waits for them, and re-layouts: 9.49 us -> 7.77 us
  transfers between devices with their start and end apart: 3 -> 4, of which waited for: 2 -> 4; matrix products, arithmetic and copies ran while one was open for 19% -> 19% of each run, Pallas kernels for 0% -> 0%
where the time goes in v2:
time: 157 us; the launch traced here: 156 us
  waiting for transfers between devices  50.4 us (32%)
  starting transfers between devices  40.7 us (26%)
  matrix products  27.9 us (18%)
  local copies, waits for them, and re-layouts  23.5 us (15%)
  other arithmetic  13.5 us (9%)
    all_to_all x1, starting transfers between devices, channel_parallel(): lax.all_to_all(long_blocks, everyone, split_axis=0, concat_axis=0, tiled=...  25.9 us
    dot_general x8, matrix products, times(): lax.dot_general(table_part, data.reshape(block_len, lanes), (((1,), (0,))...  22.6 us
    all_to_all x1, waiting for transfers between devices, channel_parallel(): lax.all_to_all(spectrum, 'ctx', split_axis=3, concat_axis=1, tiled=True)  19.3 us
    all_to_all x1, waiting for transfers between devices, channel_parallel(): lax.all_to_all(pairs, everyone, split_axis=1, concat_axis=0, tiled=True)  18.4 us
    all_to_all x1, waiting for transfers between devices, channel_parallel(): lax.all_to_all(long_blocks, everyone, split_axis=0, concat_axis=0, tiled=...  10.4 us
    unnamed x22, local copies, waits for them, and re-layouts  7.77 us
    all_to_all x1, starting transfers between devices, channel_parallel(): lax.all_to_all(pairs, everyone, split_axis=1, concat_axis=0, tiled=True)  7.08 us
    convert_element_type x1, other arithmetic, short_convolution(): short = short.astype(jnp.bfloat16)  5.43 us
  transfers between devices with their start and end apart: 4, of which 4 were waited for; matrix products, arithmetic and copies ran while one was open for 19% of the time, Pallas kernels for 0%

profile of v2, /device:TPU:1, one launch (start us, length us, event | category | flops | bytes accessed | tf_op | source)
XLA Modules:
  0.0 156.3 jit_solution(462885393333094740)
XLA Ops:
  0.0 1.9 %copy.64 = bf16[128,6144]{0,1:T(8,128)(2,1)S(1)} copy(bf16[128,6144]{1,0:T(8,128)(2,1)} %param.5) | data formatting | bytes 3145728 | tf_op args[0]
  1.9 0.0 copy-start
  1.9 0.1 slice.87
  2.0 0.0 slice-start
  2.0 0.0 copy-start.6
  2.0 1.1 copy.69
  3.1 0.4 copy-done
  3.5 7.1 %all-to-all-start = ((bf16[128,32,2,64]{0,3,2,1:T(8,128)(2,1)}), bf16[128,32,2,64]{0,3,2,1:T(8,128)(2,1)S(1)}, u32[]{:S(2)}, u32[]{:S(2)}) async-start(bf16[128,32,2,64]{0,3,2,1:T(8,128)(2,1)} %bitcast.8), calls=%async_computation | async-start | bytes 2097152 | tf_op jit(solution)/shard_map/all_to_all | solution.py:164
  10.6 0.0 slice-done
  10.6 0.1 reshape.110
  10.7 0.0 copy-done.6
  10.7 0.9 copy.71
  11.6 2.5 %copy.72 = bf16[2,256,1024]{1,0,2:T(2,128)(2,1)S(1)} copy(bf16[2,256,1024]{2,1,0:T(8,128)(2,1)} %param.9) | data formatting | bytes 2097152 | tf_op args[4]
  14.2 4.0 %pad_maximum_fusion = bf16[2,2,256,1024]{2,1,0,3:T(2,128)(2,1)} fusion(bf16[1,2,256,1024]{2,1,0,3:T(2,128)(2,1)S(1)} %bitcast.133, bf16[1,2,256,1024]{2,1,0,3:T(2,128)(2,1)S(1)} %bitcast.132), kind=kLoop, calls=%fused_computation.6 | loop fusion | flops 1048576 | bytes 4194304 | tf_op jit(solution)/shard_map/stack | solution.py:177
  18.2 18.4 %all-to-all-done = bf16[128,32,2,64]{0,3,2,1:T(8,128)(2,1)S(1)} async-done(((bf16[128,32,2,64]{0,3,2,1:T(8,128)(2,1)}), bf16[128,32,2,64]{0,3,2,1:T(8,128)(2,1)S(1)}, u32[]{:S(2)}, u32[]{:S(2)}) %all-to-all-start) | async-done | bytes 1048608 | tf_op jit(solution)/shard_map/all_to_all | solution.py:164
  36.6 0.2 convert_bitcast_fusion.1
  36.9 2.5 %copy.70 = f32[32,128,1,2,64]{1,0,4,3,2:T(8,128)} copy(f32[32,128,1,2,64]{1,4,3,0,2:T(8,128)S(1)} %convert_bitcast_fusion.1) | data formatting | bytes 4194304 | tf_op jit(solution)/shard_map/convert_element_type | solution.py:165
  39.4 1.7 %reshape.120 = f32[4096,2,64]{0,2,1:T(8,128)S(1)} reshape(f32[32,128,1,2,64]{1,0,4,3,2:T(8,128)} %copy.70) | data formatting | bytes 4194304 | tf_op jit(solution)/shard_map/convert_element_type | solution.py:165
  41.2 1.2 fusion.46
  42.4 0.1 slice_multiply_fusion
  42.5 0.3 copy.112
  42.8 0.0 copy-start.7
  42.8 4.7 %all-to-all-start.1 = ((bf16[2,2,256,1024]{2,1,0,3:T(2,128)(2,1)}), bf16[2,2,256,1024]{2,1,0,3:T(2,128)(2,1)}, u32[]{:S(2)}, u32[]{:S(2)}) async-start(bf16[2,2,256,1024]{2,1,0,3:T(2,128)(2,1)} %pad_maximum_fusion), calls=%async_computation.1 | async-start | bytes 4194304 | tf_op jit(solution)/shard_map/all_to_all | solution.py:178
  47.5 0.9 slice.66
  48.5 3.1 %collective-permute-start = (bf16[2,6144]{1,0:T(2,128)(2,1)S(1)}, bf16[2,6144]{1,0:T(2,128)(2,1)S(1)}, u32[]{:S(2)}, u32[]{:S(2)}) collective-permute-start(bf16[2,6144]{1,0:T(2,128)(2,1)S(1)} %slice.66), channel_id=1, source_target_pairs={{0,1},{1,2},{2,3},{3,4},{4,5},{5,6},{6,7},{7,8},{8,9},{9,10},{10,1... | collective-permute-start | bytes 73736 | tf_op jit(solution)/shard_map/ppermute | solution.py:14
  51.6 0.0 copy-done.7
  51.6 0.1 fusion.151
  51.6 0.1 fusion.83
  51.8 2.2 %collective-permute-done = bf16[2,6144]{1,0:T(2,128)(2,1)S(1)} collective-permute-done((bf16[2,6144]{1,0:T(2,128)(2,1)S(1)}, bf16[2,6144]{1,0:T(2,128)(2,1)S(1)}, u32[]{:S(2)}, u32[]{:S(2)}) %collective-permute-start) | collective-permute-done | bytes 24608 | tf_op jit(solution)/shard_map/ppermute | solution.py:14
  54.0 1.6 %copy.65 = bf16[2,6144]{0,1:T(8,128)(2,1)} copy(bf16[2,6144]{1,0:T(2,128)(2,1)S(1)} %collective-permute-done) | data formatting | bytes 49152 | tf_op jit(solution)/shard_map/ppermute | solution.py:14
  55.6 1.1 fusion.89
  56.7 1.5 add_bitcast_fusion.1
  58.2 4.3 %fusion.16 = f32[256,64,32]{0,1,2:T(8,128)} fusion(f32[64,32,256]{2,1,0:T(8,128)S(1)} %get-tuple-element.12), kind=kOutput, calls=%fused_computation.29 | convolution fusion | flops 806223872 | bytes 4194304 | tf_op jit(solution)/shard_map/dot_general | solution.py:198
  62.5 3.0 %fusion.18 = f32[256,64,32]{0,1,2:T(8,128)S(1)} fusion(f32[64,32,256]{2,1,0:T(8,128)S(1)} %get-tuple-element.12), kind=kOutput, calls=%fused_computation.31 | convolution fusion | flops 806223872 | bytes 4194304 | tf_op jit(solution)/shard_map/dot_general | solution.py:198
  65.5 4.4 %fusion.24 = f32[256,64,32]{0,1,2:T(8,128)} fusion(f32[256,64,32]{0,1,2:T(8,128)S(1)} %fusion.18, f32[64,32,256]{2,1,0:T(8,128)S(1)} %get-tuple-element.11), kind=kOutput, calls=%fused_computation.37 | convolution fusion | flops 806748160 | bytes 6291456 | tf_op jit(solution)/shard_map/dot_general | solution.py:198
  69.9 19.3 %all-to-all-done.1 = bf16[2,2,256,1024]{2,1,0,3:T(2,128)(2,1)} async-done(((bf16[2,2,256,1024]{2,1,0,3:T(2,128)(2,1)}), bf16[2,2,256,1024]{2,1,0,3:T(2,128)(2,1)}, u32[]{:S(2)}, u32[]{:S(2)}) %all-to-all-start.1) | async-done | bytes 2097184 | tf_op jit(solution)/shard_map/all_to_all | solution.py:178
  89.2 1.9 %copy.75 = bf16[2,2,256,1024]{2,3,1,0:T(8,128)(2,1)S(1)} copy(bf16[2,2,256,1024]{2,1,0,3:T(2,128)(2,1)} %all-to-all-done.1) | data formatting | bytes 4194304 | tf_op jit(solution)/shard_map/all_to_all | solution.py:178
  91.1 0.8 convert_bitcast_fusion
  91.9 0.0 copy-start.2
  91.9 0.0 copy-start.3
  91.9 0.5 copy.76
  92.4 1.1 copy-done.2
  93.5 0.6 copy-done.3
  94.1 3.6 %subtract_bitcast_fusion = (bf16[64,32,256]{2,0,1:T(8,128)(2,1)S(1)}, bf16[64,32,256]{2,0,1:T(8,128)(2,1)S(1)}) fusion(f32[256,64,32]{0,1,2:T(8,128)S(1)} %copy-done.2, f32[2,256,64,32]{1,2,3,0:T(8,128)S(1)} %bitcast.128, f32[256,64,32]{0,1,2:T(8,128)S(1)} %copy-done.3, f32[64,32,256]{2,1,0:T(8,128)S(1)} %get-tuple-element.11), kind=kOutput, calls=%fused_computation.17 | convolution fusion | flops 810942464 | bytes 12582912 | tf_op jit(solution)/shard_map/dot_general | solution.py:198
  97.7 1.7 %fusion.8 = f32[256,64,32]{0,2,1:T(8,128)S(1)} fusion(bf16[64,32,256]{2,0,1:T(8,128)(2,1)S(1)} %get-tuple-element.10), kind=kOutput, calls=%fused_computation.21 | convolution fusion | flops 269352960 | bytes 3145728 | tf_op jit(solution)/shard_map/dot_general | solution.py:198
  99.5 1.7 %fusion.10 = f32[256,64,32]{0,2,1:T(8,128)S(1)} fusion(bf16[64,32,256]{2,0,1:T(8,128)(2,1)S(1)} %get-tuple-element.10), kind=kOutput, calls=%fused_computation.23 | convolution fusion | flops 269352960 | bytes 3145728 | tf_op jit(solution)/shard_map/dot_general | solution.py:198
  101.2 1.9 %fusion.33 = f32[256,64,32]{0,2,1:T(8,128)S(1)} fusion(f32[256,64,32]{0,2,1:T(8,128)S(1)} %fusion.8, bf16[64,32,256]{2,0,1:T(8,128)(2,1)S(1)} %get-tuple-element.9), kind=kOutput, calls=%fused_computation.40 | convolution fusion | flops 269877248 | bytes 5242880 | tf_op jit(solution)/shard_map/dot_general | solution.py:198
  103.1 1.9 %fusion.30 = f32[256,64,32]{0,2,1:T(8,128)S(1)} fusion(f32[256,64,32]{0,2,1:T(8,128)S(1)} %fusion.10, bf16[64,32,256]{2,0,1:T(8,128)(2,1)S(1)} %get-tuple-element.9), kind=kOutput, calls=%fused_computation.39 | convolution fusion | flops 269877248 | bytes 5242880 | tf_op jit(solution)/shard_map/dot_general | solution.py:198
  105.0 0.8 fusion
  105.8 1.9 %fusion.43 = bf16[16,256,64]{1,0,2:T(8,128)(2,1)} fusion(f32[16,256,64]{1,0,2:T(8,128)S(1)} %fusion, f32[256,64,32]{0,2,1:T(8,128)S(1)} %fusion.33, f32[256,64,32]{0,2,1:T(8,128)S(1)} %fusion.30, f32[256,32]{0,1:T(8,128)S(1)} %get-tuple-element.19, f32[256,32]{0,1:T(8,128)S(1)} %get-tuple-element.20), kind=kOutput, calls=%fused_computation.45 | convolution fusion | flops 52698112 | bytes 5832704 | tf_op jit(solution)/shard_map/ja,pca->jpc/dot_general | solution.py:28
  107.7 0.0 copy-start.1
  107.7 2.2 %convert_element_type.136 = bf16[32,128,64]{1,0,2:T(8,128)(2,1)} reshape(bf16[16,256,64]{1,0,2:T(8,128)(2,1)} %fusion.43) | data formatting | bytes 1048576 | tf_op jit(solution)/shard_map/convert_element_type | solution.py:221
  109.9 2.0 %copy.89 = bf16[32,128,64]{1,2,0:T(8,128)(2,1)} copy(bf16[32,128,64]{1,0,2:T(8,128)(2,1)} %convert_element_type.136) | data formatting | bytes 1048576 | tf_op jit(solution)/shard_map/convert_element_type | solution.py:221
  111.9 25.9 %all-to-all-start.2 = ((bf16[32,128,64]{1,2,0:T(8,128)(2,1)}), bf16[32,128,64]{1,2,0:T(8,128)(2,1)}, u32[]{:S(2)}, u32[]{:S(2)}) async-start(bf16[32,128,64]{1,2,0:T(8,128)(2,1)} %copy.89), calls=%async_computation.2 | async-start | bytes 1048576 | tf_op jit(solution)/shard_map/all_to_all | solution.py:222
  137.8 0.0 copy-done.1
  137.8 0.0 copy-done.4
  137.8 5.4 %add_convert_fusion = bf16[128,6144]{0,1:T(8,128)(2,1)} fusion(bf16[128,6144]{0,1:T(8,128)(2,1)S(1)} %copy-done.1, bf16[2,6144]{0,1:T(8,128)(2,1)S(1)} %copy-done.4, f32[6144]{0:T(1024)S(1)} %bitcast.136, f32[6144]{0:T(1024)S(1)} %bitcast.135, f32[6144]{0:T(1024)S(1)} %bitcast.134), kind=kLoop, calls=%fused_computation.3 | loop fusion | flops 11796480 | bytes 3244032 | tf_op jit(solution)/shard_map/convert_element_type | solution.py:134
  143.3 10.4 %all-to-all-done.2 = bf16[32,128,64]{1,2,0:T(8,128)(2,1)} async-done(((bf16[32,128,64]{1,2,0:T(8,128)(2,1)}), bf16[32,128,64]{1,2,0:T(8,128)(2,1)}, u32[]{:S(2)}, u32[]{:S(2)}) %all-to-all-start.2) | async-done | bytes 524320 | tf_op jit(solution)/shard_map/all_to_all | solution.py:222
  153.7 1.2 convert_bitcast_fusion.2
  154.9 0.1 copy.90
  154.9 0.0 copy-done.5
  154.9 0.0 copy-done.8
  155.0 0.4 fusion.48
  155.3 1.0 copy.91
  (4 shorter events, 0.0 us)
Async XLA Ops:
  1.9 1.5 copy-start
  2.0 8.6 %slice-start = ((f32[3,6144]{1,0:T(4,128)}), f32[3,4096]{1,0:T(4,128)S(1)}, s32[]{:S(2)}) async-start(f32[3,6144]{1,0:T(4,128)} %param.6), calls=%async_computation.3 | async-start | bytes 131072 | tf_op jit(solution)/shard_map/slice | solution.py:166
  2.0 8.7 %copy-start.6 = (bf16[2,256,1024]{2,1,0:T(8,128)(2,1)S(1)}, bf16[2,256,1024]{2,1,0:T(8,128)(2,1)}, u32[]{:S(2)}) copy-start(bf16[2,256,1024]{2,1,0:T(8,128)(2,1)} %param.8) | copy-start | bytes 3145732
  3.5 33.2 %all-to-all-start = ((bf16[128,32,2,64]{0,3,2,1:T(8,128)(2,1)}), bf16[128,32,2,64]{0,3,2,1:T(8,128)(2,1)S(1)}, u32[]{:S(2)}, u32[]{:S(2)}) async-start(bf16[128,32,2,64]{0,3,2,1:T(8,128)(2,1)} %bitcast.8), calls=%async_computation | async-start | bytes 2097152 | tf_op jit(solution)/shard_map/all_to_all | solution.py:164
  42.8 8.7 %copy-start.7 = (f32[3,6144]{1,0:T(4,128)S(1)}, f32[3,6144]{1,0:T(4,128)}, u32[]{:S(2)}) copy-start(f32[3,6144]{1,0:T(4,128)} %param.6) | copy-start | bytes 221188
  42.8 46.4 %all-to-all-start.1 = ((bf16[2,2,256,1024]{2,1,0,3:T(2,128)(2,1)}), bf16[2,2,256,1024]{2,1,0,3:T(2,128)(2,1)}, u32[]{:S(2)}, u32[]{:S(2)}) async-start(bf16[2,2,256,1024]{2,1,0,3:T(2,128)(2,1)} %pad_maximum_fusion), calls=%async_computation.1 | async-start | bytes 4194304 | tf_op jit(solution)/shard_map/all_to_all | solution.py:178
  48.5 5.5 %collective-permute-start = (bf16[2,6144]{1,0:T(2,128)(2,1)S(1)}, bf16[2,6144]{1,0:T(2,128)(2,1)S(1)}, u32[]{:S(2)}, u32[]{:S(2)}) collective-permute-start(bf16[2,6144]{1,0:T(2,128)(2,1)S(1)} %slice.66), channel_id=1, source_target_pairs={{0,1},{1,2},{2,3},{3,4},{4,5},{5,6},{6,7},{7,8},{8,9},{9,10},{10,1... | collective-permute-start | bytes 73736 | tf_op jit(solution)/shard_map/ppermute | solution.py:14
  91.9 1.6 %copy-start.2 = (f32[256,64,32]{0,1,2:T(8,128)S(1)}, f32[256,64,32]{0,1,2:T(8,128)}, u32[]{:S(2)}) copy-start(f32[256,64,32]{0,1,2:T(8,128)} %fusion.24) | copy-start | bytes 6291460
  91.9 2.2 %copy-start.3 = (f32[256,64,32]{0,1,2:T(8,128)S(1)}, f32[256,64,32]{0,1,2:T(8,128)}, u32[]{:S(2)}) copy-start(f32[256,64,32]{0,1,2:T(8,128)} %fusion.16) | copy-start | bytes 6291460
  107.7 30.1 %copy-start.1 = (bf16[128,6144]{0,1:T(8,128)(2,1)S(1)}, bf16[128,6144]{0,1:T(8,128)(2,1)}, u32[]{:S(2)}) copy-start(bf16[128,6144]{0,1:T(8,128)(2,1)} %copy-done) | copy-start | bytes 4718596
  107.7 30.1 %copy-start.4 = (bf16[2,6144]{0,1:T(8,128)(2,1)S(1)}, bf16[2,6144]{0,1:T(8,128)(2,1)}, u32[]{:S(2)}) copy-start(bf16[2,6144]{0,1:T(8,128)(2,1)} %copy.65) | copy-start | bytes 73732
  111.9 41.8 %all-to-all-start.2 = ((bf16[32,128,64]{1,2,0:T(8,128)(2,1)}), bf16[32,128,64]{1,2,0:T(8,128)(2,1)}, u32[]{:S(2)}, u32[]{:S(2)}) async-start(bf16[32,128,64]{1,2,0:T(8,128)(2,1)} %copy.89), calls=%async_computation.2 | async-start | bytes 1048576 | tf_op jit(solution)/shard_map/all_to_all | solution.py:222
  143.3 11.7 %copy-start.5 = (bf16[128,6144]{0,1:T(8,128)(2,1)S(1)}, bf16[128,6144]{0,1:T(8,128)(2,1)}, u32[]{:S(2)}) copy-start(bf16[128,6144]{0,1:T(8,128)(2,1)} %add_convert_fusion) | copy-start | bytes 4718596
  143.3 11.7 %copy-start.8 = (f32[2048]{0:T(1024)S(1)}, f32[2048]{0:T(1024)}, u32[]{:S(2)}) copy-start(f32[2048]{0:T(1024)} %param.7) | copy-start | bytes 24580

commit v3 on v1

--- a/solution.py
+++ b/solution.py
@@ -163,9 +163,12 @@
     tokens = lax.all_to_all(outgoing, everyone, split_axis=1, concat_axis=0, tiled=True)
     tokens = tokens.reshape(block_count, block_len, width).astype(jnp.float32)
 
-    tokens, spectrum = lax.optimization_barrier((tokens, jnp.stack([spectrum_real, spectrum_imag])))
-    spectrum = lax.all_to_all(spectrum, "ctx", split_axis=3, concat_axis=1, tiled=True)
-    spectrum = spectrum.transpose(0, 2, 3, 1).astype(jnp.float32)
+    local_residues, spectrum_len, half = spectrum_real.shape
+    spectrum = jnp.stack([spectrum_real, spectrum_imag])
+    spectrum = spectrum.reshape(2, local_residues, spectrum_len, block_count, width).transpose(0, 2, 3, 4, 1)
+    tokens, spectrum = lax.optimization_barrier((tokens, spectrum))
+    spectrum = lax.all_to_all(spectrum, "ctx", split_axis=2, concat_axis=4, tiled=True)
+    spectrum = spectrum.reshape(2, spectrum_len, width, residues).astype(jnp.float32)
     filter_real, filter_imag = spectrum[0], spectrum[1]
 
     residue = jnp.arange(residues, dtype=jnp.int32)

time: 131 us -> 135 us (1.031)
  waiting for transfers between devices: 34.6 us -> 38.8 us
    all_to_all x1, waiting for transfers between devices: 8.34 us -> 12.6 us  [channel_parallel(): lax.all_to_all(outgoing, everyone, split_axis=1, concat_axis=0, tiled=True)]
    another operation x1 -> x0, other arithmetic: 4.04 us -> none  [channel_parallel(): jnp.stack([spectrum_real, spectrum_imag])]
    convert_element_type x2, local copies, waits for them, and re-layouts: 0.91 us -> 3.13 us  [channel_parallel(): tokens = tokens.reshape(block_count, block_len, width).astype(jnp.float32)]
    all_to_all x1 -> x0, local copies, waits for them, and re-layouts: 2.08 us -> none  [channel_parallel(): lax.all_to_all(spectrum, 'ctx', split_axis=3, concat_axis=1, tiled=True)]
    convert_element_type x1, other arithmetic: 0.57 us -> 2.34 us  [channel_parallel(): spectrum.reshape(2, spectrum_len, width, residues).astype(jnp.float32)]
    unnamed x15 -> x17, local copies, waits for them, and re-layouts: 9.49 us -> 7.89 us
    optimization_barrier x0 -> x1, local copies, waits for them, and re-layouts: none -> 1.49 us  [channel_parallel(): tokens, spectrum = lax.optimization_barrier((tokens, spectrum))]
    transpose x0 -> x1, other arithmetic: none -> 1.42 us  [channel_parallel(): spectrum.reshape(2, local_residues, spectrum_len, block_count, width)]
  transfers between devices with their start and end apart: 3 -> 3, of which waited for: 2 -> 2; matrix products, arithmetic and copies ran while one was open for 19% -> 15% of each run, Pallas kernels for 0% -> 0%
where the time goes in v3:
time: 135 us
  waiting for transfers between devices  38.8 us (29%)
  matrix products  26.6 us (20%)
  blocking collectives  26.4 us (20%)
  local copies, waits for them, and re-layouts  18.2 us (13%)
  starting transfers between devices  14.3 us (11%)
  other arithmetic  10 us (7%)
    all_to_all x1, blocking collectives, channel_parallel(): lax.all_to_all(long_blocks, everyone, split_axis=0, concat_axis=0, tiled=...  26.4 us
    all_to_all x1, waiting for transfers between devices, channel_parallel(): lax.all_to_all(spectrum, 'ctx', split_axis=2, concat_axis=4, tiled=True)  26.2 us
    dot_general x8, matrix products, times(): lax.dot_general(table_part, data.reshape(block_len, lanes), (((1,), (0,))...  22.3 us
    all_to_all x1, waiting for transfers between devices, channel_parallel(): lax.all_to_all(outgoing, everyone, split_axis=1, concat_axis=0, tiled=True)  12.6 us
    unnamed x17, local copies, waits for them, and re-layouts  7.89 us
    all_to_all x1, starting transfers between devices, channel_parallel(): lax.all_to_all(outgoing, everyone, split_axis=1, concat_axis=0, tiled=True)  5.84 us
    all_to_all x1, starting transfers between devices, channel_parallel(): lax.all_to_all(spectrum, 'ctx', split_axis=2, concat_axis=4, tiled=True)  4.53 us
    convert_element_type x1, other arithmetic, short_convolution(): short = short.astype(jnp.bfloat16)  4.37 us
  transfers between devices with their start and end apart: 3, of which 2 were waited for; matrix products, arithmetic and copies ran while one was open for 15% of the time, Pallas kernels for 0%

profile of v3, /device:TPU:1, one launch (start us, length us, event | category | flops | bytes accessed | tf_op | source)
XLA Modules:
  0.0 134.6 jit_solution(2146626211732085144)
XLA Ops:
  0.0 0.9 slice.37
  0.9 3.9 %collective-permute-start = (bf16[2,6144]{1,0:T(2,128)(2,1)S(1)}, bf16[2,6144]{1,0:T(2,128)(2,1)S(1)}, u32[]{:S(2)}, u32[]{:S(2)}) collective-permute-start(bf16[2,6144]{1,0:T(2,128)(2,1)S(1)} %slice.37), channel_id=1, source_target_pairs={{0,1},{1,2},{2,3},{3,4},{4,5},{5,6},{6,7},{7,8},{8,9},{9,10},{10,1... | collective-permute-start | bytes 73736 | tf_op jit(solution)/shard_map/ppermute | solution.py:14
  4.9 1.1 fusion.154
  6.0 1.9 %copy.62 = bf16[128,6144]{0,1:T(8,128)(2,1)S(1)} copy(bf16[128,6144]{1,0:T(8,128)(2,1)} %param.5) | data formatting | bytes 3145728 | tf_op args[0]
  7.9 0.0 collective-permute-done
  7.9 0.9 copy.63
  8.8 4.4 %add_convert_fusion = bf16[128,6144]{0,1:T(8,128)(2,1)S(1)} fusion(bf16[128,6144]{0,1:T(8,128)(2,1)S(1)} %copy.62, bf16[2,6144]{0,1:T(8,128)(2,1)S(1)} %copy.63, f32[6144]{0:T(1024)S(1)} %bitcast.120, f32[6144]{0:T(1024)S(1)} %bitcast.121, f32[6144]{0:T(1024)S(1)} %bitcast.119), kind=kLoop, calls=%fused_computation.3 | loop fusion | flops 11796480 | bytes 3244032 | tf_op jit(solution)/shard_map/convert_element_type | solution.py:134
  13.2 0.0 copy-start
  13.2 1.2 copy-done
  14.4 0.0 copy-start.4
  14.4 0.1 fusion.54
  14.5 0.0 copy-start.5
  14.5 0.8 copy.65
  15.4 5.8 %all-to-all-start = ((bf16[128,32,64]{0,2,1:T(8,128)(2,1)}), bf16[128,32,64]{0,2,1:T(8,128)(2,1)}, u32[]{:S(2)}, u32[]{:S(2)}) async-start(bf16[128,32,64]{0,2,1:T(8,128)(2,1)} %bitcast.7), calls=%async_computation | async-start | bytes 1048576 | tf_op jit(solution)/shard_map/all_to_all | solution.py:163
  21.2 0.0 copy-done.4
  21.2 0.5 copy.67
  21.8 0.0 copy-done.5
  21.8 1.3 copy.68
  23.1 1.4 %maximum_bitcast_fusion = bf16[2,256,16,64,2]{1,3,2,4,0:T(8,128)(2,1)S(1)} fusion(bf16[1,2,256,16,64]{2,4,3,1,0:T(8,128)(2,1)} %bitcast.116, bf16[1,2,256,16,64]{2,4,3,1,0:T(8,128)(2,1)S(1)} %bitcast.115), kind=kLoop, calls=%fused_computation.4 | loop fusion | flops 1048576 | bytes 4194304 | tf_op jit(solution)/shard_map/transpose | solution.py:168
  24.5 12.6 %all-to-all-done = bf16[128,32,64]{0,2,1:T(8,128)(2,1)} async-done(((bf16[128,32,64]{0,2,1:T(8,128)(2,1)}), bf16[128,32,64]{0,2,1:T(8,128)(2,1)}, u32[]{:S(2)}, u32[]{:S(2)}) %all-to-all-start) | async-done | bytes 524320 | tf_op jit(solution)/shard_map/all_to_all | solution.py:163
  37.1 1.1 convert_bitcast_fusion.2
  38.3 1.6 %copy.66 = f32[32,128,1,64]{1,0,3,2:T(8,128)} copy(f32[32,128,1,64]{1,3,0,2:T(8,128)S(1)} %convert_bitcast_fusion.2) | data formatting | bytes 2097152 | tf_op jit(solution)/shard_map/convert_element_type | solution.py:164
  39.9 1.5 %reshape.110 = f32[16,256,64]{1,0,2:T(8,128)S(1)} reshape(f32[32,128,1,64]{1,0,3,2:T(8,128)} %copy.66) | data formatting | bytes 2097152 | tf_op jit(solution)/shard_map/convert_element_type | solution.py:164
  41.4 1.5 %copy.71 = bf16[2,256,16,64,2]{1,3,4,0,2:T(8,128)(2,1)} copy(bf16[2,256,16,64,2]{1,3,2,4,0:T(8,128)(2,1)S(1)} %maximum_bitcast_fusion) | data formatting | bytes 4194304 | tf_op jit(solution)/shard_map/optimization_barrier | solution.py:169
  42.9 4.5 %all-to-all-start.1 = ((bf16[2,256,16,64,2]{1,3,4,0,2:T(8,128)(2,1)}), bf16[2,256,16,64,2]{1,3,4,0,2:T(8,128)(2,1)}, u32[]{:S(2)}, u32[]{:S(2)}) async-start(bf16[2,256,16,64,2]{1,3,4,0,2:T(8,128)(2,1)} %copy.71), calls=%async_computation.1 | async-start | bytes 4194304 | tf_op jit(solution)/shard_map/all_to_all | solution.py:170
  47.4 0.1 fusion.85
  47.6 1.1 fusion.91
  48.7 1.5 %add_bitcast_fusion = (f32[64,32,256]{2,1,0:T(8,128)S(1)}, f32[64,32,256]{2,1,0:T(8,128)S(1)}) fusion(f32[256,64,32]{0,2,1:T(8,128)S(1)} %fusion.91, f32[256,32]{0,1:T(8,128)S(1)} %get-tuple-element.18, f32[256,32]{0,1:T(8,128)S(1)} %get-tuple-element.19, f32[16,256,64]{1,0,2:T(8,128)S(1)} %reshape.110), kind=kOutput, calls=%fused_computation.20 | convolution fusion | flops 54008832 | bytes 7405568 | tf_op jit(solution)/shard_map/jpc,ja->pca/dot_general | solution.py:28
  50.2 4.3 %fusion.18 = f32[256,64,32]{0,1,2:T(8,128)} fusion(f32[64,32,256]{2,1,0:T(8,128)S(1)} %get-tuple-element.12), kind=kOutput, calls=%fused_computation.29 | convolution fusion | flops 806223872 | bytes 4194304 | tf_op jit(solution)/shard_map/dot_general | solution.py:190
  54.5 3.0 %fusion.20 = f32[256,64,32]{0,1,2:T(8,128)S(1)} fusion(f32[64,32,256]{2,1,0:T(8,128)S(1)} %get-tuple-element.12), kind=kOutput, calls=%fused_computation.31 | convolution fusion | flops 806223872 | bytes 4194304 | tf_op jit(solution)/shard_map/dot_general | solution.py:190
  57.5 4.4 %fusion.26 = f32[256,64,32]{0,1,2:T(8,128)} fusion(f32[256,64,32]{0,1,2:T(8,128)S(1)} %fusion.20, f32[64,32,256]{2,1,0:T(8,128)S(1)} %get-tuple-element.11), kind=kOutput, calls=%fused_computation.37 | convolution fusion | flops 806748160 | bytes 6291456 | tf_op jit(solution)/shard_map/dot_general | solution.py:190
  61.9 26.2 %all-to-all-done.1 = bf16[2,256,16,64,2]{1,3,4,0,2:T(8,128)(2,1)} async-done(((bf16[2,256,16,64,2]{1,3,4,0,2:T(8,128)(2,1)}), bf16[2,256,16,64,2]{1,3,4,0,2:T(8,128)(2,1)}, u32[]{:S(2)}, u32[]{:S(2)}) %all-to-all-start.1) | async-done | bytes 2097184 | tf_op jit(solution)/shard_map/all_to_all | solution.py:170
  88.1 2.3 %convert_bitcast_fusion = f32[2,256,1,64,16,2]{1,3,5,0,4,2:T(8,128)S(1)} fusion(bf16[2,256,16,64,2]{1,3,4,0,2:T(8,128)(2,1)} %all-to-all-done.1), kind=kLoop, calls=%fused_computation | loop fusion | flops 1048576 | bytes 6291456 | tf_op jit(solution)/shard_map/convert_element_type | solution.py:171
  90.5 0.0 copy-start.2
  90.5 0.0 copy-start.3
  90.5 0.5 fusion.153
  91.0 1.1 copy-done.2
  92.1 0.6 copy-done.3
  92.7 3.3 %fusion = (bf16[256,64,32]{0,1,2:T(8,128)(2,1)S(1)}, bf16[256,64,32]{0,1,2:T(8,128)(2,1)S(1)}) fusion(f32[1,256,1,64,16,2]{1,3,5,0,4,2:T(8,128)S(1)} %get-tuple-element.14, f32[256,64,32]{0,1,2:T(8,128)S(1)} %copy-done.2, f32[1,256,1,64,16,2]{1,3,5,0,4,2:T(8,128)S(1)} %get-tuple-element.13, f32[256,64,32]{0,1,2:T(8,128)S(1)} %copy-done.3, ...), kind=kOutput, calls=%fused_computation.7 | convolution fusion | flops 810942464 | bytes 12582912 | tf_op jit(solution)/shard_map/dot_general | solution.py:190
  96.1 1.7 %fusion.10 = f32[256,64,32]{0,2,1:T(8,128)S(1)} fusion(bf16[64,32,256]{2,0,1:T(8,128)(2,1)S(1)} %bitcast.113), kind=kOutput, calls=%fused_computation.21 | convolution fusion | flops 269352960 | bytes 3145728 | tf_op jit(solution)/shard_map/dot_general | solution.py:190
  97.8 1.8 %fusion.12 = f32[256,64,32]{0,2,1:T(8,128)S(1)} fusion(bf16[64,32,256]{2,0,1:T(8,128)(2,1)S(1)} %bitcast.114), kind=kOutput, calls=%fused_computation.23 | convolution fusion | flops 269352960 | bytes 3145728 | tf_op jit(solution)/shard_map/dot_general | solution.py:190
  99.6 1.9 %fusion.35 = f32[256,64,32]{0,2,1:T(8,128)S(1)} fusion(f32[256,64,32]{0,2,1:T(8,128)S(1)} %fusion.10, bf16[64,32,256]{2,0,1:T(8,128)(2,1)S(1)} %bitcast.111), kind=kOutput, calls=%fused_computation.40 | convolution fusion | flops 269877248 | bytes 5242880 | tf_op jit(solution)/shard_map/dot_general | solution.py:190
  101.4 1.9 %fusion.32 = f32[256,64,32]{0,2,1:T(8,128)S(1)} fusion(f32[256,64,32]{0,2,1:T(8,128)S(1)} %fusion.12, bf16[64,32,256]{2,0,1:T(8,128)(2,1)S(1)} %bitcast.112), kind=kOutput, calls=%fused_computation.39 | convolution fusion | flops 269877248 | bytes 5242880 | tf_op jit(solution)/shard_map/dot_general | solution.py:190
  103.3 0.8 fusion.2
  104.1 0.9 fusion.45
  105.0 0.2 convert_element_type.137
  105.2 0.2 copy.84
  105.4 26.4 %all_to_all.23 = bf16[32,128,64]{1,2,0:T(8,128)(2,1)S(1)} all-to-all(bf16[32,128,64]{1,2,0:T(8,128)(2,1)S(1)} %copy.84), channel_id=1, replica_groups=mesh['ctx'=16,'grp'=2] {'ctx','grp'}, dimensions={0} | all-to-all | bytes 1048576 | tf_op jit(solution)/shard_map/all_to_all | solution.py:214
  131.8 0.0 copy-start.1
  131.8 0.0 copy-start.6
  131.8 0.1 convert_bitcast_fusion.1
  131.9 0.1 copy.85
  132.0 1.2 copy-done.1
  133.2 0.0 copy-done.6
  133.2 0.3 fusion.49
  133.6 1.0 copy.86
Async XLA Ops:
  0.9 7.0 %collective-permute-start = (bf16[2,6144]{1,0:T(2,128)(2,1)S(1)}, bf16[2,6144]{1,0:T(2,128)(2,1)S(1)}, u32[]{:S(2)}, u32[]{:S(2)}) collective-permute-start(bf16[2,6144]{1,0:T(2,128)(2,1)S(1)} %slice.37), channel_id=1, source_target_pairs={{0,1},{1,2},{2,3},{3,4},{4,5},{5,6},{6,7},{7,8},{8,9},{9,10},{10,1... | collective-permute-start | bytes 73736 | tf_op jit(solution)/shard_map/ppermute | solution.py:14
  13.2 1.2 copy-start
  14.4 6.8 %copy-start.4 = (bf16[2,256,1024]{2,1,0:T(8,128)(2,1)S(1)}, bf16[2,256,1024]{2,1,0:T(8,128)(2,1)}, u32[]{:S(2)}) copy-start(bf16[2,256,1024]{2,1,0:T(8,128)(2,1)} %param.8) | copy-start | bytes 3145732
  14.5 7.2 %copy-start.5 = (bf16[2,256,1024]{2,1,0:T(8,128)(2,1)S(1)}, bf16[2,256,1024]{2,1,0:T(8,128)(2,1)}, u32[]{:S(2)}) copy-start(bf16[2,256,1024]{2,1,0:T(8,128)(2,1)} %param.9) | copy-start | bytes 3145732
  15.4 21.7 %all-to-all-start = ((bf16[128,32,64]{0,2,1:T(8,128)(2,1)}), bf16[128,32,64]{0,2,1:T(8,128)(2,1)}, u32[]{:S(2)}, u32[]{:S(2)}) async-start(bf16[128,32,64]{0,2,1:T(8,128)(2,1)} %bitcast.7), calls=%async_computation | async-start | bytes 1048576 | tf_op jit(solution)/shard_map/all_to_all | solution.py:163
  42.9 45.2 %all-to-all-start.1 = ((bf16[2,256,16,64,2]{1,3,4,0,2:T(8,128)(2,1)}), bf16[2,256,16,64,2]{1,3,4,0,2:T(8,128)(2,1)}, u32[]{:S(2)}, u32[]{:S(2)}) async-start(bf16[2,256,16,64,2]{1,3,4,0,2:T(8,128)(2,1)} %copy.71), calls=%async_computation.1 | async-start | bytes 4194304 | tf_op jit(solution)/shard_map/all_to_all | solution.py:170
  90.5 1.6 %copy-start.2 = (f32[256,64,32]{0,1,2:T(8,128)S(1)}, f32[256,64,32]{0,1,2:T(8,128)}, u32[]{:S(2)}) copy-start(f32[256,64,32]{0,1,2:T(8,128)} %fusion.26) | copy-start | bytes 6291460
  90.5 2.2 %copy-start.3 = (f32[256,64,32]{0,1,2:T(8,128)S(1)}, f32[256,64,32]{0,1,2:T(8,128)}, u32[]{:S(2)}) copy-start(f32[256,64,32]{0,1,2:T(8,128)} %fusion.18) | copy-start | bytes 6291460
  131.8 1.4 %copy-start.1 = (bf16[128,6144]{0,1:T(8,128)(2,1)S(1)}, bf16[128,6144]{0,1:T(8,128)(2,1)}, u32[]{:S(2)}) copy-start(bf16[128,6144]{0,1:T(8,128)(2,1)} %copy-done) | copy-start | bytes 4718596
  131.8 1.4 %copy-start.6 = (f32[2048]{0:T(1024)S(1)}, f32[2048]{0:T(1024)}, u32[]{:S(2)}) copy-start(f32[2048]{0:T(1024)} %param.7) | copy-start | bytes 24580

commit v4 on v1

--- a/solution.py
+++ b/solution.py
@@ -145,8 +145,27 @@
     return jnp.cos(angles), jnp.sin(angles)
 
 
+def split_convolution(projected, conv_weight):
+    channels = conv_weight.shape[1] // 3
+    rim_rows = conv_weight.shape[0] - 1
+    row_count = projected.shape[0]
+    rim = shifted(projected[row_count - rim_rows :], ("ctx", "grp"), 1)
+    extended = jnp.concatenate([rim, projected], axis=0)
+
+    def columns(first, last):
+        total = jnp.zeros((row_count, last - first), jnp.float32)
+        for offset in range(rim_rows + 1):
+            rows = extended[rim_rows - offset : rim_rows - offset + row_count, first:last]
+            total = total + conv_weight[offset, first:last] * rows.astype(jnp.float32)
+        return total.astype(jnp.bfloat16)
+
+    pairs = columns(channels, 3 * channels).astype(jnp.float32)
+    gated = pairs[:, :channels] * pairs[:, channels:]
+    return gated, lambda: columns(0, channels)
+
+
 def channel_parallel(projected, conv_weight, skip_gain, spectrum_real, spectrum_imag):
-    query, gated = short_convolution(projected, conv_weight)
+    gated, query_of = split_convolution(projected, conv_weight)
     row_count, channels = gated.shape
     block_count = lax.axis_size("ctx")
     group_count = lax.axis_size("grp")
@@ -197,6 +216,7 @@
 
     spectra_real = times(within_cos, twisted_real) + times(within_sin, twisted_imag)
     spectra_imag = times(within_cos, twisted_imag) - times(within_sin, twisted_real)
+    query, spectra_real, spectra_imag = lax.optimization_barrier((query_of(), spectra_real, spectra_imag))
     product_real = spectra_real * filter_real - spectra_imag * filter_imag
     product_imag = spectra_real * filter_imag + spectra_imag * filter_real
     restored_real = inverse(within_cos, product_real) - inverse(within_sin, product_imag)

time: 131 us -> 133 us (1.015)
  waiting for transfers between devices: 34.6 us -> 23.5 us
  local copies, waits for them, and re-layouts: 18.2 us -> 26.6 us
  other arithmetic: 9.81 us -> 15.1 us
    all_to_all x1, waiting for transfers between devices: 26.2 us -> 20.5 us  [channel_parallel(): lax.all_to_all(spectrum, 'ctx', split_axis=3, concat_axis=1, tiled=True)]
    all_to_all x1, waiting for transfers between devices: 8.34 us -> 3.01 us  [channel_parallel(): lax.all_to_all(outgoing, everyone, split_axis=1, concat_axis=0, tiled=True)]
    unnamed x15, local copies, waits for them, and re-layouts: 9.49 us -> 13.1 us
    convert_element_type x2, local copies, waits for them, and re-layouts: 0.91 us -> 4.1 us  [channel_parallel(): tokens = tokens.reshape(block_count, block_len, width).astype(jnp.float32)]
    dot_general x8, matrix products: 22.6 us -> 20.8 us  [times(): lax.dot_general(table_part, data.reshape(block_len, lanes), (((1,), (0,))...]
    another operation x1, other arithmetic: 4.04 us -> 5.56 us  [channel_parallel(): jnp.stack([spectrum_real, spectrum_imag])]
    convert_element_type x1 -> x2, other arithmetic: 4.37 us -> 5.89 us  [the longest x1 3.12 us: columns(): return total.astype(jnp.bfloat16)]
    slice x2 -> x3, local copies, waits for them, and re-layouts: 2.04 us -> 2.82 us  [the longest x2 1.9 us: columns(): total = total + conv_weight[offset, first:last] * rows.astype(jnp.float32)]
  transfers between devices with their start and end apart: 3 -> 3, of which waited for: 2 -> 2; matrix products, arithmetic and copies ran while one was open for 19% -> 27% of each run, Pallas kernels for 0% -> 0%
where the time goes in v4:
time: 133 us; the launch traced here: 132 us
  local copies, waits for them, and re-layouts  26.6 us (20%)
  blocking collectives  26.4 us (20%)
  matrix products  26.2 us (20%)
  waiting for transfers between devices  23.5 us (18%)
  other arithmetic  15.1 us (11%)
  starting transfers between devices  14.2 us (11%)
    all_to_all x1, blocking collectives, channel_parallel(): lax.all_to_all(long_blocks, everyone, split_axis=0, concat_axis=0, tiled=...  26.4 us
    dot_general x8, matrix products, times(): lax.dot_general(table_part, data.reshape(block_len, lanes), (((1,), (0,))...  20.8 us
    all_to_all x1, waiting for transfers between devices, channel_parallel(): lax.all_to_all(spectrum, 'ctx', split_axis=3, concat_axis=1, tiled=True)  20.5 us
    unnamed x15, local copies, waits for them, and re-layouts  13.1 us
    all_to_all x1, starting transfers between devices, channel_parallel(): lax.all_to_all(outgoing, everyone, split_axis=1, concat_axis=0, tiled=True)  5.96 us
    another operation x1, other arithmetic, channel_parallel(): jnp.stack([spectrum_real, spectrum_imag])  5.56 us
    dot_general x4, matrix products, contract(): jnp.einsum(form, table, data, precision=precision, preferred_element_type...  5.33 us
    all_to_all x1, starting transfers between devices, channel_parallel(): lax.all_to_all(spectrum, 'ctx', split_axis=3, concat_axis=1, tiled=True)  4.34 us
  transfers between devices with their start and end apart: 3, of which 2 were waited for; matrix products, arithmetic and copies ran while one was open for 27% of the time, Pallas kernels for 0%

profile of v4, /device:TPU:1, one launch (start us, length us, event | category | flops | bytes accessed | tf_op | source)
XLA Modules:
  0.0 132.2 jit_solution(15139352987297334742)
XLA Ops:
  0.0 0.9 slice.54
  0.9 3.9 %collective-permute-start = (bf16[2,6144]{1,0:T(2,128)(2,1)S(1)}, bf16[2,6144]{1,0:T(2,128)(2,1)S(1)}, u32[]{:S(2)}, u32[]{:S(2)}) collective-permute-start(bf16[2,6144]{1,0:T(2,128)(2,1)S(1)} %slice.54), channel_id=1, source_target_pairs={{0,1},{1,2},{2,3},{3,4},{4,5},{5,6},{6,7},{7,8},{8,9},{9,10},{10,1... | collective-permute-start | bytes 73736 | tf_op jit(solution)/shard_map/ppermute | solution.py:14
  4.9 1.0 fusion.151
  5.9 1.9 %copy.61 = bf16[128,6144]{0,1:T(8,128)(2,1)S(1)} copy(bf16[128,6144]{1,0:T(8,128)(2,1)} %param.5) | data formatting | bytes 3145728 | tf_op args[0]
  7.8 0.0 collective-permute-done
  7.8 0.9 copy.62
  8.7 2.8 %fusion.45 = f32[128,4096]{0,1:T(8,128)S(1)} fusion(bf16[128,6144]{0,1:T(8,128)(2,1)S(1)} %copy.61, bf16[2,6144]{0,1:T(8,128)(2,1)S(1)} %copy.62, f32[4096]{0:T(1024)S(1)} %bitcast.120, f32[4096]{0:T(1024)S(1)} %bitcast.121, f32[4096]{0:T(1024)S(1)} %bitcast.119), kind=kLoop, calls=%fused_computation.40 | loop fusion | flops 8388608 | bytes 6340608 | tf_op jit(solution)/shard_map/convert_element_type | solution.py:162
  11.5 0.0 copy-start
  11.5 1.3 %copy-done = f32[128,4096]{0,1:T(8,128)} copy-done((f32[128,4096]{0,1:T(8,128)}, f32[128,4096]{0,1:T(8,128)S(1)}, u32[]{:S(2)}) %copy-start) | copy-done | bytes 2097176
  12.8 0.1 fusion.52
  12.9 0.8 copy.65
  13.7 6.0 %all-to-all-start = ((bf16[128,32,64]{0,2,1:T(8,128)(2,1)}), bf16[128,32,64]{0,2,1:T(8,128)(2,1)}, u32[]{:S(2)}, u32[]{:S(2)}) async-start(bf16[128,32,64]{0,2,1:T(8,128)(2,1)} %bitcast.118), calls=%async_computation | async-start | bytes 1048576 | tf_op jit(solution)/shard_map/all_to_all | solution.py:182
  19.7 3.7 %copy.67 = bf16[2,256,1024]{1,0,2:T(2,128)(2,1)} copy(bf16[2,256,1024]{2,1,0:T(8,128)(2,1)} %param.8) | data formatting | bytes 2097152 | tf_op args[3]
  23.4 3.7 %copy.68 = bf16[2,256,1024]{1,0,2:T(2,128)(2,1)} copy(bf16[2,256,1024]{2,1,0:T(8,128)(2,1)} %param.9) | data formatting | bytes 2097152 | tf_op args[4]
  27.0 5.6 %pad_maximum_fusion = bf16[2,2,256,1024]{2,1,0,3:T(2,128)(2,1)} fusion(bf16[1,2,256,1024]{2,1,0,3:T(2,128)(2,1)} %bitcast.115, bf16[1,2,256,1024]{2,1,0,3:T(2,128)(2,1)} %bitcast.114), kind=kLoop, calls=%fused_computation.3 | loop fusion | flops 1048576 | bytes 4194304 | tf_op jit(solution)/shard_map/stack | solution.py:185
  32.6 3.0 %all-to-all-done = bf16[128,32,64]{0,2,1:T(8,128)(2,1)} async-done(((bf16[128,32,64]{0,2,1:T(8,128)(2,1)}), bf16[128,32,64]{0,2,1:T(8,128)(2,1)}, u32[]{:S(2)}, u32[]{:S(2)}) %all-to-all-start) | async-done | bytes 524320 | tf_op jit(solution)/shard_map/all_to_all | solution.py:182
  35.6 1.1 convert_bitcast_fusion.2
  36.8 1.6 %copy.66 = f32[32,128,1,64]{1,0,3,2:T(8,128)} copy(f32[32,128,1,64]{1,3,0,2:T(8,128)S(1)} %convert_bitcast_fusion.2) | data formatting | bytes 2097152 | tf_op jit(solution)/shard_map/convert_element_type | solution.py:183
  38.3 2.5 %reshape.100 = f32[16,256,64]{1,0,2:T(8,128)} reshape(f32[32,128,1,64]{1,0,3,2:T(8,128)} %copy.66) | data formatting | bytes 2097152 | tf_op jit(solution)/shard_map/convert_element_type | solution.py:183
  40.9 4.3 %all-to-all-start.1 = ((bf16[2,2,256,1024]{2,1,0,3:T(2,128)(2,1)}), bf16[2,2,256,1024]{2,1,0,3:T(2,128)(2,1)}, u32[]{:S(2)}, u32[]{:S(2)}) async-start(bf16[2,2,256,1024]{2,1,0,3:T(2,128)(2,1)} %pad_maximum_fusion), calls=%async_computation.1 | async-start | bytes 4194304 | tf_op jit(solution)/shard_map/all_to_all | solution.py:186
  45.2 0.1 fusion.83
  45.4 0.9 fusion.152
  46.3 0.0 copy-start.2
  46.3 3.1 %add_convert_fusion.1 = bf16[128,2048]{0,1:T(8,128)(2,1)} fusion(bf16[128,6144]{0,1:T(8,128)(2,1)S(1)} %copy.61, bf16[2,6144]{0,1:T(8,128)(2,1)S(1)} %copy.62, f32[2048]{0:T(1024)S(1)} %bitcast.123, f32[2048]{0:T(1024)S(1)} %bitcast.124, f32[2048]{0:T(1024)S(1)} %bitcast.122), kind=kLoop, calls=%fused_computation.52 | loop fusion | flops 3932160 | bytes 4218880 | tf_op jit(solution)/shard_map/convert_element_type | solution.py:160
  49.4 0.0 copy-done.2
  49.4 1.1 fusion.89
  50.5 1.5 %add_bitcast_fusion.1 = (f32[64,32,256]{2,1,0:T(8,128)S(1)}, f32[64,32,256]{2,1,0:T(8,128)S(1)}) fusion(f32[256,64,32]{0,2,1:T(8,128)S(1)} %fusion.89, f32[256,32]{0,1:T(8,128)S(1)} %get-tuple-element.25, f32[256,32]{0,1:T(8,128)S(1)} %get-tuple-element.26, f32[16,256,64]{1,0,2:T(8,128)S(1)} %copy-done.2), kind=kOutput, calls=%fused_computation.15 | convolution fusion | flops 54008832 | bytes 7405568 | tf_op jit(solution)/shard_map/jpc,ja->pca/dot_general | solution.py:28
  52.0 3.0 %fusion.16 = f32[256,64,32]{0,1,2:T(8,128)S(1)} fusion(f32[64,32,256]{2,1,0:T(8,128)S(1)} %get-tuple-element.18), kind=kOutput, calls=%fused_computation.25 | convolution fusion | flops 806223872 | bytes 4194304 | tf_op jit(solution)/shard_map/dot_general | solution.py:206
  55.0 3.0 %fusion.18 = f32[256,64,32]{0,1,2:T(8,128)S(1)} fusion(f32[64,32,256]{2,1,0:T(8,128)S(1)} %get-tuple-element.18), kind=kOutput, calls=%fused_computation.27 | convolution fusion | flops 806223872 | bytes 4194304 | tf_op jit(solution)/shard_map/dot_general | solution.py:206
  58.0 3.0 %fusion.24 = f32[256,64,32]{0,1,2:T(8,128)S(1)} fusion(f32[256,64,32]{0,1,2:T(8,128)S(1)} %fusion.18, f32[64,32,256]{2,1,0:T(8,128)S(1)} %get-tuple-element.17), kind=kOutput, calls=%fused_computation.33 | convolution fusion | flops 806748160 | bytes 6291456 | tf_op jit(solution)/shard_map/dot_general | solution.py:206
  61.0 4.6 %fusion.27 = f32[256,64,32]{0,1,2:T(8,128)} fusion(f32[256,64,32]{0,1,2:T(8,128)S(1)} %fusion.16, f32[64,32,256]{2,1,0:T(8,128)S(1)} %get-tuple-element.17), kind=kOutput, calls=%fused_computation.34 | convolution fusion | flops 806748160 | bytes 6291456 | tf_op jit(solution)/shard_map/dot_general | solution.py:206
  65.6 20.5 %all-to-all-done.1 = bf16[2,2,256,1024]{2,1,0,3:T(2,128)(2,1)} async-done(((bf16[2,2,256,1024]{2,1,0,3:T(2,128)(2,1)}), bf16[2,2,256,1024]{2,1,0,3:T(2,128)(2,1)}, u32[]{:S(2)}, u32[]{:S(2)}) %all-to-all-start.1) | async-done | bytes 2097184 | tf_op jit(solution)/shard_map/all_to_all | solution.py:186
  86.1 1.9 %copy.73 = bf16[2,2,256,1024]{2,3,1,0:T(8,128)(2,1)S(1)} copy(bf16[2,2,256,1024]{2,1,0,3:T(2,128)(2,1)} %all-to-all-done.1) | data formatting | bytes 4194304 | tf_op jit(solution)/shard_map/all_to_all | solution.py:186
  88.0 0.5 convert_bitcast_fusion
  88.5 0.0 copy-start.3
  88.5 0.5 copy.74
  89.0 1.1 copy-done.3
  90.1 1.2 subtract_bitcast_fusion
  91.3 1.7 %fusion.8 = f32[256,64,32]{0,2,1:T(8,128)S(1)} fusion(bf16[64,32,256]{2,0,1:T(8,128)(2,1)S(1)} %get-tuple-element.16), kind=kOutput, calls=%fused_computation.17 | convolution fusion | flops 269352960 | bytes 3145728 | tf_op jit(solution)/shard_map/dot_general | solution.py:206
  93.0 1.8 %fusion.10 = f32[256,64,32]{0,2,1:T(8,128)S(1)} fusion(bf16[64,32,256]{2,0,1:T(8,128)(2,1)S(1)} %get-tuple-element.16), kind=kOutput, calls=%fused_computation.19 | convolution fusion | flops 269352960 | bytes 3145728 | tf_op jit(solution)/shard_map/dot_general | solution.py:206
  94.8 1.9 %fusion.33 = f32[256,64,32]{0,2,1:T(8,128)S(1)} fusion(f32[256,64,32]{0,2,1:T(8,128)S(1)} %fusion.8, bf16[64,32,256]{2,0,1:T(8,128)(2,1)S(1)} %get-tuple-element.15), kind=kOutput, calls=%fused_computation.36 | convolution fusion | flops 269877248 | bytes 5242880 | tf_op jit(solution)/shard_map/dot_general | solution.py:206
  96.6 1.9 %fusion.30 = f32[256,64,32]{0,2,1:T(8,128)S(1)} fusion(f32[256,64,32]{0,2,1:T(8,128)S(1)} %fusion.10, bf16[64,32,256]{2,0,1:T(8,128)(2,1)S(1)} %get-tuple-element.15), kind=kOutput, calls=%fused_computation.35 | convolution fusion | flops 269877248 | bytes 5242880 | tf_op jit(solution)/shard_map/dot_general | solution.py:206
  98.5 1.1 fusion
  99.6 1.7 %fusion.42 = bf16[16,256,64]{1,0,2:T(8,128)(2,1)} fusion(f32[16,256,64]{1,0,2:T(8,128)S(1)} %fusion, f32[256,64,32]{0,2,1:T(8,128)S(1)} %fusion.33, f32[256,64,32]{0,2,1:T(8,128)S(1)} %fusion.30, f32[256,32]{0,1:T(8,128)S(1)} %get-tuple-element.25, f32[256,32]{0,1:T(8,128)S(1)} %get-tuple-element.26), kind=kOutput, calls=%fused_computation.39 | convolution fusion | flops 52698112 | bytes 5832704 | tf_op jit(solution)/shard_map/ja,pca->jpc/dot_general | solution.py:28
  101.3 1.2 convert_element_type.156
  102.5 0.2 copy.85
  102.7 26.4 %all_to_all.23 = bf16[32,128,64]{1,2,0:T(8,128)(2,1)S(1)} all-to-all(bf16[32,128,64]{1,2,0:T(8,128)(2,1)S(1)} %copy.85), channel_id=1, replica_groups=mesh['ctx'=16,'grp'=2] {'ctx','grp'}, dimensions={0} | all-to-all | bytes 1048576 | tf_op jit(solution)/shard_map/all_to_all | solution.py:231
  129.1 0.0 copy-start.1
  129.1 0.0 copy-start.4
  129.1 0.0 copy-start.5
  129.1 0.1 convert_bitcast_fusion.1
  129.3 0.1 copy.86
  129.3 1.4 %copy-done.1 = f32[128,4096]{0,1:T(8,128)S(1)} copy-done((f32[128,4096]{0,1:T(8,128)S(1)}, f32[128,4096]{0,1:T(8,128)}, u32[]{:S(2)}) %copy-start.1) | copy-done | bytes 2097176
  130.7 0.1 copy-done.4
  130.8 0.0 copy-done.5
  130.8 0.4 fusion.47
  131.2 1.0 copy.87
Async XLA Ops:
  0.9 6.9 %collective-permute-start = (bf16[2,6144]{1,0:T(2,128)(2,1)S(1)}, bf16[2,6144]{1,0:T(2,128)(2,1)S(1)}, u32[]{:S(2)}, u32[]{:S(2)}) collective-permute-start(bf16[2,6144]{1,0:T(2,128)(2,1)S(1)} %slice.54), channel_id=1, source_target_pairs={{0,1},{1,2},{2,3},{3,4},{4,5},{5,6},{6,7},{7,8},{8,9},{9,10},{10,1... | collective-permute-start | bytes 73736 | tf_op jit(solution)/shard_map/ppermute | solution.py:14
  11.5 1.3 %copy-start = (f32[128,4096]{0,1:T(8,128)}, f32[128,4096]{0,1:T(8,128)S(1)}, u32[]{:S(2)}) copy-start(f32[128,4096]{0,1:T(8,128)S(1)} %fusion.45) | copy-start | bytes 6291460
  13.7 21.9 %all-to-all-start = ((bf16[128,32,64]{0,2,1:T(8,128)(2,1)}), bf16[128,32,64]{0,2,1:T(8,128)(2,1)}, u32[]{:S(2)}, u32[]{:S(2)}) async-start(bf16[128,32,64]{0,2,1:T(8,128)(2,1)} %bitcast.118), calls=%async_computation | async-start | bytes 1048576 | tf_op jit(solution)/shard_map/all_to_all | solution.py:182
  40.9 45.2 %all-to-all-start.1 = ((bf16[2,2,256,1024]{2,1,0,3:T(2,128)(2,1)}), bf16[2,2,256,1024]{2,1,0,3:T(2,128)(2,1)}, u32[]{:S(2)}, u32[]{:S(2)}) async-start(bf16[2,2,256,1024]{2,1,0,3:T(2,128)(2,1)} %pad_maximum_fusion), calls=%async_computation.1 | async-start | bytes 4194304 | tf_op jit(solution)/shard_map/all_to_all | solution.py:186
  46.3 3.1 %copy-start.2 = (f32[16,256,64]{1,0,2:T(8,128)S(1)}, f32[16,256,64]{1,0,2:T(8,128)}, u32[]{:S(2)}) copy-start(f32[16,256,64]{1,0,2:T(8,128)} %reshape.100) | copy-start | bytes 3145732
  88.5 1.6 %copy-start.3 = (f32[256,64,32]{0,1,2:T(8,128)S(1)}, f32[256,64,32]{0,1,2:T(8,128)}, u32[]{:S(2)}) copy-start(f32[256,64,32]{0,1,2:T(8,128)} %fusion.27) | copy-start | bytes 6291460
  129.1 1.6 %copy-start.1 = (f32[128,4096]{0,1:T(8,128)S(1)}, f32[128,4096]{0,1:T(8,128)}, u32[]{:S(2)}) copy-start(f32[128,4096]{0,1:T(8,128)} %copy-done) | copy-start | bytes 6291460
  129.1 1.7 %copy-start.4 = (bf16[128,2048]{0,1:T(8,128)(2,1)S(1)}, bf16[128,2048]{0,1:T(8,128)(2,1)}, u32[]{:S(2)}) copy-start(bf16[128,2048]{0,1:T(8,128)(2,1)} %add_convert_fusion.1) | copy-start | bytes 1572868
  129.1 1.7 %copy-start.5 = (f32[2048]{0:T(1024)S(1)}, f32[2048]{0:T(1024)}, u32[]{:S(2)}) copy-start(f32[2048]{0:T(1024)} %param.7) | copy-start | bytes 24580

commit v5 on v1

--- a/solution.py
+++ b/solution.py
@@ -161,11 +161,11 @@
     outgoing = outgoing.reshape(row_count, devices, width)
     outgoing = outgoing.astype(jnp.bfloat16)
     tokens = lax.all_to_all(outgoing, everyone, split_axis=1, concat_axis=0, tiled=True)
-    tokens = tokens.reshape(block_count, block_len, width).astype(jnp.float32)
+    tokens = tokens.reshape(block_count, block_len, width).astype(jnp.float32).transpose(0, 2, 1)
 
     tokens, spectrum = lax.optimization_barrier((tokens, jnp.stack([spectrum_real, spectrum_imag])))
     spectrum = lax.all_to_all(spectrum, "ctx", split_axis=3, concat_axis=1, tiled=True)
-    spectrum = spectrum.transpose(0, 2, 3, 1).astype(jnp.float32)
+    spectrum = spectrum.transpose(0, 1, 3, 2).astype(jnp.float32)
     filter_real, filter_imag = spectrum[0], spectrum[1]
 
     residue = jnp.arange(residues, dtype=jnp.int32)
@@ -173,24 +173,24 @@
     position = jnp.arange(block_len, dtype=jnp.int32)
 
     across_cos, across_sin = angle_table(block_order, residue, residues)
-    folded_real = contract_high("jpc,ja->pca", tokens, across_cos)
-    folded_imag = -contract_high("jpc,ja->pca", tokens, across_sin)
-    turn_cos, turn_sin = angle_table(position, residue, fft_len)
+    folded_real = contract_high("ja,jcp->acp", across_cos, tokens)
+    folded_imag = -contract_high("ja,jcp->acp", across_sin, tokens)
+    turn_cos, turn_sin = angle_table(residue, position, fft_len)
     turn_cos, turn_sin = turn_cos[:, None, :], turn_sin[:, None, :]
     twisted_real = folded_real * turn_cos + folded_imag * turn_sin
     twisted_imag = folded_imag * turn_cos - folded_real * turn_sin
 
     within_cos, within_sin = angle_table(position, position, block_len)
-    lanes = width * residues
+    rows = residues * width
 
     def times(table_part, data, precision=lax.Precision.HIGH):
         return lax.dot_general(
+            data.reshape(rows, block_len),
             table_part,
-            data.reshape(block_len, lanes),
             (((1,), (0,)), ((), ())),
             precision=precision,
             preferred_element_type=jnp.float32,
-        ).reshape(block_len, width, residues)
+        ).reshape(residues, width, block_len)
 
     def inverse(table_part, data):
         return times(table_part, data, lax.Precision.DEFAULT)
@@ -203,9 +203,11 @@
     restored_imag = inverse(within_cos, product_imag) + inverse(within_sin, product_real)
     unturned_real = restored_real * turn_cos - restored_imag * turn_sin
     unturned_imag = restored_real * turn_sin + restored_imag * turn_cos
-    long_blocks = contract_high("ja,pca->jpc", across_cos, unturned_real) - contract_high(
-        "ja,pca->jpc", across_sin, unturned_imag
-    )
+    long_blocks = contract_high("ja,acp->jcp", across_cos, unturned_real) - contract_high(
+        "ja,acp->jcp", across_sin, unturned_imag
+    )
+    halves = block_len // row_count
+    long_blocks = long_blocks.reshape(block_count, width, halves, row_count).transpose(0, 2, 3, 1)
     long_blocks = (long_blocks * (1.0 / fft_len)).reshape(devices, row_count, width)
     long_blocks = long_blocks.astype(jnp.bfloat16)
     returned = lax.all_to_all(long_blocks, everyone, split_axis=0, concat_axis=0, tiled=True)

time: 131 us -> 131 us (level)
  no operation moved by 1% of the time
where the time goes in v5:
time: 131 us; the launch traced here: 130 us
  waiting for transfers between devices  34.6 us (26%)
  matrix products  26.6 us (20%)
  blocking collectives  26.4 us (20%)
  local copies, waits for them, and re-layouts  18.1 us (14%)
  starting transfers between devices  14.3 us (11%)
  other arithmetic  9.81 us (7%)
    all_to_all x1, blocking collectives, channel_parallel(): lax.all_to_all(long_blocks, everyone, split_axis=0, concat_axis=0, tiled=...  26.4 us
    all_to_all x1, waiting for transfers between devices, channel_parallel(): lax.all_to_all(spectrum, 'ctx', split_axis=3, concat_axis=1, tiled=True)  26.2 us
    dot_general x8, matrix products, times(): lax.dot_general(data.reshape(rows, block_len), table_part, (((1,), (0,)),...  22.4 us
    unnamed x15, local copies, waits for them, and re-layouts  9.49 us
    all_to_all x1, waiting for transfers between devices, channel_parallel(): lax.all_to_all(outgoing, everyone, split_axis=1, concat_axis=0, tiled=True)  8.34 us
    all_to_all x1, starting transfers between devices, channel_parallel(): lax.all_to_all(outgoing, everyone, split_axis=1, concat_axis=0, tiled=True)  5.79 us
    all_to_all x1, starting transfers between devices, channel_parallel(): lax.all_to_all(spectrum, 'ctx', split_axis=3, concat_axis=1, tiled=True)  4.53 us
    convert_element_type x1, other arithmetic, short_convolution(): short = short.astype(jnp.bfloat16)  4.37 us
  transfers between devices with their start and end apart: 3, of which 2 were waited for; matrix products, arithmetic and copies ran while one was open for 19% of the time, Pallas kernels for 0%

profile of v5, /device:TPU:1, one launch (start us, length us, event | category | flops | bytes accessed | tf_op | source)
XLA Modules:
  0.0 130.1 jit_solution(14907142256946853739)
XLA Ops:
  0.0 0.9 slice.35
  0.9 3.9 %collective-permute-start = (bf16[2,6144]{1,0:T(2,128)(2,1)S(1)}, bf16[2,6144]{1,0:T(2,128)(2,1)S(1)}, u32[]{:S(2)}, u32[]{:S(2)}) collective-permute-start(bf16[2,6144]{1,0:T(2,128)(2,1)S(1)} %slice.35), channel_id=1, source_target_pairs={{0,1},{1,2},{2,3},{3,4},{4,5},{5,6},{6,7},{7,8},{8,9},{9,10},{10,1... | collective-permute-start | bytes 73736 | tf_op jit(solution)/shard_map/ppermute | solution.py:14
  4.9 1.1 fusion.151
  6.0 1.9 %copy.52 = bf16[128,6144]{0,1:T(8,128)(2,1)S(1)} copy(bf16[128,6144]{1,0:T(8,128)(2,1)} %param.5) | data formatting | bytes 3145728 | tf_op args[0]
  7.9 0.0 collective-permute-done
  7.9 0.9 copy.53
  8.8 4.4 %add_convert_fusion = bf16[128,6144]{0,1:T(8,128)(2,1)S(1)} fusion(bf16[128,6144]{0,1:T(8,128)(2,1)S(1)} %copy.52, bf16[2,6144]{0,1:T(8,128)(2,1)S(1)} %copy.53, f32[6144]{0:T(1024)S(1)} %bitcast.97, f32[6144]{0:T(1024)S(1)} %bitcast.98, f32[6144]{0:T(1024)S(1)} %bitcast.96), kind=kLoop, calls=%fused_computation.3 | loop fusion | flops 11796480 | bytes 3244032 | tf_op jit(solution)/shard_map/convert_element_type | solution.py:134
  13.2 0.0 copy-start
  13.2 1.2 copy-done
  14.4 0.0 copy-start.4
  14.4 0.1 fusion.52
  14.5 0.8 copy.55
  15.4 5.8 %all-to-all-start = ((bf16[128,32,64]{0,2,1:T(8,128)(2,1)}), bf16[128,32,64]{0,2,1:T(8,128)(2,1)S(1)}, u32[]{:S(2)}, u32[]{:S(2)}) async-start(bf16[128,32,64]{0,2,1:T(8,128)(2,1)} %bitcast.6), calls=%async_computation | async-start | bytes 1048576 | tf_op jit(solution)/shard_map/all_to_all | solution.py:163
  21.2 0.0 copy-done.4
  21.2 0.9 copy.57
  22.1 2.5 %copy.58 = bf16[2,256,1024]{1,0,2:T(2,128)(2,1)S(1)} copy(bf16[2,256,1024]{2,1,0:T(8,128)(2,1)} %param.9) | data formatting | bytes 2097152 | tf_op args[4]
  24.6 4.0 %pad_maximum_fusion = bf16[2,2,256,1024]{2,1,0,3:T(2,128)(2,1)} fusion(bf16[1,2,256,1024]{2,1,0,3:T(2,128)(2,1)S(1)} %bitcast.91, bf16[1,2,256,1024]{2,1,0,3:T(2,128)(2,1)S(1)} %bitcast.90), kind=kLoop, calls=%fused_computation.6 | loop fusion | flops 1048576 | bytes 4194304 | tf_op jit(solution)/shard_map/stack | solution.py:166
  28.7 8.3 %all-to-all-done = bf16[128,32,64]{0,2,1:T(8,128)(2,1)S(1)} async-done(((bf16[128,32,64]{0,2,1:T(8,128)(2,1)}), bf16[128,32,64]{0,2,1:T(8,128)(2,1)S(1)}, u32[]{:S(2)}, u32[]{:S(2)}) %all-to-all-start) | async-done | bytes 524320 | tf_op jit(solution)/shard_map/all_to_all | solution.py:163
  37.0 0.1 convert_bitcast_fusion.2
  37.1 0.6 copy.56
  37.8 0.3 reshape.102
  38.1 4.5 %all-to-all-start.1 = ((bf16[2,2,256,1024]{2,1,0,3:T(2,128)(2,1)}), bf16[2,2,256,1024]{2,1,0,3:T(2,128)(2,1)}, u32[]{:S(2)}, u32[]{:S(2)}) async-start(bf16[2,2,256,1024]{2,1,0,3:T(2,128)(2,1)} %pad_maximum_fusion), calls=%async_computation.1 | async-start | bytes 4194304 | tf_op jit(solution)/shard_map/all_to_all | solution.py:167
  42.6 0.1 fusion.83
  42.7 1.1 fusion.89
  43.8 1.5 %multiply_add_fusion.1 = (f32[32,64,256]{2,0,1:T(8,128)S(1)}, f32[32,64,256]{2,0,1:T(8,128)S(1)}) fusion(f32[32,64,256]{2,0,1:T(8,128)S(1)} %fusion.89, f32[32,256]{1,0:T(8,128)S(1)} %get-tuple-element.16, f32[32,256]{1,0:T(8,128)S(1)} %get-tuple-element.17, f32[16,64,256]{2,0,1:T(8,128)S(1)} %bitcast.87), kind=kOutput, calls=%fused_computation.18 | convolution fusion | flops 54008832 | bytes 7405568 | tf_op jit(solution)/shard_map/ja,jcp->acp/dot_general | solution.py:28
  45.3 4.3 %fusion.16 = f32[32,64,256]{2,1,0:T(8,128)} fusion(f32[32,64,256]{2,0,1:T(8,128)S(1)} %get-tuple-element.12), kind=kOutput, calls=%fused_computation.27 | convolution fusion | flops 806223872 | bytes 4194304 | tf_op jit(solution)/shard_map/dot_general | solution.py:187
  49.7 3.0 %fusion.18 = f32[32,64,256]{2,1,0:T(8,128)S(1)} fusion(f32[32,64,256]{2,0,1:T(8,128)S(1)} %get-tuple-element.12), kind=kOutput, calls=%fused_computation.29 | convolution fusion | flops 806223872 | bytes 4194304 | tf_op jit(solution)/shard_map/dot_general | solution.py:187
  52.7 4.4 %fusion.24 = f32[32,64,256]{2,1,0:T(8,128)} fusion(f32[32,64,256]{2,1,0:T(8,128)S(1)} %fusion.18, f32[32,64,256]{2,0,1:T(8,128)S(1)} %get-tuple-element.11), kind=kOutput, calls=%fused_computation.35 | convolution fusion | flops 806748160 | bytes 6291456 | tf_op jit(solution)/shard_map/dot_general | solution.py:187
  57.1 26.2 %all-to-all-done.1 = bf16[2,2,256,1024]{2,1,0,3:T(2,128)(2,1)} async-done(((bf16[2,2,256,1024]{2,1,0,3:T(2,128)(2,1)}), bf16[2,2,256,1024]{2,1,0,3:T(2,128)(2,1)}, u32[]{:S(2)}, u32[]{:S(2)}) %all-to-all-start.1) | async-done | bytes 2097184 | tf_op jit(solution)/shard_map/all_to_all | solution.py:167
  83.3 2.1 %copy.61 = bf16[2,2,256,1024]{2,3,1,0:T(8,128)(2,1)S(1)} copy(bf16[2,2,256,1024]{2,1,0,3:T(2,128)(2,1)} %all-to-all-done.1) | data formatting | bytes 4194304 | tf_op jit(solution)/shard_map/all_to_all | solution.py:167
  85.4 0.6 convert_bitcast_fusion
  86.0 0.0 copy-start.2
  86.0 0.0 copy-start.3
  86.0 0.5 copy.62
  86.5 1.1 copy-done.2
  87.6 0.6 copy-done.3
  88.2 3.5 %multiply_subtract_fusion = (bf16[32,64,256]{2,1,0:T(8,128)(2,1)S(1)}, bf16[32,64,256]{2,1,0:T(8,128)(2,1)S(1)}) fusion(f32[32,64,256]{2,1,0:T(8,128)S(1)} %copy-done.2, f32[2,32,64,256]{3,2,1,0:T(8,128)S(1)} %bitcast.88, f32[32,64,256]{2,1,0:T(8,128)S(1)} %copy-done.3, f32[32,64,256]{2,0,1:T(8,128)S(1)} %get-tuple-element.11), kind=kOutput, calls=%fused_computation.16 | convolution fusion | flops 810942464 | bytes 12582912 | tf_op jit(solution)/shard_map/dot_general | solution.py:187
  91.7 1.7 %fusion.8 = f32[32,64,256]{2,0,1:T(8,128)S(1)} fusion(bf16[32,64,256]{2,1,0:T(8,128)(2,1)S(1)} %get-tuple-element.10), kind=kOutput, calls=%fused_computation.19 | convolution fusion | flops 269352960 | bytes 3145728 | tf_op jit(solution)/shard_map/dot_general | solution.py:187
  93.4 1.8 %fusion.10 = f32[32,64,256]{2,0,1:T(8,128)S(1)} fusion(bf16[32,64,256]{2,1,0:T(8,128)(2,1)S(1)} %get-tuple-element.10), kind=kOutput, calls=%fused_computation.21 | convolution fusion | flops 269352960 | bytes 3145728 | tf_op jit(solution)/shard_map/dot_general | solution.py:187
  95.2 1.9 %fusion.33 = f32[32,64,256]{2,0,1:T(8,128)S(1)} fusion(f32[32,64,256]{2,0,1:T(8,128)S(1)} %fusion.8, bf16[32,64,256]{2,1,0:T(8,128)(2,1)S(1)} %get-tuple-element.9), kind=kOutput, calls=%fused_computation.38 | convolution fusion | flops 269877248 | bytes 5242880 | tf_op jit(solution)/shard_map/dot_general | solution.py:187
  97.0 1.8 %fusion.30 = f32[32,64,256]{2,0,1:T(8,128)S(1)} fusion(f32[32,64,256]{2,0,1:T(8,128)S(1)} %fusion.10, bf16[32,64,256]{2,1,0:T(8,128)(2,1)S(1)} %get-tuple-element.9), kind=kOutput, calls=%fused_computation.37 | convolution fusion | flops 269877248 | bytes 5242880 | tf_op jit(solution)/shard_map/dot_general | solution.py:187
  98.9 0.8 fusion
  99.7 0.9 fusion.43
  100.6 0.1 convert_element_type.147
  100.7 0.2 copy.69
  100.9 26.4 %all_to_all.23 = bf16[32,128,64]{1,2,0:T(8,128)(2,1)S(1)} all-to-all(bf16[32,128,64]{1,2,0:T(8,128)(2,1)S(1)} %bitcast.95), channel_id=1, replica_groups=mesh['ctx'=16,'grp'=2] {'ctx','grp'}, dimensions={0} | all-to-all | bytes 1048576 | tf_op jit(solution)/shard_map/all_to_all | solution.py:213
  127.3 0.0 copy-start.1
  127.4 0.0 copy-start.5
  127.4 0.1 convert_bitcast_fusion.1
  127.5 0.1 copy.70
  127.5 1.2 copy-done.1
  128.8 0.0 copy-done.5
  128.8 0.3 fusion.47
  129.1 1.0 copy.71
Async XLA Ops:
  0.9 7.0 %collective-permute-start = (bf16[2,6144]{1,0:T(2,128)(2,1)S(1)}, bf16[2,6144]{1,0:T(2,128)(2,1)S(1)}, u32[]{:S(2)}, u32[]{:S(2)}) collective-permute-start(bf16[2,6144]{1,0:T(2,128)(2,1)S(1)} %slice.35), channel_id=1, source_target_pairs={{0,1},{1,2},{2,3},{3,4},{4,5},{5,6},{6,7},{7,8},{8,9},{9,10},{10,1... | collective-permute-start | bytes 73736 | tf_op jit(solution)/shard_map/ppermute | solution.py:14
  13.2 1.2 copy-start
  14.4 6.8 %copy-start.4 = (bf16[2,256,1024]{2,1,0:T(8,128)(2,1)S(1)}, bf16[2,256,1024]{2,1,0:T(8,128)(2,1)}, u32[]{:S(2)}) copy-start(bf16[2,256,1024]{2,1,0:T(8,128)(2,1)} %param.8) | copy-start | bytes 3145732
  15.4 21.6 %all-to-all-start = ((bf16[128,32,64]{0,2,1:T(8,128)(2,1)}), bf16[128,32,64]{0,2,1:T(8,128)(2,1)S(1)}, u32[]{:S(2)}, u32[]{:S(2)}) async-start(bf16[128,32,64]{0,2,1:T(8,128)(2,1)} %bitcast.6), calls=%async_computation | async-start | bytes 1048576 | tf_op jit(solution)/shard_map/all_to_all | solution.py:163
  38.1 45.2 %all-to-all-start.1 = ((bf16[2,2,256,1024]{2,1,0,3:T(2,128)(2,1)}), bf16[2,2,256,1024]{2,1,0,3:T(2,128)(2,1)}, u32[]{:S(2)}, u32[]{:S(2)}) async-start(bf16[2,2,256,1024]{2,1,0,3:T(2,128)(2,1)} %pad_maximum_fusion), calls=%async_computation.1 | async-start | bytes 4194304 | tf_op jit(solution)/shard_map/all_to_all | solution.py:167
  86.0 1.6 %copy-start.2 = (f32[32,64,256]{2,1,0:T(8,128)S(1)}, f32[32,64,256]{2,1,0:T(8,128)}, u32[]{:S(2)}) copy-start(f32[32,64,256]{2,1,0:T(8,128)} %fusion.24) | copy-start | bytes 6291460
  86.0 2.2 %copy-start.3 = (f32[32,64,256]{2,1,0:T(8,128)S(1)}, f32[32,64,256]{2,1,0:T(8,128)}, u32[]{:S(2)}) copy-start(f32[32,64,256]{2,1,0:T(8,128)} %fusion.16) | copy-start | bytes 6291460
  127.3 1.4 %copy-start.1 = (bf16[128,6144]{0,1:T(8,128)(2,1)S(1)}, bf16[128,6144]{0,1:T(8,128)(2,1)}, u32[]{:S(2)}) copy-start(bf16[128,6144]{0,1:T(8,128)(2,1)} %copy-done) | copy-start | bytes 4718596
  127.4 1.4 %copy-start.5 = (f32[2048]{0:T(1024)S(1)}, f32[2048]{0:T(1024)}, u32[]{:S(2)}) copy-start(f32[2048]{0:T(1024)} %param.7) | copy-start | bytes 24580

commit v6 on v5

--- a/solution.py
+++ b/solution.py
@@ -163,12 +163,24 @@
     tokens = lax.all_to_all(outgoing, everyone, split_axis=1, concat_axis=0, tiled=True)
     tokens = tokens.reshape(block_count, block_len, width).astype(jnp.float32).transpose(0, 2, 1)
 
-    tokens, spectrum = lax.optimization_barrier((tokens, jnp.stack([spectrum_real, spectrum_imag])))
+    middle = residues // 2
+    local_residues = spectrum_real.shape[0]
+    held = lax.axis_index("ctx") * local_residues + jnp.arange(local_residues, dtype=jnp.int32)
+    above = (held > middle)[:, None, None]
+    send_real = jnp.where(above, jnp.flip(spectrum_real, axis=1), spectrum_real)
+    send_imag = jnp.where(above, -jnp.flip(spectrum_imag, axis=1), spectrum_imag)
+    tokens, spectrum = lax.optimization_barrier((tokens, jnp.stack([send_real, send_imag])))
     spectrum = lax.all_to_all(spectrum, "ctx", split_axis=3, concat_axis=1, tiled=True)
     spectrum = spectrum.transpose(0, 1, 3, 2).astype(jnp.float32)
-    filter_real, filter_imag = spectrum[0], spectrum[1]
-
-    residue = jnp.arange(residues, dtype=jnp.int32)
+
+    def paired(part):
+        mirrored = part[1:middle] + part[residues - 1 : middle : -1]
+        return jnp.concatenate([part[:1], mirrored, part[middle : middle + 1]], axis=0)
+
+    filter_real, filter_imag = paired(spectrum[0]), paired(spectrum[1])
+    kept = middle + 1
+
+    residue = jnp.arange(kept, dtype=jnp.int32)
     block_order = jnp.arange(block_count, dtype=jnp.int32)
     position = jnp.arange(block_len, dtype=jnp.int32)
 
@@ -181,7 +193,7 @@
     twisted_imag = folded_imag * turn_cos - folded_real * turn_sin
 
     within_cos, within_sin = angle_table(position, position, block_len)
-    rows = residues * width
+    rows = kept * width
 
     def times(table_part, data, precision=lax.Precision.HIGH):
         return lax.dot_general(
@@ -190,7 +202,7 @@
             (((1,), (0,)), ((), ())),
             precision=precision,
             preferred_element_type=jnp.float32,
-        ).reshape(residues, width, block_len)
+        ).reshape(kept, width, block_len)
 
     def inverse(table_part, data):
         return times(table_part, data, lax.Precision.DEFAULT)

time: 131 us -> 159 us (1.21)
  local copies, waits for them, and re-layouts: 18.1 us -> 35.5 us
  other arithmetic: 9.81 us -> 17.9 us
  waiting for transfers between devices: 34.6 us -> 39.9 us
  matrix products: 26.6 us -> 24.2 us
    rev x0 -> x2, local copies, waits for them, and re-layouts: none -> 15.8 us  [the longest x1 7.96 us: channel_parallel(): jnp.flip(spectrum_imag, axis=1)]
    dot_general x8, matrix products: 22.4 us -> 13.7 us  [times(): lax.dot_general(data.reshape(rows, block_len), table_part, (((1,), (0,)),...]
    dot_general x4, matrix products: 4.27 us -> 10.5 us  [contract(): jnp.einsum(form, table, data, precision=precision, preferred_element_type...]
    all_to_all x1, waiting for transfers between devices: 26.2 us -> 32 us  [channel_parallel(): lax.all_to_all(spectrum, 'ctx', split_axis=3, concat_axis=1, tiled=True)]
    convert_element_type x1, other arithmetic: 4.37 us -> 8.35 us  [short_convolution(): short = short.astype(jnp.bfloat16)]
    another operation x1 -> x2, other arithmetic: 4.04 us -> 7.91 us  [channel_parallel(): jnp.stack([send_real, send_imag])]
    transpose x2, local copies, waits for them, and re-layouts: 0.91 us -> 3.13 us  [channel_parallel(): tokens.reshape(block_count, block_len, width).astype(jnp.float32)]
  transfers between devices with their start and end apart: 3 -> 3, of which waited for: 2 -> 2; matrix products, arithmetic and copies ran while one was open for 19% -> 25% of each run, Pallas kernels for 0% -> 0%
where the time goes in v6:
time: 159 us; the launch traced here: 158 us
  waiting for transfers between devices  39.9 us (25%)
  local copies, waits for them, and re-layouts  35.5 us (22%)
  blocking collectives  26.4 us (17%)
  matrix products  24.2 us (15%)
  other arithmetic  17.9 us (11%)
  starting transfers between devices  14.1 us (9%)
    all_to_all x1, waiting for transfers between devices, channel_parallel(): lax.all_to_all(spectrum, 'ctx', split_axis=3, concat_axis=1, tiled=True)  32 us
    all_to_all x1, blocking collectives, channel_parallel(): lax.all_to_all(long_blocks, everyone, split_axis=0, concat_axis=0, tiled=...  26.4 us
    dot_general x8, matrix products, times(): lax.dot_general(data.reshape(rows, block_len), table_part, (((1,), (0,)),...  13.7 us
    dot_general x4, matrix products, contract(): jnp.einsum(form, table, data, precision=precision, preferred_element_type...  10.5 us
    convert_element_type x1, other arithmetic, short_convolution(): short = short.astype(jnp.bfloat16)  8.35 us
    unnamed x15, local copies, waits for them, and re-layouts  8.05 us
    rev x1, local copies, waits for them, and re-layouts, channel_parallel(): jnp.flip(spectrum_imag, axis=1)  7.96 us
    all_to_all x1, waiting for transfers between devices, channel_parallel(): lax.all_to_all(outgoing, everyone, split_axis=1, concat_axis=0, tiled=True)  7.93 us
  transfers between devices with their start and end apart: 3, of which 2 were waited for; matrix products, arithmetic and copies ran while one was open for 25% of the time, Pallas kernels for 0%

profile of v6, /device:TPU:1, one launch (start us, length us, event | category | flops | bytes accessed | tf_op | source)
XLA Modules:
  0.0 158.3 jit_solution(13497297192577337250)
XLA Ops:
  0.0 0.9 slice.87
  0.9 3.9 %collective-permute-start = (bf16[2,6144]{1,0:T(2,128)(2,1)S(1)}, bf16[2,6144]{1,0:T(2,128)(2,1)S(1)}, u32[]{:S(2)}, u32[]{:S(2)}) collective-permute-start(bf16[2,6144]{1,0:T(2,128)(2,1)S(1)} %slice.87), channel_id=1, source_target_pairs={{0,1},{1,2},{2,3},{3,4},{4,5},{5,6},{6,7},{7,8},{8,9},{9,10},{10,1... | collective-permute-start | bytes 73736 | tf_op jit(solution)/shard_map/ppermute | solution.py:14
  4.9 1.1 fusion.136
  6.0 0.0 copy-start.4
  6.0 2.7 %copy.56 = bf16[128,6144]{0,1:T(8,128)(2,1)} copy(bf16[128,6144]{1,0:T(8,128)(2,1)} %param.5) | data formatting | bytes 3145728 | tf_op args[0]
  8.7 0.0 copy-done.4
  8.7 0.9 copy.61
  9.7 2.5 %copy.63 = bf16[2,256,1024]{1,0,2:T(2,128)(2,1)S(1)} copy(bf16[2,256,1024]{2,1,0:T(8,128)(2,1)} %param.9) | data formatting | bytes 2097152 | tf_op args[4]
  12.2 0.0 copy-start
  12.2 8.0 %rev.14 = bf16[2,256,1024]{1,0,2:T(2,128)(2,1)} reverse(bf16[2,256,1024]{1,0,2:T(2,128)(2,1)S(1)} %copy.63), dimensions={1} | reverse | bytes 2097152 | tf_op jit(solution)/shard_map/jit(_flip)/rev | solution.py:171
  20.1 7.9 %rev.13 = bf16[2,256,1024]{1,0,2:T(2,128)(2,1)} reverse(bf16[2,256,1024]{1,0,2:T(2,128)(2,1)S(1)} %copy.61), dimensions={1} | reverse | bytes 2097152 | tf_op jit(solution)/shard_map/jit(_flip)/rev | solution.py:170
  28.0 0.0 copy-done
  28.0 0.0 collective-permute-done
  28.0 1.6 %copy.57 = bf16[2,6144]{0,1:T(8,128)(2,1)} copy(bf16[2,6144]{1,0:T(2,128)(2,1)S(1)} %collective-permute-done) | data formatting | bytes 49152 | tf_op jit(solution)/shard_map/ppermute | solution.py:14
  29.6 8.3 %add_convert_fusion = bf16[128,6144]{0,1:T(8,128)(2,1)S(1)} fusion(bf16[128,6144]{0,1:T(8,128)(2,1)} %copy.56, bf16[2,6144]{0,1:T(8,128)(2,1)} %copy.57, f32[6144]{0:T(1024)S(1)} %bitcast.114, f32[6144]{0:T(1024)S(1)} %bitcast.115, f32[6144]{0:T(1024)S(1)} %bitcast.113), kind=kLoop, calls=%fused_computation.3 | loop fusion | flops 11796480 | bytes 3244032 | tf_op jit(solution)/shard_map/convert_element_type | solution.py:134
  38.0 0.1 fusion.22
  38.1 0.8 copy.59
  39.0 5.6 %all-to-all-start = ((bf16[128,32,64]{0,2,1:T(8,128)(2,1)}), bf16[128,32,64]{0,2,1:T(8,128)(2,1)S(1)}, u32[]{:S(2)}, u32[]{:S(2)}) async-start(bf16[128,32,64]{0,2,1:T(8,128)(2,1)} %bitcast.110), calls=%async_computation | async-start | bytes 1048576 | tf_op jit(solution)/shard_map/all_to_all | solution.py:163
  44.6 3.9 %fusion.20 = (bf16[1,2,256,1024]{2,1,0,3:T(2,128)(2,1)S(1)}, bf16[1,2,256,1024]{2,1,0,3:T(2,128)(2,1)S(1)}) fusion(bf16[2,256,1024]{1,0,2:T(2,128)(2,1)} %rev.13, bf16[2,256,1024]{1,0,2:T(2,128)(2,1)S(1)} %copy.61, pred[2]{0:T(512)(128)(4,1)S(1)} %add_compare_fusion, bf16[2,256,1024]{1,0,2:T(2,128)(2,1)} %copy-done, bf16[2,256,1024]{1,0,2:T(2,128)(2,1)} %rev.14), kind=kLoop, calls=%fused_computation.37 | loop fusion | flops 1572864 | bytes 6291458 | tf_op jit(solution)/shard_map/stack | solution.py:172
  48.5 4.0 %pad_maximum_fusion = bf16[2,2,256,1024]{2,1,0,3:T(2,128)(2,1)} fusion(bf16[1,2,256,1024]{2,1,0,3:T(2,128)(2,1)S(1)} %get-tuple-element.25, bf16[1,2,256,1024]{2,1,0,3:T(2,128)(2,1)S(1)} %get-tuple-element.24), kind=kLoop, calls=%fused_computation.4 | loop fusion | flops 1048576 | bytes 4194304 | tf_op jit(solution)/shard_map/stack | solution.py:172
  52.5 7.9 %all-to-all-done = bf16[128,32,64]{0,2,1:T(8,128)(2,1)S(1)} async-done(((bf16[128,32,64]{0,2,1:T(8,128)(2,1)}), bf16[128,32,64]{0,2,1:T(8,128)(2,1)S(1)}, u32[]{:S(2)}, u32[]{:S(2)}) %all-to-all-start) | async-done | bytes 524320 | tf_op jit(solution)/shard_map/all_to_all | solution.py:163
  60.4 0.1 convert_bitcast_fusion.2
  60.5 1.6 %copy.60 = f32[32,128,1,64]{1,0,3,2:T(8,128)} copy(f32[32,128,1,64]{1,3,0,2:T(8,128)S(1)} %convert_bitcast_fusion.2) | data formatting | bytes 2097152 | tf_op jit(solution)/shard_map/transpose | solution.py:164
  62.1 1.5 reshape.115
  63.7 4.5 %all-to-all-start.1 = ((bf16[2,2,256,1024]{2,1,0,3:T(2,128)(2,1)}), bf16[2,2,256,1024]{2,1,0,3:T(2,128)(2,1)}, u32[]{:S(2)}, u32[]{:S(2)}) async-start(bf16[2,2,256,1024]{2,1,0,3:T(2,128)(2,1)} %pad_maximum_fusion), calls=%async_computation.1 | async-start | bytes 4194304 | tf_op jit(solution)/shard_map/all_to_all | solution.py:173
  68.2 0.1 fusion.69
  68.3 0.9 fusion.77
  69.2 1.2 multiply_add_fusion
  70.4 0.0 copy-start.1
  70.4 1.8 %fusion.29 = f32[17,64,256]{2,1,0:T(8,128)S(1)} fusion(f32[17,64,256]{2,0,1:T(8,128)S(1)} %get-tuple-element.19), kind=kOutput, calls=%fused_computation.50 | convolution fusion | flops 428736512 | bytes 2228224 | tf_op jit(solution)/shard_map/dot_general | solution.py:199
  72.3 1.8 %fusion.25 = f32[17,64,256]{2,1,0:T(8,128)S(1)} fusion(f32[17,64,256]{2,0,1:T(8,128)S(1)} %get-tuple-element.20), kind=kOutput, calls=%fused_computation.46 | convolution fusion | flops 428736512 | bytes 2228224 | tf_op jit(solution)/shard_map/dot_general | solution.py:199
  74.1 0.0 copy-done.1
  74.1 2.9 %convolution_add_fusion = f32[17,64,256]{2,1,0:T(8,128)} fusion(f32[17,64,256]{2,1,0:T(8,128)S(1)} %fusion.29, f32[17,64,256]{2,0,1:T(8,128)S(1)} %get-tuple-element.20), kind=kOutput, calls=%fused_computation.23 | convolution fusion | flops 429015040 | bytes 3342336 | tf_op jit(solution)/shard_map/dot_general | solution.py:199
  77.0 32.0 %all-to-all-done.1 = bf16[2,2,256,1024]{2,1,0,3:T(2,128)(2,1)} async-done(((bf16[2,2,256,1024]{2,1,0,3:T(2,128)(2,1)}), bf16[2,2,256,1024]{2,1,0,3:T(2,128)(2,1)}, u32[]{:S(2)}, u32[]{:S(2)}) %all-to-all-start.1) | async-done | bytes 2097184 | tf_op jit(solution)/shard_map/all_to_all | solution.py:173
  108.9 1.9 %copy.68 = bf16[2,2,256,1024]{2,3,1,0:T(8,128)(2,1)S(1)} copy(bf16[2,2,256,1024]{2,1,0,3:T(2,128)(2,1)} %all-to-all-done.1) | data formatting | bytes 4194304 | tf_op jit(solution)/shard_map/all_to_all | solution.py:173
  110.8 0.5 convert_bitcast_fusion
  111.3 0.5 copy.69
  111.9 0.2 slice_bitcast_fusion.2
  112.1 0.0 copy-start.2
  112.1 0.0 copy-start.3
  112.1 0.3 fusion.24
  112.4 1.1 copy-done.2
  113.5 0.3 copy-done.3
  113.8 2.0 %multiply_subtract_fusion.1 = (bf16[17,64,256]{2,1,0:T(8,128)(2,1)S(1)}, bf16[17,64,256]{2,1,0:T(8,128)(2,1)S(1)}) fusion(f32[17,64,256]{2,1,0:T(8,128)S(1)} %copy-done.3, f32[1,64,256]{2,1,0:T(8,128)S(1)} %get-tuple-element.12, f32[15,64,256]{2,1,0:T(8,128)S(1)} %get-tuple-element.16, f32[1,64,256]{2,1,0:T(8,128)S(1)} %get-tuple-element.13, ...), kind=kOutput, calls=%fused_computation.30 | convolution fusion | flops 432357376 | bytes 6684672 | tf_op jit(solution)/shard_map/dot_general | solution.py:199
  115.8 1.4 fusion.38
  117.3 1.2 fusion.46
  118.5 1.2 fusion.44
  119.7 1.2 fusion.40
  121.0 4.2 %fusion.1 = f32[16,64,256]{2,0,1:T(8,128)S(1)} fusion(f32[17,64,256]{2,1,0:T(8,128)S(1)} %fusion.40, f32[17,64,256]{2,1,0:T(8,128)S(1)} %fusion.46, f32[17,64,256]{2,1,0:T(8,128)S(1)} %fusion.38, f32[17,64,256]{2,1,0:T(8,128)S(1)} %fusion.44, f32[17,256]{1,0:T(8,128)S(1)} %get-tuple-element.26, f32[17,256]{1,0:T(8,128)S(1)} %get-tuple-element.27), kind=kOutput, calls=%fused_computation.11 | convolution fusion | flops 28135136 | bytes 5539840 | tf_op jit(solution)/shard_map/ja,acp->jcp/dot_general | solution.py:28
  125.2 4.3 %fusion.15 = bf16[16,64,256]{2,0,1:T(8,128)(2,1)S(1)} fusion(f32[16,64,256]{2,0,1:T(8,128)S(1)} %fusion.1, f32[17,64,256]{2,1,0:T(8,128)S(1)} %fusion.40, f32[17,64,256]{2,1,0:T(8,128)S(1)} %fusion.46, f32[17,64,256]{2,1,0:T(8,128)S(1)} %fusion.38, f32[17,64,256]{2,1,0:T(8,128)S(1)} %fusion.44, f32[17,256]{1,0:T(8,128)S(1)} %get-tuple-element.26, ...), kind=kOutput, calls=%fused_computation.26 | convolution fusion | flops 28921568 | bytes 6064128 | tf_op jit(solution)/shard_map/ja,acp->jcp/dot_general | solution.py:28
  129.4 0.1 convert_element_type.147
  129.6 0.2 copy.76
  129.8 26.4 %all_to_all.23 = bf16[32,128,64]{1,2,0:T(8,128)(2,1)S(1)} all-to-all(bf16[32,128,64]{1,2,0:T(8,128)(2,1)S(1)} %bitcast.112), channel_id=1, replica_groups=mesh['ctx'=16,'grp'=2] {'ctx','grp'}, dimensions={0} | all-to-all | bytes 1048576 | tf_op jit(solution)/shard_map/all_to_all | solution.py:225
  156.2 0.0 copy-start.5
  156.2 0.1 convert_bitcast_fusion.1
  156.3 0.1 copy.77
  156.4 0.5 copy-done.5
  156.9 0.4 fusion.19
  157.3 1.0 copy.78
  (2 shorter events, 0.0 us)
Async XLA Ops:
  0.9 27.1 %collective-permute-start = (bf16[2,6144]{1,0:T(2,128)(2,1)S(1)}, bf16[2,6144]{1,0:T(2,128)(2,1)S(1)}, u32[]{:S(2)}, u32[]{:S(2)}) collective-permute-start(bf16[2,6144]{1,0:T(2,128)(2,1)S(1)} %slice.87), channel_id=1, source_target_pairs={{0,1},{1,2},{2,3},{3,4},{4,5},{5,6},{6,7},{7,8},{8,9},{9,10},{10,1... | collective-permute-start | bytes 73736 | tf_op jit(solution)/shard_map/ppermute | solution.py:14
  6.0 2.7 %copy-start.4 = (bf16[2,256,1024]{2,1,0:T(8,128)(2,1)S(1)}, bf16[2,256,1024]{2,1,0:T(8,128)(2,1)}, u32[]{:S(2)}) copy-start(bf16[2,256,1024]{2,1,0:T(8,128)(2,1)} %param.8) | copy-start | bytes 3145732
  12.2 15.9 %copy-start = (bf16[2,256,1024]{1,0,2:T(2,128)(2,1)}, bf16[2,256,1024]{1,0,2:T(2,128)(2,1)S(1)}, u32[]{:S(2)}) copy-start(bf16[2,256,1024]{1,0,2:T(2,128)(2,1)S(1)} %copy.63) | copy-start | bytes 3145732
  39.0 21.5 %all-to-all-start = ((bf16[128,32,64]{0,2,1:T(8,128)(2,1)}), bf16[128,32,64]{0,2,1:T(8,128)(2,1)S(1)}, u32[]{:S(2)}, u32[]{:S(2)}) async-start(bf16[128,32,64]{0,2,1:T(8,128)(2,1)} %bitcast.110), calls=%async_computation | async-start | bytes 1048576 | tf_op jit(solution)/shard_map/all_to_all | solution.py:163
  63.7 45.2 %all-to-all-start.1 = ((bf16[2,2,256,1024]{2,1,0,3:T(2,128)(2,1)}), bf16[2,2,256,1024]{2,1,0,3:T(2,128)(2,1)}, u32[]{:S(2)}, u32[]{:S(2)}) async-start(bf16[2,2,256,1024]{2,1,0,3:T(2,128)(2,1)} %pad_maximum_fusion), calls=%async_computation.1 | async-start | bytes 4194304 | tf_op jit(solution)/shard_map/all_to_all | solution.py:173
  70.4 3.7 %copy-start.1 = (f32[17,64,256]{2,0,1:T(8,128)}, f32[17,64,256]{2,0,1:T(8,128)S(1)}, u32[]{:S(2)}) copy-start(f32[17,64,256]{2,0,1:T(8,128)S(1)} %get-tuple-element.19) | copy-start | bytes 3342340
  112.1 1.4 copy-start.2
  112.1 1.7 %copy-start.3 = (f32[17,64,256]{2,1,0:T(8,128)S(1)}, f32[17,64,256]{2,1,0:T(8,128)}, u32[]{:S(2)}) copy-start(f32[17,64,256]{2,1,0:T(8,128)} %convolution_add_fusion) | copy-start | bytes 3342340
  156.2 0.7 copy-start.5

commit v7 on v1

--- a/solution.py
+++ b/solution.py
@@ -160,11 +160,20 @@
     outgoing = gated.reshape(row_count, group_count, block_count, width).transpose(0, 2, 1, 3)
     outgoing = outgoing.reshape(row_count, devices, width)
     outgoing = outgoing.astype(jnp.bfloat16)
+
+    def spread(part):
+        return lax.all_to_all(part, "ctx", split_axis=3, concat_axis=1, tiled=True)
+
+    early = spread(jnp.stack([spectrum_real[0::2], spectrum_imag[0::2]]))
+    early, outgoing = lax.optimization_barrier((early, outgoing))
     tokens = lax.all_to_all(outgoing, everyone, split_axis=1, concat_axis=0, tiled=True)
     tokens = tokens.reshape(block_count, block_len, width).astype(jnp.float32)
 
-    tokens, spectrum = lax.optimization_barrier((tokens, jnp.stack([spectrum_real, spectrum_imag])))
-    spectrum = lax.all_to_all(spectrum, "ctx", split_axis=3, concat_axis=1, tiled=True)
+    tokens, late = lax.optimization_barrier(
+        (tokens, jnp.stack([spectrum_real[1::2], spectrum_imag[1::2]]))
+    )
+    late = spread(late)
+    spectrum = jnp.stack([early, late], axis=2).reshape(2, residues, block_len, width)
     spectrum = spectrum.transpose(0, 2, 3, 1).astype(jnp.float32)
     filter_real, filter_imag = spectrum[0], spectrum[1]
 

time: 131 us -> 136 us (1.038)
  starting transfers between devices: 14.3 us -> 20.5 us
  other arithmetic: 9.81 us -> 5.68 us
  blocking collectives: 26.4 us -> 22.3 us
  waiting for transfers between devices: 34.6 us -> 38.5 us
  local copies, waits for them, and re-layouts: 18.2 us -> 21.4 us
    all_to_all x1, waiting for transfers between devices: 8.34 us -> 15.7 us  [channel_parallel(): lax.all_to_all(outgoing, everyone, split_axis=1, concat_axis=0, tiled=True)]
    all_to_all x1 -> x2, starting transfers between devices: 4.53 us -> 11.2 us  [spread(): return lax.all_to_all(part, 'ctx', split_axis=3, concat_axis=1, tiled=True)]
    another operation x0 -> x2, local copies, waits for them, and re-layouts: none -> 4.75 us  [the longest x1 2.71 us: channel_parallel(): jnp.stack([spectrum_real[1::2], spectrum_imag[1::2]])]
    unnamed x15 -> x21, local copies, waits for them, and re-layouts: 9.49 us -> 5.04 us
    all_to_all x1, blocking collectives: 26.4 us -> 22.3 us  [channel_parallel(): lax.all_to_all(long_blocks, everyone, split_axis=0, concat_axis=0, tiled=...]
    another operation x1 -> x2, other arithmetic: 4.04 us -> 0.2 us  [the longest x1 0.1 us: channel_parallel(): jnp.stack([spectrum_real[1::2], spectrum_imag[1::2]])]
    all_to_all x1 -> x2, waiting for transfers between devices: 26.2 us -> 22.8 us  [spread(): return lax.all_to_all(part, 'ctx', split_axis=3, concat_axis=1, tiled=True)]
    optimization_barrier x0 -> x1, local copies, waits for them, and re-layouts: none -> 2.11 us  [channel_parallel(): lax.optimization_barrier((tokens, jnp.stack([spectrum_real[1::2], spectru...]
  transfers between devices with their start and end apart: 3 -> 4, of which waited for: 2 -> 3; matrix products, arithmetic and copies ran while one was open for 19% -> 20% of each run, Pallas kernels for 0% -> 0%
where the time goes in v7:
time: 136 us; the launch traced here: 135 us
  waiting for transfers between devices  38.5 us (28%)
  matrix products  26.5 us (19%)
  blocking collectives  22.3 us (16%)
  local copies, waits for them, and re-layouts  21.4 us (16%)
  starting transfers between devices  20.5 us (15%)
  other arithmetic  5.68 us (4%)
    all_to_all x2, waiting for transfers between devices, spread(): return lax.all_to_all(part, 'ctx', split_axis=3, concat_axis=1, tiled=True)  22.8 us
    all_to_all x1, blocking collectives, channel_parallel(): lax.all_to_all(long_blocks, everyone, split_axis=0, concat_axis=0, tiled=...  22.3 us
    dot_general x8, matrix products, times(): lax.dot_general(table_part, data.reshape(block_len, lanes), (((1,), (0,))...  22.2 us
    all_to_all x1, waiting for transfers between devices, channel_parallel(): lax.all_to_all(outgoing, everyone, split_axis=1, concat_axis=0, tiled=True)  15.7 us
    all_to_all x2, starting transfers between devices, spread(): return lax.all_to_all(part, 'ctx', split_axis=3, concat_axis=1, tiled=True)  11.2 us
    all_to_all x1, starting transfers between devices, channel_parallel(): lax.all_to_all(outgoing, everyone, split_axis=1, concat_axis=0, tiled=True)  5.32 us
    unnamed x21, local copies, waits for them, and re-layouts  5.04 us
    convert_element_type x1, other arithmetic, short_convolution(): short = short.astype(jnp.bfloat16)  4.37 us
  transfers between devices with their start and end apart: 4, of which 3 were waited for; matrix products, arithmetic and copies ran while one was open for 20% of the time, Pallas kernels for 0%

profile of v7, /device:TPU:1, one launch (start us, length us, event | category | flops | bytes accessed | tf_op | source)
XLA Modules:
  0.0 135.1 jit_solution(10069189976367178016)
XLA Ops:
  0.0 0.9 slice.51
  0.9 3.9 %collective-permute-start = (bf16[2,6144]{1,0:T(2,128)(2,1)S(1)}, bf16[2,6144]{1,0:T(2,128)(2,1)S(1)}, u32[]{:S(2)}, u32[]{:S(2)}) collective-permute-start(bf16[2,6144]{1,0:T(2,128)(2,1)S(1)} %slice.51), channel_id=1, source_target_pairs={{0,1},{1,2},{2,3},{3,4},{4,5},{5,6},{6,7},{7,8},{8,9},{9,10},{10,1... | collective-permute-start | bytes 73736 | tf_op jit(solution)/shard_map/ppermute | solution.py:14
  4.9 2.7 %slice_bitcast_fusion.2 = (bf16[1,1,256,1024]{3,2,1,0:T(8,128)(2,1)}, bf16[1,1,256,1024]{3,2,1,0:T(8,128)(2,1)S(1)}, bf16[1,1,256,1024]{3,2,1,0:T(8,128)(2,1)S(1)}, bf16[1,1,256,1024]{3,2,1,0:T(8,128)(2,1)}) fusion(bf16[2,256,1024]{2,1,0:T(8,128)(2,1)} %param.9, bf16[2,256,1024]{2,1,0:T(8,128)(2,1)} %param.8), kind=kLoop, calls=%fused_computation.56 | loop fusion | bytes 4194304 | tf_op jit(solution)/shard_map/stack | solution.py:173
  7.6 0.1 pad_maximum_fusion.1
  7.7 0.0 copy-start.8
  7.7 0.0 copy-start.7
  7.7 2.0 %copy.96 = bf16[2,1,256,1024]{2,0,1,3:T(2,128)(2,1)} copy(bf16[2,1,256,1024]{3,2,1,0:T(8,128)(2,1)S(1)} %pad_maximum_fusion.1) | data formatting | bytes 2097152 | tf_op jit(solution)/shard_map/stack | solution.py:167
  9.7 6.8 %all-to-all-start = ((bf16[2,1,256,1024]{2,0,1,3:T(2,128)(2,1)}), bf16[2,1,256,1024]{2,0,1,3:T(2,128)(2,1)}, u32[]{:S(2)}, u32[]{:S(2)}) async-start(bf16[2,1,256,1024]{2,0,1,3:T(2,128)(2,1)} %copy.96), calls=%async_computation | async-start | bytes 2097152 | tf_op jit(solution)/shard_map/all_to_all | solution.py:165
  16.5 0.0 copy-done.8
  16.6 0.1 fusion.151
  16.6 0.0 copy-done.7
  16.6 0.9 copy.93
  17.5 0.0 collective-permute-done
  17.5 0.9 copy.94
  18.4 4.4 %add_convert_fusion = bf16[128,6144]{0,1:T(8,128)(2,1)S(1)} fusion(bf16[128,6144]{0,1:T(8,128)(2,1)S(1)} %copy.93, bf16[2,6144]{0,1:T(8,128)(2,1)S(1)} %copy.94, f32[6144]{0:T(1024)S(1)} %bitcast.128, f32[6144]{0:T(1024)S(1)} %bitcast.129, f32[6144]{0:T(1024)S(1)} %bitcast.127), kind=kLoop, calls=%fused_computation.2 | loop fusion | flops 11796480 | bytes 3244032 | tf_op jit(solution)/shard_map/convert_element_type | solution.py:134
  22.8 0.0 copy-start
  22.8 1.2 copy-done
  24.0 0.1 fusion.52
  24.1 0.0 copy-start.5
  24.2 0.0 copy-start.6
  24.2 0.8 copy.98
  25.0 14.8 %all-to-all-done = bf16[2,1,256,1024]{2,0,1,3:T(2,128)(2,1)} async-done(((bf16[2,1,256,1024]{2,0,1,3:T(2,128)(2,1)}), bf16[2,1,256,1024]{2,0,1,3:T(2,128)(2,1)}, u32[]{:S(2)}, u32[]{:S(2)}) %all-to-all-start) | async-done | bytes 1048608 | tf_op jit(solution)/shard_map/all_to_all | solution.py:165
  39.8 2.3 %copy.97 = bf16[2,1,256,1024]{2,3,0,1:T(8,128)(2,1)} copy(bf16[2,1,256,1024]{2,0,1,3:T(2,128)(2,1)} %all-to-all-done) | data formatting | bytes 2097152 | tf_op jit(solution)/shard_map/all_to_all | solution.py:165
  42.2 5.3 %all-to-all-start.1 = ((bf16[128,32,64]{0,2,1:T(8,128)(2,1)}), bf16[128,32,64]{0,2,1:T(8,128)(2,1)S(1)}, u32[]{:S(2)}, u32[]{:S(2)}) async-start(bf16[128,32,64]{0,2,1:T(8,128)(2,1)} %bitcast.12), calls=%async_computation.1 | async-start | bytes 1048576 | tf_op jit(solution)/shard_map/all_to_all | solution.py:169
  47.5 0.0 copy-done.5
  47.5 0.0 copy-done.6
  47.5 0.1 pad_maximum_fusion.2
  47.6 15.7 %all-to-all-done.1 = bf16[128,32,64]{0,2,1:T(8,128)(2,1)S(1)} async-done(((bf16[128,32,64]{0,2,1:T(8,128)(2,1)}), bf16[128,32,64]{0,2,1:T(8,128)(2,1)S(1)}, u32[]{:S(2)}, u32[]{:S(2)}) %all-to-all-start.1) | async-done | bytes 524320 | tf_op jit(solution)/shard_map/all_to_all | solution.py:169
  63.4 0.1 convert_bitcast_fusion.1
  63.5 0.6 copy.99
  64.1 0.3 reshape.100
  64.4 2.1 %copy.102 = bf16[2,1,256,1024]{2,0,1,3:T(2,128)(2,1)} copy(bf16[2,1,256,1024]{3,2,1,0:T(8,128)(2,1)S(1)} %pad_maximum_fusion.2) | data formatting | bytes 2097152 | tf_op jit(solution)/shard_map/optimization_barrier | solution.py:172
  66.5 4.4 %all-to-all-start.2 = ((bf16[2,1,256,1024]{2,0,1,3:T(2,128)(2,1)}), bf16[2,1,256,1024]{2,0,1,3:T(2,128)(2,1)}, u32[]{:S(2)}, u32[]{:S(2)}) async-start(bf16[2,1,256,1024]{2,0,1,3:T(2,128)(2,1)} %copy.102), calls=%async_computation.2 | async-start | bytes 2097152 | tf_op jit(solution)/shard_map/all_to_all | solution.py:165
  70.9 0.1 fusion.83
  71.1 1.1 fusion.89
  72.2 1.5 %add_bitcast_fusion.1 = (f32[64,32,256]{2,1,0:T(8,128)S(1)}, f32[64,32,256]{2,1,0:T(8,128)S(1)}) fusion(f32[256,64,32]{0,2,1:T(8,128)S(1)} %fusion.89, f32[256,32]{0,1:T(8,128)S(1)} %get-tuple-element.26, f32[256,32]{0,1:T(8,128)S(1)} %get-tuple-element.27, f32[16,256,64]{1,0,2:T(8,128)S(1)} %reshape.100), kind=kOutput, calls=%fused_computation.17 | convolution fusion | flops 54008832 | bytes 7405568 | tf_op jit(solution)/shard_map/jpc,ja->pca/dot_general | solution.py:28
  73.6 4.3 %fusion.16 = f32[256,64,32]{0,1,2:T(8,128)} fusion(f32[64,32,256]{2,1,0:T(8,128)S(1)} %get-tuple-element.16), kind=kOutput, calls=%fused_computation.26 | convolution fusion | flops 806223872 | bytes 4194304 | tf_op jit(solution)/shard_map/dot_general | solution.py:196
  78.0 3.0 %fusion.18 = f32[256,64,32]{0,1,2:T(8,128)S(1)} fusion(f32[64,32,256]{2,1,0:T(8,128)S(1)} %get-tuple-element.16), kind=kOutput, calls=%fused_computation.28 | convolution fusion | flops 806223872 | bytes 4194304 | tf_op jit(solution)/shard_map/dot_general | solution.py:196
  81.0 4.4 %fusion.24 = f32[256,64,32]{0,1,2:T(8,128)} fusion(f32[256,64,32]{0,1,2:T(8,128)S(1)} %fusion.18, f32[64,32,256]{2,1,0:T(8,128)S(1)} %get-tuple-element.15), kind=kOutput, calls=%fused_computation.34 | convolution fusion | flops 806748160 | bytes 6291456 | tf_op jit(solution)/shard_map/dot_general | solution.py:196
  85.4 7.9 %all-to-all-done.2 = bf16[2,1,256,1024]{2,0,1,3:T(2,128)(2,1)} async-done(((bf16[2,1,256,1024]{2,0,1,3:T(2,128)(2,1)}), bf16[2,1,256,1024]{2,0,1,3:T(2,128)(2,1)}, u32[]{:S(2)}, u32[]{:S(2)}) %all-to-all-start.2) | async-done | bytes 1048608 | tf_op jit(solution)/shard_map/all_to_all | solution.py:165
  93.3 1.6 %copy.103 = bf16[2,1,256,1024]{2,3,0,1:T(8,128)(2,1)S(1)} copy(bf16[2,1,256,1024]{2,0,1,3:T(2,128)(2,1)} %all-to-all-done.2) | data formatting | bytes 2097152 | tf_op jit(solution)/shard_map/all_to_all | solution.py:165
  94.9 0.0 copy-done.4
  94.9 0.3 maximum_convert_fusion
  95.2 0.0 copy-start.2
  95.2 0.0 copy-start.3
  95.2 0.5 copy.104
  95.7 1.1 copy-done.2
  96.7 0.6 copy-done.3
  97.4 3.3 %subtract_bitcast_fusion = (bf16[64,32,256]{2,0,1:T(8,128)(2,1)S(1)}, bf16[64,32,256]{2,0,1:T(8,128)(2,1)S(1)}) fusion(f32[256,64,32]{0,1,2:T(8,128)S(1)} %copy-done.2, f32[2,256,64,32]{1,2,3,0:T(8,128)S(1)} %bitcast.122, f32[256,64,32]{0,1,2:T(8,128)S(1)} %copy-done.3, f32[64,32,256]{2,1,0:T(8,128)S(1)} %get-tuple-element.15), kind=kOutput, calls=%fused_computation.15 | convolution fusion | flops 810942464 | bytes 12582912 | tf_op jit(solution)/shard_map/dot_general | solution.py:196
  100.7 1.7 %fusion.8 = f32[256,64,32]{0,2,1:T(8,128)S(1)} fusion(bf16[64,32,256]{2,0,1:T(8,128)(2,1)S(1)} %get-tuple-element.14), kind=kOutput, calls=%fused_computation.18 | convolution fusion | flops 269352960 | bytes 3145728 | tf_op jit(solution)/shard_map/dot_general | solution.py:196
  102.5 1.7 %fusion.10 = f32[256,64,32]{0,2,1:T(8,128)S(1)} fusion(bf16[64,32,256]{2,0,1:T(8,128)(2,1)S(1)} %get-tuple-element.14), kind=kOutput, calls=%fused_computation.20 | convolution fusion | flops 269352960 | bytes 3145728 | tf_op jit(solution)/shard_map/dot_general | solution.py:196
  104.2 1.9 %fusion.33 = f32[256,64,32]{0,2,1:T(8,128)S(1)} fusion(f32[256,64,32]{0,2,1:T(8,128)S(1)} %fusion.8, bf16[64,32,256]{2,0,1:T(8,128)(2,1)S(1)} %get-tuple-element.13), kind=kOutput, calls=%fused_computation.37 | convolution fusion | flops 269877248 | bytes 5242880 | tf_op jit(solution)/shard_map/dot_general | solution.py:196
  106.1 1.9 %fusion.30 = f32[256,64,32]{0,2,1:T(8,128)S(1)} fusion(f32[256,64,32]{0,2,1:T(8,128)S(1)} %fusion.10, bf16[64,32,256]{2,0,1:T(8,128)(2,1)S(1)} %get-tuple-element.13), kind=kOutput, calls=%fused_computation.36 | convolution fusion | flops 269877248 | bytes 5242880 | tf_op jit(solution)/shard_map/dot_general | solution.py:196
  108.0 0.8 fusion
  108.8 0.9 fusion.43
  109.7 0.2 convert_element_type.136
  109.8 0.2 copy.117
  110.1 22.3 %all_to_all.47 = bf16[32,128,64]{1,2,0:T(8,128)(2,1)S(1)} all-to-all(bf16[32,128,64]{1,2,0:T(8,128)(2,1)S(1)} %copy.117), channel_id=1, replica_groups=mesh['ctx'=16,'grp'=2] {'ctx','grp'}, dimensions={0} | all-to-all | bytes 1048576 | tf_op jit(solution)/shard_map/all_to_all | solution.py:220
  132.3 0.1 convert_bitcast_fusion
  132.4 0.1 copy.118
  132.5 1.2 copy-done.1
  133.7 0.0 copy-done.9
  133.7 0.3 fusion.47
  134.1 1.0 copy.119
  (3 shorter events, 0.0 us)
Async XLA Ops:
  0.9 16.6 %collective-permute-start = (bf16[2,6144]{1,0:T(2,128)(2,1)S(1)}, bf16[2,6144]{1,0:T(2,128)(2,1)S(1)}, u32[]{:S(2)}, u32[]{:S(2)}) collective-permute-start(bf16[2,6144]{1,0:T(2,128)(2,1)S(1)} %slice.51), channel_id=1, source_target_pairs={{0,1},{1,2},{2,3},{3,4},{4,5},{5,6},{6,7},{7,8},{8,9},{9,10},{10,1... | collective-permute-start | bytes 73736 | tf_op jit(solution)/shard_map/ppermute | solution.py:14
  7.7 8.9 %copy-start.8 = (f32[3,6144]{1,0:T(4,128)S(1)}, f32[3,6144]{1,0:T(4,128)}, u32[]{:S(2)}) copy-start(f32[3,6144]{1,0:T(4,128)} %param.6) | copy-start | bytes 221188
  7.7 8.9 %copy-start.7 = (bf16[128,6144]{1,0:T(8,128)(2,1)S(1)}, bf16[128,6144]{1,0:T(8,128)(2,1)}, u32[]{:S(2)}) copy-start(bf16[128,6144]{1,0:T(8,128)(2,1)} %param.5) | copy-start | bytes 4718596
  9.7 30.1 %all-to-all-start = ((bf16[2,1,256,1024]{2,0,1,3:T(2,128)(2,1)}), bf16[2,1,256,1024]{2,0,1,3:T(2,128)(2,1)}, u32[]{:S(2)}, u32[]{:S(2)}) async-start(bf16[2,1,256,1024]{2,0,1,3:T(2,128)(2,1)} %copy.96), calls=%async_computation | async-start | bytes 2097152 | tf_op jit(solution)/shard_map/all_to_all | solution.py:165
  22.8 1.2 copy-start
  24.1 23.4 %copy-start.5 = (bf16[1,1,256,1024]{3,2,1,0:T(8,128)(2,1)S(1)}, bf16[1,1,256,1024]{3,2,1,0:T(8,128)(2,1)}, u32[]{:S(2)}) copy-start(bf16[1,1,256,1024]{3,2,1,0:T(8,128)(2,1)} %get-tuple-element.19) | copy-start | bytes 1572868
  24.2 23.4 %copy-start.6 = (bf16[1,1,256,1024]{3,2,1,0:T(8,128)(2,1)S(1)}, bf16[1,1,256,1024]{3,2,1,0:T(8,128)(2,1)}, u32[]{:S(2)}) copy-start(bf16[1,1,256,1024]{3,2,1,0:T(8,128)(2,1)} %get-tuple-element.25) | copy-start | bytes 1572868
  42.2 21.2 %all-to-all-start.1 = ((bf16[128,32,64]{0,2,1:T(8,128)(2,1)}), bf16[128,32,64]{0,2,1:T(8,128)(2,1)S(1)}, u32[]{:S(2)}, u32[]{:S(2)}) async-start(bf16[128,32,64]{0,2,1:T(8,128)(2,1)} %bitcast.12), calls=%async_computation.1 | async-start | bytes 1048576 | tf_op jit(solution)/shard_map/all_to_all | solution.py:169
  66.5 26.8 %all-to-all-start.2 = ((bf16[2,1,256,1024]{2,0,1,3:T(2,128)(2,1)}), bf16[2,1,256,1024]{2,0,1,3:T(2,128)(2,1)}, u32[]{:S(2)}, u32[]{:S(2)}) async-start(bf16[2,1,256,1024]{2,0,1,3:T(2,128)(2,1)} %copy.102), calls=%async_computation.2 | async-start | bytes 2097152 | tf_op jit(solution)/shard_map/all_to_all | solution.py:165
  85.4 9.5 %copy-start.4 = (bf16[2,1,256,1024]{2,3,0,1:T(8,128)(2,1)S(1)}, bf16[2,1,256,1024]{2,3,0,1:T(8,128)(2,1)}, u32[]{:S(2)}) copy-start(bf16[2,1,256,1024]{2,3,0,1:T(8,128)(2,1)} %copy.97) | copy-start | bytes 3145732
  95.2 1.6 %copy-start.2 = (f32[256,64,32]{0,1,2:T(8,128)S(1)}, f32[256,64,32]{0,1,2:T(8,128)}, u32[]{:S(2)}) copy-start(f32[256,64,32]{0,1,2:T(8,128)} %fusion.24) | copy-start | bytes 6291460
  95.2 2.2 %copy-start.3 = (f32[256,64,32]{0,1,2:T(8,128)S(1)}, f32[256,64,32]{0,1,2:T(8,128)}, u32[]{:S(2)}) copy-start(f32[256,64,32]{0,1,2:T(8,128)} %fusion.16) | copy-start | bytes 6291460
  132.3 1.4 %copy-start.1 = (bf16[128,6144]{0,1:T(8,128)(2,1)S(1)}, bf16[128,6144]{0,1:T(8,128)(2,1)}, u32[]{:S(2)}) copy-start(bf16[128,6144]{0,1:T(8,128)(2,1)} %copy-done) | copy-start | bytes 4718596
  132.3 1.4 %copy-start.9 = (f32[2048]{0:T(1024)S(1)}, f32[2048]{0:T(1024)}, u32[]{:S(2)}) copy-start(f32[2048]{0:T(1024)} %param.7) | copy-start | bytes 24580

commit v8 on v5

--- a/solution.py
+++ b/solution.py
@@ -163,10 +163,14 @@
     tokens = lax.all_to_all(outgoing, everyone, split_axis=1, concat_axis=0, tiled=True)
     tokens = tokens.reshape(block_count, block_len, width).astype(jnp.float32).transpose(0, 2, 1)
 
-    tokens, spectrum = lax.optimization_barrier((tokens, jnp.stack([spectrum_real, spectrum_imag])))
-    spectrum = lax.all_to_all(spectrum, "ctx", split_axis=3, concat_axis=1, tiled=True)
-    spectrum = spectrum.transpose(0, 1, 3, 2).astype(jnp.float32)
-    filter_real, filter_imag = spectrum[0], spectrum[1]
+    local_residues, spectrum_len, half = spectrum_real.shape
+    spectrum = jnp.stack([spectrum_real, spectrum_imag])
+    spectrum = spectrum.reshape(2, local_residues, spectrum_len, block_count, width)
+    spectrum = spectrum.transpose(3, 0, 1, 4, 2)
+    tokens, spectrum = lax.optimization_barrier((tokens, spectrum))
+    spectrum = lax.all_to_all(spectrum, "ctx", split_axis=0, concat_axis=0, tiled=True)
+    spectrum = spectrum.transpose(1, 0, 2, 3, 4).reshape(2, residues, width, spectrum_len)
+    filter_real, filter_imag = spectrum[0].astype(jnp.float32), spectrum[1].astype(jnp.float32)
 
     residue = jnp.arange(residues, dtype=jnp.int32)
     block_order = jnp.arange(block_count, dtype=jnp.int32)

time: 131 us -> 134 us (1.023)
  waiting for transfers between devices: 34.6 us -> 38.8 us
  other arithmetic: 9.81 us -> 7.66 us
    all_to_all x1, waiting for transfers between devices: 8.34 us -> 12.6 us  [channel_parallel(): lax.all_to_all(outgoing, everyone, split_axis=1, concat_axis=0, tiled=True)]
    another operation x1 -> x0, other arithmetic: 4.04 us -> none  [channel_parallel(): jnp.stack([spectrum_real, spectrum_imag])]
    unnamed x15 -> x17, local copies, waits for them, and re-layouts: 9.49 us -> 6.88 us
    transpose x2, local copies, waits for them, and re-layouts: 0.91 us -> 3.13 us  [channel_parallel(): tokens.reshape(block_count, block_len, width).astype(jnp.float32)]
    slice x0 -> x1, local copies, waits for them, and re-layouts: none -> 2.13 us  [channel_parallel(): spectrum[1].astype(jnp.float32)]
    all_to_all x1 -> x0, local copies, waits for them, and re-layouts: 2.08 us -> none  [channel_parallel(): lax.all_to_all(spectrum, 'ctx', split_axis=3, concat_axis=1, tiled=True)]
    optimization_barrier x0 -> x1, local copies, waits for them, and re-layouts: none -> 1.49 us  [channel_parallel(): tokens, spectrum = lax.optimization_barrier((tokens, spectrum))]
    transpose x0 -> x1, other arithmetic: none -> 1.42 us  [channel_parallel(): spectrum = spectrum.transpose(3, 0, 1, 4, 2)]
  transfers between devices with their start and end apart: 3 -> 3, of which waited for: 2 -> 2; matrix products, arithmetic and copies ran while one was open for 19% -> 16% of each run, Pallas kernels for 0% -> 0%
where the time goes in v8:
time: 134 us; the launch traced here: 133 us
  waiting for transfers between devices  38.8 us (29%)
  matrix products  26.8 us (20%)
  blocking collectives  26.4 us (20%)
  local copies, waits for them, and re-layouts  18.8 us (14%)
  starting transfers between devices  14.3 us (11%)
  other arithmetic  7.66 us (6%)
    all_to_all x1, blocking collectives, channel_parallel(): lax.all_to_all(long_blocks, everyone, split_axis=0, concat_axis=0, tiled=...  26.4 us
    all_to_all x1, waiting for transfers between devices, channel_parallel(): lax.all_to_all(spectrum, 'ctx', split_axis=0, concat_axis=0, tiled=True)  26.2 us
    dot_general x8, matrix products, times(): lax.dot_general(data.reshape(rows, block_len), table_part, (((1,), (0,)),...  22.6 us
    all_to_all x1, waiting for transfers between devices, channel_parallel(): lax.all_to_all(outgoing, everyone, split_axis=1, concat_axis=0, tiled=True)  12.6 us
    unnamed x17, local copies, waits for them, and re-layouts  6.88 us
    all_to_all x1, starting transfers between devices, channel_parallel(): lax.all_to_all(outgoing, everyone, split_axis=1, concat_axis=0, tiled=True)  5.84 us
    all_to_all x1, starting transfers between devices, channel_parallel(): lax.all_to_all(spectrum, 'ctx', split_axis=0, concat_axis=0, tiled=True)  4.53 us
    convert_element_type x1, other arithmetic, short_convolution(): short = short.astype(jnp.bfloat16)  4.37 us
  transfers between devices with their start and end apart: 3, of which 2 were waited for; matrix products, arithmetic and copies ran while one was open for 16% of the time, Pallas kernels for 0%

profile of v8, /device:TPU:1, one launch (start us, length us, event | category | flops | bytes accessed | tf_op | source)
XLA Modules:
  0.0 133.1 jit_solution(788078369493166475)
XLA Ops:
  0.0 0.9 slice.37
  0.9 3.9 %collective-permute-start = (bf16[2,6144]{1,0:T(2,128)(2,1)S(1)}, bf16[2,6144]{1,0:T(2,128)(2,1)S(1)}, u32[]{:S(2)}, u32[]{:S(2)}) collective-permute-start(bf16[2,6144]{1,0:T(2,128)(2,1)S(1)} %slice.37), channel_id=1, source_target_pairs={{0,1},{1,2},{2,3},{3,4},{4,5},{5,6},{6,7},{7,8},{8,9},{9,10},{10,1... | collective-permute-start | bytes 73736 | tf_op jit(solution)/shard_map/ppermute | solution.py:14
  4.9 1.1 fusion.154
  6.0 1.9 %copy.55 = bf16[128,6144]{0,1:T(8,128)(2,1)S(1)} copy(bf16[128,6144]{1,0:T(8,128)(2,1)} %param.5) | data formatting | bytes 3145728 | tf_op args[0]
  7.9 0.0 collective-permute-done
  7.9 0.9 copy.56
  8.8 4.4 %add_convert_fusion = bf16[128,6144]{0,1:T(8,128)(2,1)S(1)} fusion(bf16[128,6144]{0,1:T(8,128)(2,1)S(1)} %copy.55, bf16[2,6144]{0,1:T(8,128)(2,1)S(1)} %copy.56, f32[6144]{0:T(1024)S(1)} %bitcast.87, f32[6144]{0:T(1024)S(1)} %bitcast.88, f32[6144]{0:T(1024)S(1)} %bitcast.86), kind=kLoop, calls=%fused_computation.2 | loop fusion | flops 11796480 | bytes 3244032 | tf_op jit(solution)/shard_map/convert_element_type | solution.py:134
  13.2 0.0 copy-start
  13.2 1.2 copy-done
  14.4 0.0 copy-start.4
  14.4 0.1 fusion.54
  14.5 0.0 copy-start.5
  14.5 0.8 copy.58
  15.4 5.8 %all-to-all-start = ((bf16[128,32,64]{0,2,1:T(8,128)(2,1)}), bf16[128,32,64]{0,2,1:T(8,128)(2,1)}, u32[]{:S(2)}, u32[]{:S(2)}) async-start(bf16[128,32,64]{0,2,1:T(8,128)(2,1)} %bitcast.6), calls=%async_computation | async-start | bytes 1048576 | tf_op jit(solution)/shard_map/all_to_all | solution.py:163
  21.2 0.0 copy-done.4
  21.2 0.5 copy.60
  21.8 0.0 copy-done.5
  21.8 1.3 copy.61
  23.1 1.4 %maximum_bitcast_fusion = bf16[16,2,2,64,256]{4,3,0,2,1:T(8,128)(2,1)S(1)} fusion(bf16[1,2,256,16,64]{2,4,3,1,0:T(8,128)(2,1)} %bitcast.81, bf16[1,2,256,16,64]{2,4,3,1,0:T(8,128)(2,1)S(1)} %bitcast.80), kind=kLoop, calls=%fused_computation.9 | loop fusion | flops 1048576 | bytes 4194304 | tf_op jit(solution)/shard_map/transpose | solution.py:169
  24.5 12.6 %all-to-all-done = bf16[128,32,64]{0,2,1:T(8,128)(2,1)} async-done(((bf16[128,32,64]{0,2,1:T(8,128)(2,1)}), bf16[128,32,64]{0,2,1:T(8,128)(2,1)}, u32[]{:S(2)}, u32[]{:S(2)}) %all-to-all-start) | async-done | bytes 524320 | tf_op jit(solution)/shard_map/all_to_all | solution.py:163
  37.1 1.1 convert_bitcast_fusion.1
  38.3 1.6 %copy.59 = f32[32,128,1,64]{1,0,3,2:T(8,128)} copy(f32[32,128,1,64]{1,3,0,2:T(8,128)S(1)} %convert_bitcast_fusion.1) | data formatting | bytes 2097152 | tf_op jit(solution)/shard_map/transpose | solution.py:164
  39.9 1.5 %reshape.114 = f32[16,256,64]{1,0,2:T(8,128)S(1)} reshape(f32[32,128,1,64]{1,0,3,2:T(8,128)} %copy.59) | data formatting | bytes 2097152 | tf_op jit(solution)/shard_map/transpose | solution.py:164
  41.4 1.5 %copy.64 = bf16[16,2,2,64,256]{4,3,2,1,0:T(8,128)(2,1)} copy(bf16[16,2,2,64,256]{4,3,0,2,1:T(8,128)(2,1)S(1)} %maximum_bitcast_fusion) | data formatting | bytes 4194304 | tf_op jit(solution)/shard_map/optimization_barrier | solution.py:170
  42.9 4.5 %all-to-all-start.1 = ((bf16[16,2,2,64,256]{4,3,2,1,0:T(8,128)(2,1)}), bf16[16,2,2,64,256]{4,3,2,1,0:T(8,128)(2,1)}, u32[]{:S(2)}, u32[]{:S(2)}) async-start(bf16[16,2,2,64,256]{4,3,2,1,0:T(8,128)(2,1)} %copy.64), calls=%async_computation.1 | async-start | bytes 4194304 | tf_op jit(solution)/shard_map/all_to_all | solution.py:171
  47.4 0.1 fusion.85
  47.6 1.1 fusion.91
  48.7 1.5 %multiply_add_fusion = (f32[32,64,256]{2,0,1:T(8,128)S(1)}, f32[32,64,256]{2,0,1:T(8,128)S(1)}) fusion(f32[32,64,256]{2,0,1:T(8,128)S(1)} %fusion.91, f32[32,256]{1,0:T(8,128)S(1)} %get-tuple-element.18, f32[32,256]{1,0:T(8,128)S(1)} %get-tuple-element.19, f32[16,64,256]{2,0,1:T(8,128)S(1)} %bitcast.79), kind=kOutput, calls=%fused_computation.19 | convolution fusion | flops 54008832 | bytes 7405568 | tf_op jit(solution)/shard_map/ja,jcp->acp/dot_general | solution.py:28
  50.2 4.3 %fusion.18 = f32[32,64,256]{2,1,0:T(8,128)} fusion(f32[32,64,256]{2,0,1:T(8,128)S(1)} %get-tuple-element.12), kind=kOutput, calls=%fused_computation.28 | convolution fusion | flops 806223872 | bytes 4194304 | tf_op jit(solution)/shard_map/dot_general | solution.py:191
  54.5 3.0 %fusion.20 = f32[32,64,256]{2,1,0:T(8,128)S(1)} fusion(f32[32,64,256]{2,0,1:T(8,128)S(1)} %get-tuple-element.12), kind=kOutput, calls=%fused_computation.30 | convolution fusion | flops 806223872 | bytes 4194304 | tf_op jit(solution)/shard_map/dot_general | solution.py:191
  57.5 4.4 %fusion.26 = f32[32,64,256]{2,1,0:T(8,128)} fusion(f32[32,64,256]{2,1,0:T(8,128)S(1)} %fusion.20, f32[32,64,256]{2,0,1:T(8,128)S(1)} %get-tuple-element.11), kind=kOutput, calls=%fused_computation.36 | convolution fusion | flops 806748160 | bytes 6291456 | tf_op jit(solution)/shard_map/dot_general | solution.py:191
  61.9 26.2 %all-to-all-done.1 = bf16[16,2,2,64,256]{4,3,2,1,0:T(8,128)(2,1)} async-done(((bf16[16,2,2,64,256]{4,3,2,1,0:T(8,128)(2,1)}), bf16[16,2,2,64,256]{4,3,2,1,0:T(8,128)(2,1)}, u32[]{:S(2)}, u32[]{:S(2)}) %all-to-all-start.1) | async-done | bytes 2097184 | tf_op jit(solution)/shard_map/all_to_all | solution.py:171
  88.1 0.0 copy-start.2
  88.1 0.0 copy-start.3
  88.1 2.1 %fusion.153 = (bf16[1,16,2,64,256]{4,3,2,0,1:T(8,128)(2,1)S(1)}, bf16[1,16,2,64,256]{4,3,2,0,1:T(8,128)(2,1)S(1)}) fusion(bf16[2,16,2,64,256]{4,3,2,0,1:T(8,128)(2,1)} %bitcast.16), kind=kLoop, calls=%fused_computation.151 | loop fusion | bytes 4194304 | tf_op jit(solution)/shard_map/slice | solution.py:173
  90.3 0.1 copy-done.2
  90.4 0.6 copy-done.3
  91.0 3.7 %fusion = (bf16[32,64,256]{2,1,0:T(8,128)(2,1)S(1)}, bf16[32,64,256]{2,1,0:T(8,128)(2,1)S(1)}) fusion(f32[32,64,256]{2,1,0:T(8,128)S(1)} %copy-done.2, bf16[1,16,2,64,256]{4,3,2,0,1:T(8,128)(2,1)S(1)} %get-tuple-element.14, bf16[1,16,2,64,256]{4,3,2,0,1:T(8,128)(2,1)S(1)} %get-tuple-element.13, f32[32,64,256]{2,1,0:T(8,128)S(1)} %copy-done.3, ...), kind=kOutput, calls=%fused_computation.7 | convolution fusion | flops 811991040 | bytes 10485760 | tf_op jit(solution)/shard_map/dot_general | solution.py:191
  94.7 1.7 %fusion.10 = f32[32,64,256]{2,0,1:T(8,128)S(1)} fusion(bf16[32,64,256]{2,1,0:T(8,128)(2,1)S(1)} %get-tuple-element.10), kind=kOutput, calls=%fused_computation.20 | convolution fusion | flops 269352960 | bytes 3145728 | tf_op jit(solution)/shard_map/dot_general | solution.py:191
  96.4 1.8 %fusion.12 = f32[32,64,256]{2,0,1:T(8,128)S(1)} fusion(bf16[32,64,256]{2,1,0:T(8,128)(2,1)S(1)} %get-tuple-element.10), kind=kOutput, calls=%fused_computation.22 | convolution fusion | flops 269352960 | bytes 3145728 | tf_op jit(solution)/shard_map/dot_general | solution.py:191
  98.2 1.9 %fusion.35 = f32[32,64,256]{2,0,1:T(8,128)S(1)} fusion(f32[32,64,256]{2,0,1:T(8,128)S(1)} %fusion.10, bf16[32,64,256]{2,1,0:T(8,128)(2,1)S(1)} %get-tuple-element.9), kind=kOutput, calls=%fused_computation.39 | convolution fusion | flops 269877248 | bytes 5242880 | tf_op jit(solution)/shard_map/dot_general | solution.py:191
  100.0 1.8 %fusion.32 = f32[32,64,256]{2,0,1:T(8,128)S(1)} fusion(f32[32,64,256]{2,0,1:T(8,128)S(1)} %fusion.12, bf16[32,64,256]{2,1,0:T(8,128)(2,1)S(1)} %get-tuple-element.9), kind=kOutput, calls=%fused_computation.38 | convolution fusion | flops 269877248 | bytes 5242880 | tf_op jit(solution)/shard_map/dot_general | solution.py:191
  101.9 0.8 fusion.2
  102.7 0.9 fusion.45
  103.6 0.1 convert_element_type.143
  103.7 0.2 copy.71
  103.9 26.4 %all_to_all.19 = bf16[32,128,64]{1,2,0:T(8,128)(2,1)S(1)} all-to-all(bf16[32,128,64]{1,2,0:T(8,128)(2,1)S(1)} %bitcast.85), channel_id=1, replica_groups=mesh['ctx'=16,'grp'=2] {'ctx','grp'}, dimensions={0} | all-to-all | bytes 1048576 | tf_op jit(solution)/shard_map/all_to_all | solution.py:217
  130.4 0.0 copy-start.1
  130.4 0.0 copy-start.6
  130.4 0.1 convert_bitcast_fusion
  130.5 0.1 copy.72
  130.6 1.2 copy-done.1
  131.8 0.0 copy-done.6
  131.8 0.3 fusion.49
  132.1 1.0 copy.73
Async XLA Ops:
  0.9 7.0 %collective-permute-start = (bf16[2,6144]{1,0:T(2,128)(2,1)S(1)}, bf16[2,6144]{1,0:T(2,128)(2,1)S(1)}, u32[]{:S(2)}, u32[]{:S(2)}) collective-permute-start(bf16[2,6144]{1,0:T(2,128)(2,1)S(1)} %slice.37), channel_id=1, source_target_pairs={{0,1},{1,2},{2,3},{3,4},{4,5},{5,6},{6,7},{7,8},{8,9},{9,10},{10,1... | collective-permute-start | bytes 73736 | tf_op jit(solution)/shard_map/ppermute | solution.py:14
  13.2 1.2 copy-start
  14.4 6.8 %copy-start.4 = (bf16[2,256,1024]{2,1,0:T(8,128)(2,1)S(1)}, bf16[2,256,1024]{2,1,0:T(8,128)(2,1)}, u32[]{:S(2)}) copy-start(bf16[2,256,1024]{2,1,0:T(8,128)(2,1)} %param.8) | copy-start | bytes 3145732
  14.5 7.2 %copy-start.5 = (bf16[2,256,1024]{2,1,0:T(8,128)(2,1)S(1)}, bf16[2,256,1024]{2,1,0:T(8,128)(2,1)}, u32[]{:S(2)}) copy-start(bf16[2,256,1024]{2,1,0:T(8,128)(2,1)} %param.9) | copy-start | bytes 3145732
  15.4 21.7 %all-to-all-start = ((bf16[128,32,64]{0,2,1:T(8,128)(2,1)}), bf16[128,32,64]{0,2,1:T(8,128)(2,1)}, u32[]{:S(2)}, u32[]{:S(2)}) async-start(bf16[128,32,64]{0,2,1:T(8,128)(2,1)} %bitcast.6), calls=%async_computation | async-start | bytes 1048576 | tf_op jit(solution)/shard_map/all_to_all | solution.py:163
  42.9 45.2 %all-to-all-start.1 = ((bf16[16,2,2,64,256]{4,3,2,1,0:T(8,128)(2,1)}), bf16[16,2,2,64,256]{4,3,2,1,0:T(8,128)(2,1)}, u32[]{:S(2)}, u32[]{:S(2)}) async-start(bf16[16,2,2,64,256]{4,3,2,1,0:T(8,128)(2,1)} %copy.64), calls=%async_computation.1 | async-start | bytes 4194304 | tf_op jit(solution)/shard_map/all_to_all | solution.py:171
  88.1 2.2 %copy-start.2 = (f32[32,64,256]{2,1,0:T(8,128)S(1)}, f32[32,64,256]{2,1,0:T(8,128)}, u32[]{:S(2)}) copy-start(f32[32,64,256]{2,1,0:T(8,128)} %fusion.26) | copy-start | bytes 6291460
  88.1 2.9 %copy-start.3 = (f32[32,64,256]{2,1,0:T(8,128)S(1)}, f32[32,64,256]{2,1,0:T(8,128)}, u32[]{:S(2)}) copy-start(f32[32,64,256]{2,1,0:T(8,128)} %fusion.18) | copy-start | bytes 6291460
  130.4 1.4 %copy-start.1 = (bf16[128,6144]{0,1:T(8,128)(2,1)S(1)}, bf16[128,6144]{0,1:T(8,128)(2,1)}, u32[]{:S(2)}) copy-start(bf16[128,6144]{0,1:T(8,128)(2,1)} %copy-done) | copy-start | bytes 4718596
  130.4 1.4 %copy-start.6 = (f32[2048]{0:T(1024)S(1)}, f32[2048]{0:T(1024)}, u32[]{:S(2)}) copy-start(f32[2048]{0:T(1024)} %param.7) | copy-start | bytes 24580

commit v9 on v8

--- a/solution.py
+++ b/solution.py
@@ -161,7 +161,6 @@
     outgoing = outgoing.reshape(row_count, devices, width)
     outgoing = outgoing.astype(jnp.bfloat16)
     tokens = lax.all_to_all(outgoing, everyone, split_axis=1, concat_axis=0, tiled=True)
-    tokens = tokens.reshape(block_count, block_len, width).astype(jnp.float32).transpose(0, 2, 1)
 
     local_residues, spectrum_len, half = spectrum_real.shape
     spectrum = jnp.stack([spectrum_real, spectrum_imag])
@@ -171,6 +170,7 @@
     spectrum = lax.all_to_all(spectrum, "ctx", split_axis=0, concat_axis=0, tiled=True)
     spectrum = spectrum.transpose(1, 0, 2, 3, 4).reshape(2, residues, width, spectrum_len)
     filter_real, filter_imag = spectrum[0].astype(jnp.float32), spectrum[1].astype(jnp.float32)
+    tokens = tokens.reshape(block_count, block_len, width).astype(jnp.float32).transpose(0, 2, 1)
 
     residue = jnp.arange(residues, dtype=jnp.int32)
     block_order = jnp.arange(block_count, dtype=jnp.int32)

time: 134 us -> 131 us (0.978)
  local copies, waits for them, and re-layouts: 18.8 us -> 16.9 us
    transpose x2 -> x0, local copies, waits for them, and re-layouts: 3.13 us -> none  [channel_parallel(): tokens.reshape(block_count, block_len, width).astype(jnp.float32)]
    unnamed x17 -> x18, local copies, waits for them, and re-layouts: 6.88 us -> 7.19 us
where the time goes in v9:
time: 131 us; the launch traced here: 130 us
  waiting for transfers between devices  39.3 us (30%)
  matrix products  26.5 us (20%)
  blocking collectives  26.4 us (20%)
  local copies, waits for them, and re-layouts  16.9 us (13%)
  starting transfers between devices  14.3 us (11%)
  other arithmetic  6.52 us (5%)
    all_to_all x1, waiting for transfers between devices, channel_parallel(): lax.all_to_all(spectrum, 'ctx', split_axis=0, concat_axis=0, tiled=True)  26.7 us
    all_to_all x1, blocking collectives, channel_parallel(): lax.all_to_all(long_blocks, everyone, split_axis=0, concat_axis=0, tiled=...  26.4 us
    dot_general x8, matrix products, times(): lax.dot_general(data.reshape(rows, block_len), table_part, (((1,), (0,)),...  22.8 us
    all_to_all x1, waiting for transfers between devices, channel_parallel(): lax.all_to_all(outgoing, everyone, split_axis=1, concat_axis=0, tiled=True)  12.6 us
    unnamed x18, local copies, waits for them, and re-layouts  7.19 us
    all_to_all x1, starting transfers between devices, channel_parallel(): lax.all_to_all(outgoing, everyone, split_axis=1, concat_axis=0, tiled=True)  5.84 us
    all_to_all x1, starting transfers between devices, channel_parallel(): lax.all_to_all(spectrum, 'ctx', split_axis=0, concat_axis=0, tiled=True)  4.53 us
    convert_element_type x1, other arithmetic, short_convolution(): short = short.astype(jnp.bfloat16)  4.37 us
  transfers between devices with their start and end apart: 3, of which 2 were waited for; matrix products, arithmetic and copies ran while one was open for 16% of the time, Pallas kernels for 0%

profile of v9, /device:TPU:1, one launch (start us, length us, event | category | flops | bytes accessed | tf_op | source)
XLA Modules:
  0.0 130.2 jit_solution(16042061083132045928)
XLA Ops:
  0.0 0.9 slice.37
  0.9 3.9 %collective-permute-start = (bf16[2,6144]{1,0:T(2,128)(2,1)S(1)}, bf16[2,6144]{1,0:T(2,128)(2,1)S(1)}, u32[]{:S(2)}, u32[]{:S(2)}) collective-permute-start(bf16[2,6144]{1,0:T(2,128)(2,1)S(1)} %slice.37), channel_id=1, source_target_pairs={{0,1},{1,2},{2,3},{3,4},{4,5},{5,6},{6,7},{7,8},{8,9},{9,10},{10,1... | collective-permute-start | bytes 73736 | tf_op jit(solution)/shard_map/ppermute | solution.py:14
  4.9 1.1 fusion.156
  6.0 1.9 %copy.55 = bf16[128,6144]{0,1:T(8,128)(2,1)S(1)} copy(bf16[128,6144]{1,0:T(8,128)(2,1)} %param.5) | data formatting | bytes 3145728 | tf_op args[0]
  7.9 0.0 collective-permute-done
  7.9 0.9 copy.56
  8.8 4.4 %add_convert_fusion = bf16[128,6144]{0,1:T(8,128)(2,1)S(1)} fusion(bf16[128,6144]{0,1:T(8,128)(2,1)S(1)} %copy.55, bf16[2,6144]{0,1:T(8,128)(2,1)S(1)} %copy.56, f32[6144]{0:T(1024)S(1)} %bitcast.96, f32[6144]{0:T(1024)S(1)} %bitcast.97, f32[6144]{0:T(1024)S(1)} %bitcast.95), kind=kLoop, calls=%fused_computation.2 | loop fusion | flops 11796480 | bytes 3244032 | tf_op jit(solution)/shard_map/convert_element_type | solution.py:134
  13.2 0.0 copy-start
  13.2 1.2 copy-done
  14.4 0.0 copy-start.4
  14.4 0.1 fusion.54
  14.5 0.0 copy-start.5
  14.5 0.8 copy.58
  15.4 5.8 %all-to-all-start = ((bf16[128,32,64]{0,2,1:T(8,128)(2,1)}), bf16[128,32,64]{0,2,1:T(8,128)(2,1)}, u32[]{:S(2)}, u32[]{:S(2)}) async-start(bf16[128,32,64]{0,2,1:T(8,128)(2,1)} %bitcast.6), calls=%async_computation | async-start | bytes 1048576 | tf_op jit(solution)/shard_map/all_to_all | solution.py:163
  21.2 0.0 copy-done.4
  21.2 0.5 copy.60
  21.8 0.0 copy-done.5
  21.8 1.3 %copy.61 = bf16[2,256,1024]{1,2,0:T(8,128)(2,1)} copy(bf16[2,256,1024]{2,1,0:T(8,128)(2,1)S(1)} %copy-done.5) | data formatting | bytes 2097152 | tf_op args[4]
  23.1 1.4 %maximum_bitcast_fusion = bf16[16,2,2,64,256]{4,3,0,2,1:T(8,128)(2,1)S(1)} fusion(bf16[1,2,256,16,64]{2,4,3,1,0:T(8,128)(2,1)} %bitcast.89, bf16[1,2,256,16,64]{2,4,3,1,0:T(8,128)(2,1)S(1)} %bitcast.88), kind=kLoop, calls=%fused_computation.9 | loop fusion | flops 1048576 | bytes 4194304 | tf_op jit(solution)/shard_map/transpose | solution.py:168
  24.5 12.6 %all-to-all-done = bf16[128,32,64]{0,2,1:T(8,128)(2,1)} async-done(((bf16[128,32,64]{0,2,1:T(8,128)(2,1)}), bf16[128,32,64]{0,2,1:T(8,128)(2,1)}, u32[]{:S(2)}, u32[]{:S(2)}) %all-to-all-start) | async-done | bytes 524320 | tf_op jit(solution)/shard_map/all_to_all | solution.py:163
  37.1 1.1 copy_bitcast_fusion
  38.2 1.5 %copy.64 = bf16[16,2,2,64,256]{4,3,2,1,0:T(8,128)(2,1)} copy(bf16[16,2,2,64,256]{4,3,0,2,1:T(8,128)(2,1)S(1)} %maximum_bitcast_fusion) | data formatting | bytes 4194304 | tf_op jit(solution)/shard_map/optimization_barrier | solution.py:169
  39.7 4.5 %all-to-all-start.1 = ((bf16[16,2,2,64,256]{4,3,2,1,0:T(8,128)(2,1)}), bf16[16,2,2,64,256]{4,3,2,1,0:T(8,128)(2,1)}, u32[]{:S(2)}, u32[]{:S(2)}) async-start(bf16[16,2,2,64,256]{4,3,2,1,0:T(8,128)(2,1)} %copy.64), calls=%async_computation.1 | async-start | bytes 4194304 | tf_op jit(solution)/shard_map/all_to_all | solution.py:170
  44.3 0.1 fusion.89
  44.4 0.1 copy.81
  44.5 0.8 fusion.55
  45.3 1.3 multiply_add_fusion
  46.6 4.3 %fusion.18 = f32[32,64,256]{2,1,0:T(8,128)} fusion(f32[32,64,256]{2,0,1:T(8,128)S(1)} %get-tuple-element.12), kind=kOutput, calls=%fused_computation.28 | convolution fusion | flops 806223872 | bytes 4194304 | tf_op jit(solution)/shard_map/dot_general | solution.py:191
  50.9 3.0 %fusion.20 = f32[32,64,256]{2,1,0:T(8,128)S(1)} fusion(f32[32,64,256]{2,0,1:T(8,128)S(1)} %get-tuple-element.12), kind=kOutput, calls=%fused_computation.30 | convolution fusion | flops 806223872 | bytes 4194304 | tf_op jit(solution)/shard_map/dot_general | solution.py:191
  53.9 4.4 %fusion.26 = f32[32,64,256]{2,1,0:T(8,128)} fusion(f32[32,64,256]{2,1,0:T(8,128)S(1)} %fusion.20, f32[32,64,256]{2,0,1:T(8,128)S(1)} %get-tuple-element.11), kind=kOutput, calls=%fused_computation.36 | convolution fusion | flops 806748160 | bytes 6291456 | tf_op jit(solution)/shard_map/dot_general | solution.py:191
  58.3 26.7 %all-to-all-done.1 = bf16[16,2,2,64,256]{4,3,2,1,0:T(8,128)(2,1)} async-done(((bf16[16,2,2,64,256]{4,3,2,1,0:T(8,128)(2,1)}), bf16[16,2,2,64,256]{4,3,2,1,0:T(8,128)(2,1)}, u32[]{:S(2)}, u32[]{:S(2)}) %all-to-all-start.1) | async-done | bytes 2097184 | tf_op jit(solution)/shard_map/all_to_all | solution.py:170
  85.0 0.0 copy-start.2
  85.0 0.0 copy-start.3
  85.0 1.9 %fusion.155 = (bf16[1,16,2,64,256]{4,3,2,0,1:T(8,128)(2,1)S(1)}, bf16[1,16,2,64,256]{4,3,2,0,1:T(8,128)(2,1)S(1)}) fusion(bf16[2,16,2,64,256]{4,3,2,0,1:T(8,128)(2,1)} %bitcast.16), kind=kLoop, calls=%fused_computation.153 | loop fusion | bytes 4194304 | tf_op jit(solution)/shard_map/slice | solution.py:172
  86.9 0.3 copy-done.2
  87.2 0.6 copy-done.3
  87.8 3.9 %fusion = (bf16[32,64,256]{2,1,0:T(8,128)(2,1)S(1)}, bf16[32,64,256]{2,1,0:T(8,128)(2,1)S(1)}) fusion(f32[32,64,256]{2,1,0:T(8,128)S(1)} %copy-done.2, bf16[1,16,2,64,256]{4,3,2,0,1:T(8,128)(2,1)S(1)} %get-tuple-element.14, bf16[1,16,2,64,256]{4,3,2,0,1:T(8,128)(2,1)S(1)} %get-tuple-element.13, f32[32,64,256]{2,1,0:T(8,128)S(1)} %copy-done.3, ...), kind=kOutput, calls=%fused_computation.7 | convolution fusion | flops 811991040 | bytes 10485760 | tf_op jit(solution)/shard_map/dot_general | solution.py:191
  91.7 1.7 %fusion.10 = f32[32,64,256]{2,0,1:T(8,128)S(1)} fusion(bf16[32,64,256]{2,1,0:T(8,128)(2,1)S(1)} %get-tuple-element.10), kind=kOutput, calls=%fused_computation.20 | convolution fusion | flops 269352960 | bytes 3145728 | tf_op jit(solution)/shard_map/dot_general | solution.py:191
  93.4 1.8 %fusion.12 = f32[32,64,256]{2,0,1:T(8,128)S(1)} fusion(bf16[32,64,256]{2,1,0:T(8,128)(2,1)S(1)} %get-tuple-element.10), kind=kOutput, calls=%fused_computation.22 | convolution fusion | flops 269352960 | bytes 3145728 | tf_op jit(solution)/shard_map/dot_general | solution.py:191
  95.2 1.9 %fusion.35 = f32[32,64,256]{2,0,1:T(8,128)S(1)} fusion(f32[32,64,256]{2,0,1:T(8,128)S(1)} %fusion.10, bf16[32,64,256]{2,1,0:T(8,128)(2,1)S(1)} %get-tuple-element.9), kind=kOutput, calls=%fused_computation.39 | convolution fusion | flops 269877248 | bytes 5242880 | tf_op jit(solution)/shard_map/dot_general | solution.py:191
  97.1 1.8 %fusion.32 = f32[32,64,256]{2,0,1:T(8,128)S(1)} fusion(f32[32,64,256]{2,0,1:T(8,128)S(1)} %fusion.12, bf16[32,64,256]{2,1,0:T(8,128)(2,1)S(1)} %get-tuple-element.9), kind=kOutput, calls=%fused_computation.38 | convolution fusion | flops 269877248 | bytes 5242880 | tf_op jit(solution)/shard_map/dot_general | solution.py:191
  98.9 0.8 fusion.2
  99.8 0.9 fusion.45
  100.6 0.1 convert_element_type.131
  100.8 0.2 copy.71
  101.0 26.4 %all_to_all.28 = bf16[32,128,64]{1,2,0:T(8,128)(2,1)S(1)} all-to-all(bf16[32,128,64]{1,2,0:T(8,128)(2,1)S(1)} %bitcast.94), channel_id=1, replica_groups=mesh['ctx'=16,'grp'=2] {'ctx','grp'}, dimensions={0} | all-to-all | bytes 1048576 | tf_op jit(solution)/shard_map/all_to_all | solution.py:217
  127.4 0.0 copy-start.1
  127.4 0.0 copy-start.6
  127.4 0.1 convert_bitcast_fusion
  127.5 0.1 copy.72
  127.6 1.2 copy-done.1
  128.8 0.0 copy-done.6
  128.8 0.3 fusion.49
  129.1 1.0 copy.73
Async XLA Ops:
  0.9 7.0 %collective-permute-start = (bf16[2,6144]{1,0:T(2,128)(2,1)S(1)}, bf16[2,6144]{1,0:T(2,128)(2,1)S(1)}, u32[]{:S(2)}, u32[]{:S(2)}) collective-permute-start(bf16[2,6144]{1,0:T(2,128)(2,1)S(1)} %slice.37), channel_id=1, source_target_pairs={{0,1},{1,2},{2,3},{3,4},{4,5},{5,6},{6,7},{7,8},{8,9},{9,10},{10,1... | collective-permute-start | bytes 73736 | tf_op jit(solution)/shard_map/ppermute | solution.py:14
  13.2 1.2 copy-start
  14.4 6.8 %copy-start.4 = (bf16[2,256,1024]{2,1,0:T(8,128)(2,1)S(1)}, bf16[2,256,1024]{2,1,0:T(8,128)(2,1)}, u32[]{:S(2)}) copy-start(bf16[2,256,1024]{2,1,0:T(8,128)(2,1)} %param.8) | copy-start | bytes 3145732
  14.5 7.2 %copy-start.5 = (bf16[2,256,1024]{2,1,0:T(8,128)(2,1)S(1)}, bf16[2,256,1024]{2,1,0:T(8,128)(2,1)}, u32[]{:S(2)}) copy-start(bf16[2,256,1024]{2,1,0:T(8,128)(2,1)} %param.9) | copy-start | bytes 3145732
  15.4 21.7 %all-to-all-start = ((bf16[128,32,64]{0,2,1:T(8,128)(2,1)}), bf16[128,32,64]{0,2,1:T(8,128)(2,1)}, u32[]{:S(2)}, u32[]{:S(2)}) async-start(bf16[128,32,64]{0,2,1:T(8,128)(2,1)} %bitcast.6), calls=%async_computation | async-start | bytes 1048576 | tf_op jit(solution)/shard_map/all_to_all | solution.py:163
  39.7 45.2 %all-to-all-start.1 = ((bf16[16,2,2,64,256]{4,3,2,1,0:T(8,128)(2,1)}), bf16[16,2,2,64,256]{4,3,2,1,0:T(8,128)(2,1)}, u32[]{:S(2)}, u32[]{:S(2)}) async-start(bf16[16,2,2,64,256]{4,3,2,1,0:T(8,128)(2,1)} %copy.64), calls=%async_computation.1 | async-start | bytes 4194304 | tf_op jit(solution)/shard_map/all_to_all | solution.py:170
  85.0 2.2 %copy-start.2 = (f32[32,64,256]{2,1,0:T(8,128)S(1)}, f32[32,64,256]{2,1,0:T(8,128)}, u32[]{:S(2)}) copy-start(f32[32,64,256]{2,1,0:T(8,128)} %fusion.26) | copy-start | bytes 6291460
  85.0 2.9 %copy-start.3 = (f32[32,64,256]{2,1,0:T(8,128)S(1)}, f32[32,64,256]{2,1,0:T(8,128)}, u32[]{:S(2)}) copy-start(f32[32,64,256]{2,1,0:T(8,128)} %fusion.18) | copy-start | bytes 6291460
  127.4 1.4 %copy-start.1 = (bf16[128,6144]{0,1:T(8,128)(2,1)S(1)}, bf16[128,6144]{0,1:T(8,128)(2,1)}, u32[]{:S(2)}) copy-start(bf16[128,6144]{0,1:T(8,128)(2,1)} %copy-done) | copy-start | bytes 4718596
  127.4 1.4 %copy-start.6 = (f32[2048]{0:T(1024)S(1)}, f32[2048]{0:T(1024)}, u32[]{:S(2)}) copy-start(f32[2048]{0:T(1024)} %param.7) | copy-start | bytes 24580

commit v10 on v1

--- a/solution.py
+++ b/solution.py
@@ -199,8 +199,19 @@
     spectra_imag = times(within_cos, twisted_imag) - times(within_sin, twisted_real)
     product_real = spectra_real * filter_real - spectra_imag * filter_imag
     product_imag = spectra_real * filter_imag + spectra_imag * filter_real
-    restored_real = inverse(within_cos, product_real) - inverse(within_sin, product_imag)
-    restored_imag = inverse(within_cos, product_imag) + inverse(within_sin, product_real)
+    product = jnp.stack([product_real, product_imag]).reshape(2 * block_len, lanes)
+
+    def inverse_part(left, right):
+        return lax.dot_general(
+            jnp.concatenate([left, right], axis=1),
+            product,
+            (((1,), (0,)), ((), ())),
+            precision=lax.Precision.DEFAULT,
+            preferred_element_type=jnp.float32,
+        ).reshape(block_len, width, residues)
+
+    restored_real = inverse_part(within_cos, -within_sin)
+    restored_imag = inverse_part(within_sin, within_cos)
     unturned_real = restored_real * turn_cos - restored_imag * turn_sin
     unturned_imag = restored_real * turn_sin + restored_imag * turn_cos
     long_blocks = contract_high("ja,pca->jpc", across_cos, unturned_real) - contract_high(

time: 131 us -> 128 us (0.977)
  matrix products: 26.8 us -> 21.2 us
  local copies, waits for them, and re-layouts: 18.2 us -> 20.9 us
  other arithmetic: 9.81 us -> 12.3 us
  waiting for transfers between devices: 34.6 us -> 32.4 us
    dot_general x8 -> x4, matrix products: 22.6 us -> 15.4 us  [times(): lax.dot_general(table_part, data.reshape(block_len, lanes), (((1,), (0,))...]
    all_to_all x1, waiting for transfers between devices: 26.2 us -> 24 us  [channel_parallel(): lax.all_to_all(spectrum, 'ctx', split_axis=3, concat_axis=1, tiled=True)]
    another operation x0 -> x1, local copies, waits for them, and re-layouts: none -> 2.16 us  [channel_parallel(): jnp.stack([product_real, product_imag]).reshape(2 * block_len, lanes)]
    dot_general x0 -> x2, matrix products: none -> 1.47 us  [inverse_part(): lax.dot_general(jnp.concatenate([left, right], axis=1), product, (((1,),...]
    unnamed x15 -> x24, local copies, waits for them, and re-layouts: 9.49 us -> 10.1 us
  transfers between devices with their start and end apart: 3 -> 3, of which waited for: 2 -> 2; matrix products, arithmetic and copies ran while one was open for 19% -> 21% of each run, Pallas kernels for 0% -> 0%
where the time goes in v10:
time: 128 us
  waiting for transfers between devices  32.4 us (25%)
  blocking collectives  26.4 us (21%)
  matrix products  21.2 us (17%)
  local copies, waits for them, and re-layouts  20.9 us (16%)
  starting transfers between devices  14.1 us (11%)
  other arithmetic  12.3 us (10%)
    all_to_all x1, blocking collectives, channel_parallel(): lax.all_to_all(long_blocks, everyone, split_axis=0, concat_axis=0, tiled=...  26.4 us
    all_to_all x1, waiting for transfers between devices, channel_parallel(): lax.all_to_all(spectrum, 'ctx', split_axis=3, concat_axis=1, tiled=True)  24 us
    dot_general x4, matrix products, times(): lax.dot_general(table_part, data.reshape(block_len, lanes), (((1,), (0,))...  15.4 us
    unnamed x24, local copies, waits for them, and re-layouts  10.1 us
    all_to_all x1, waiting for transfers between devices, channel_parallel(): lax.all_to_all(outgoing, everyone, split_axis=1, concat_axis=0, tiled=True)  8.36 us
    all_to_all x1, starting transfers between devices, channel_parallel(): lax.all_to_all(outgoing, everyone, split_axis=1, concat_axis=0, tiled=True)  5.79 us
    convert_element_type x1, other arithmetic, short_convolution(): short = short.astype(jnp.bfloat16)  4.37 us
    all_to_all x1, starting transfers between devices, channel_parallel(): lax.all_to_all(spectrum, 'ctx', split_axis=3, concat_axis=1, tiled=True)  4.34 us
  transfers between devices with their start and end apart: 3, of which 2 were waited for; matrix products, arithmetic and copies ran while one was open for 21% of the time, Pallas kernels for 0%

profile of v10, /device:TPU:1, one launch (start us, length us, event | category | flops | bytes accessed | tf_op | source)
XLA Modules:
  0.0 127.6 jit_solution(17140887543482979727)
XLA Ops:
  0.0 0.9 slice.35
  0.9 3.9 %collective-permute-start = (bf16[2,6144]{1,0:T(2,128)(2,1)S(1)}, bf16[2,6144]{1,0:T(2,128)(2,1)S(1)}, u32[]{:S(2)}, u32[]{:S(2)}) collective-permute-start(bf16[2,6144]{1,0:T(2,128)(2,1)S(1)} %slice.35), channel_id=1, source_target_pairs={{0,1},{1,2},{2,3},{3,4},{4,5},{5,6},{6,7},{7,8},{8,9},{9,10},{10,1... | collective-permute-start | bytes 73736 | tf_op jit(solution)/shard_map/ppermute | solution.py:14
  4.9 1.1 fusion.122
  6.0 1.9 %copy.53 = bf16[128,6144]{0,1:T(8,128)(2,1)S(1)} copy(bf16[128,6144]{1,0:T(8,128)(2,1)} %param.5) | data formatting | bytes 3145728 | tf_op args[0]
  7.9 0.0 collective-permute-done
  7.9 0.9 copy.54
  8.8 4.4 %add_convert_fusion = bf16[128,6144]{0,1:T(8,128)(2,1)S(1)} fusion(bf16[128,6144]{0,1:T(8,128)(2,1)S(1)} %copy.53, bf16[2,6144]{0,1:T(8,128)(2,1)S(1)} %copy.54, f32[6144]{0:T(1024)S(1)} %bitcast.118, f32[6144]{0:T(1024)S(1)} %bitcast.119, f32[6144]{0:T(1024)S(1)} %bitcast.117), kind=kLoop, calls=%fused_computation.4 | loop fusion | flops 11796480 | bytes 3244032 | tf_op jit(solution)/shard_map/convert_element_type | solution.py:134
  13.2 0.0 copy-start
  13.2 1.2 copy-done
  14.4 0.0 copy-start.4
  14.4 0.1 fusion.38
  14.6 0.8 copy.56
  15.4 5.8 %all-to-all-start = ((bf16[128,32,64]{0,2,1:T(8,128)(2,1)}), bf16[128,32,64]{0,2,1:T(8,128)(2,1)S(1)}, u32[]{:S(2)}, u32[]{:S(2)}) async-start(bf16[128,32,64]{0,2,1:T(8,128)(2,1)} %bitcast.8), calls=%async_computation | async-start | bytes 1048576 | tf_op jit(solution)/shard_map/all_to_all | solution.py:163
  21.2 0.0 copy-done.4
  21.2 0.9 copy.58
  22.1 2.5 %copy.59 = bf16[2,256,1024]{1,0,2:T(2,128)(2,1)S(1)} copy(bf16[2,256,1024]{2,1,0:T(8,128)(2,1)} %param.9) | data formatting | bytes 2097152 | tf_op args[4]
  24.7 4.0 %pad_maximum_fusion.1 = bf16[2,2,256,1024]{2,1,0,3:T(2,128)(2,1)} fusion(bf16[1,2,256,1024]{2,1,0,3:T(2,128)(2,1)S(1)} %bitcast.114, bf16[1,2,256,1024]{2,1,0,3:T(2,128)(2,1)S(1)} %bitcast.113), kind=kLoop, calls=%fused_computation.7 | loop fusion | flops 1048576 | bytes 4194304 | tf_op jit(solution)/shard_map/stack | solution.py:166
  28.7 8.4 %all-to-all-done = bf16[128,32,64]{0,2,1:T(8,128)(2,1)S(1)} async-done(((bf16[128,32,64]{0,2,1:T(8,128)(2,1)}), bf16[128,32,64]{0,2,1:T(8,128)(2,1)S(1)}, u32[]{:S(2)}, u32[]{:S(2)}) %all-to-all-start) | async-done | bytes 524320 | tf_op jit(solution)/shard_map/all_to_all | solution.py:163
  37.0 0.1 convert_bitcast_fusion.2
  37.1 0.6 copy.57
  37.8 0.3 reshape.90
  38.1 4.3 %all-to-all-start.1 = ((bf16[2,2,256,1024]{2,1,0,3:T(2,128)(2,1)}), bf16[2,2,256,1024]{2,1,0,3:T(2,128)(2,1)}, u32[]{:S(2)}, u32[]{:S(2)}) async-start(bf16[2,2,256,1024]{2,1,0,3:T(2,128)(2,1)} %pad_maximum_fusion.1), calls=%async_computation.1 | async-start | bytes 4194304 | tf_op jit(solution)/shard_map/all_to_all | solution.py:167
  42.4 0.1 fusion.68
  42.6 0.0 copy-start.5
  42.6 0.0 copy-start.7
  42.6 1.0 fusion.59
  43.6 1.3 %fusion.55 = (bf16[256,256]{1,0:T(8,128)(2,1)S(1)}, bf16[256,256]{1,0:T(8,128)(2,1)S(1)}) fusion(), kind=kLoop, calls=%fused_computation.67 | loop fusion | flops 1048576 | bytes 262144 | tf_op jit(solution)/shard_map/sin | solution.py:145
  44.9 1.1 fusion.74
  46.0 1.5 %add_bitcast_fusion.1 = (f32[64,32,256]{2,1,0:T(8,128)S(1)}, f32[64,32,256]{2,1,0:T(8,128)S(1)}) fusion(f32[256,64,32]{0,2,1:T(8,128)S(1)} %fusion.74, f32[256,32]{0,1:T(8,128)S(1)} %get-tuple-element.16, f32[256,32]{0,1:T(8,128)S(1)} %get-tuple-element.17, f32[16,256,64]{1,0,2:T(8,128)S(1)} %reshape.90), kind=kOutput, calls=%fused_computation.19 | convolution fusion | flops 54008832 | bytes 7405568 | tf_op jit(solution)/shard_map/jpc,ja->pca/dot_general | solution.py:28
  47.5 0.0 copy-done.5
  47.5 0.0 copy-done.7
  47.5 4.4 %fusion.8 = f32[256,64,32]{0,1,2:T(8,128)} fusion(f32[64,32,256]{2,1,0:T(8,128)S(1)} %get-tuple-element.12), kind=kOutput, calls=%fused_computation.20 | convolution fusion | flops 806223872 | bytes 4194304 | tf_op jit(solution)/shard_map/dot_general | solution.py:187
  51.8 3.0 %fusion.10 = f32[256,64,32]{0,1,2:T(8,128)S(1)} fusion(f32[64,32,256]{2,1,0:T(8,128)S(1)} %get-tuple-element.12), kind=kOutput, calls=%fused_computation.22 | convolution fusion | flops 806223872 | bytes 4194304 | tf_op jit(solution)/shard_map/dot_general | solution.py:187
  54.9 4.4 %fusion.16 = f32[256,64,32]{0,1,2:T(8,128)} fusion(f32[256,64,32]{0,1,2:T(8,128)S(1)} %fusion.10, f32[64,32,256]{2,1,0:T(8,128)S(1)} %get-tuple-element.11), kind=kOutput, calls=%fused_computation.28 | convolution fusion | flops 806748160 | bytes 6291456 | tf_op jit(solution)/shard_map/dot_general | solution.py:187
  59.3 24.0 %all-to-all-done.1 = bf16[2,2,256,1024]{2,1,0,3:T(2,128)(2,1)} async-done(((bf16[2,2,256,1024]{2,1,0,3:T(2,128)(2,1)}), bf16[2,2,256,1024]{2,1,0,3:T(2,128)(2,1)}, u32[]{:S(2)}, u32[]{:S(2)}) %all-to-all-start.1) | async-done | bytes 2097184 | tf_op jit(solution)/shard_map/all_to_all | solution.py:167
  83.3 2.1 %copy.62 = bf16[2,2,256,1024]{2,3,1,0:T(8,128)(2,1)S(1)} copy(bf16[2,2,256,1024]{2,1,0,3:T(2,128)(2,1)} %all-to-all-done.1) | data formatting | bytes 4194304 | tf_op jit(solution)/shard_map/all_to_all | solution.py:167
  85.4 0.6 convert_bitcast_fusion
  86.0 0.0 copy-start.2
  86.0 0.0 copy-start.3
  86.0 0.5 copy.63
  86.5 1.1 copy-done.2
  87.6 0.6 copy-done.3
  88.2 3.6 %subtract_bitcast_fusion = (bf16[1,256,64,32]{1,2,3,0:T(8,128)(2,1)S(1)}, bf16[1,256,64,32]{1,2,3,0:T(8,128)(2,1)S(1)}) fusion(f32[256,64,32]{0,1,2:T(8,128)S(1)} %copy-done.2, f32[2,256,64,32]{1,2,3,0:T(8,128)S(1)} %bitcast.110, f32[256,64,32]{0,1,2:T(8,128)S(1)} %copy-done.3, f32[64,32,256]{2,1,0:T(8,128)S(1)} %get-tuple-element.11), kind=kOutput, calls=%fused_computation.17 | convolution fusion | flops 810942464 | bytes 12582912 | tf_op jit(solution)/shard_map/dot_general | solution.py:187
  91.8 0.2 pad_maximum_fusion
  92.0 2.2 %copy.66 = bf16[2,256,64,32]{1,0,3,2:T(2,128)(2,1)S(1)} copy(bf16[2,256,64,32]{1,2,3,0:T(8,128)(2,1)S(1)} %pad_maximum_fusion) | data formatting | bytes 4194304 | tf_op jit(solution)/shard_map/stack | solution.py:202
  94.2 0.5 copy.80
  94.7 0.7 fusion.42
  95.5 0.0 copy-start.6
  95.5 0.0 copy-start.8
  95.5 0.7 fusion.39
  96.2 0.0 copy-done.6
  96.3 0.0 copy-done.8
  96.3 0.9 fusion
  97.1 0.9 fusion.29
  98.0 0.2 convert_element_type.144
  98.2 0.2 copy.73
  98.4 26.4 %all_to_all.23 = bf16[32,128,64]{1,2,0:T(8,128)(2,1)S(1)} all-to-all(bf16[32,128,64]{1,2,0:T(8,128)(2,1)S(1)} %copy.73), channel_id=1, replica_groups=mesh['ctx'=16,'grp'=2] {'ctx','grp'}, dimensions={0} | all-to-all | bytes 1048576 | tf_op jit(solution)/shard_map/all_to_all | solution.py:222
  124.8 0.0 copy-start.1
  124.9 0.1 convert_bitcast_fusion.1
  125.0 0.1 copy.74
  125.0 1.2 copy-done.1
  126.3 0.0 copy-done.9
  126.3 0.3 fusion.33
  126.6 1.0 copy.75
  (1 shorter events, 0.0 us)
Async XLA Ops:
  0.9 7.0 %collective-permute-start = (bf16[2,6144]{1,0:T(2,128)(2,1)S(1)}, bf16[2,6144]{1,0:T(2,128)(2,1)S(1)}, u32[]{:S(2)}, u32[]{:S(2)}) collective-permute-start(bf16[2,6144]{1,0:T(2,128)(2,1)S(1)} %slice.35), channel_id=1, source_target_pairs={{0,1},{1,2},{2,3},{3,4},{4,5},{5,6},{6,7},{7,8},{8,9},{9,10},{10,1... | collective-permute-start | bytes 73736 | tf_op jit(solution)/shard_map/ppermute | solution.py:14
  13.2 1.2 copy-start
  14.4 6.8 %copy-start.4 = (bf16[2,256,1024]{2,1,0:T(8,128)(2,1)S(1)}, bf16[2,256,1024]{2,1,0:T(8,128)(2,1)}, u32[]{:S(2)}) copy-start(bf16[2,256,1024]{2,1,0:T(8,128)(2,1)} %param.8) | copy-start | bytes 3145732
  15.4 21.6 %all-to-all-start = ((bf16[128,32,64]{0,2,1:T(8,128)(2,1)}), bf16[128,32,64]{0,2,1:T(8,128)(2,1)S(1)}, u32[]{:S(2)}, u32[]{:S(2)}) async-start(bf16[128,32,64]{0,2,1:T(8,128)(2,1)} %bitcast.8), calls=%async_computation | async-start | bytes 1048576 | tf_op jit(solution)/shard_map/all_to_all | solution.py:163
  38.1 45.2 %all-to-all-start.1 = ((bf16[2,2,256,1024]{2,1,0,3:T(2,128)(2,1)}), bf16[2,2,256,1024]{2,1,0,3:T(2,128)(2,1)}, u32[]{:S(2)}, u32[]{:S(2)}) async-start(bf16[2,2,256,1024]{2,1,0,3:T(2,128)(2,1)} %pad_maximum_fusion.1), calls=%async_computation.1 | async-start | bytes 4194304 | tf_op jit(solution)/shard_map/all_to_all | solution.py:167
  42.6 4.9 %copy-start.5 = (f32[256,32]{0,1:T(8,128)}, f32[256,32]{0,1:T(8,128)S(1)}, u32[]{:S(2)}) copy-start(f32[256,32]{0,1:T(8,128)S(1)} %get-tuple-element.16) | copy-start | bytes 98308
  42.6 4.9 %copy-start.7 = (f32[256,32]{0,1:T(8,128)}, f32[256,32]{0,1:T(8,128)S(1)}, u32[]{:S(2)}) copy-start(f32[256,32]{0,1:T(8,128)S(1)} %get-tuple-element.17) | copy-start | bytes 98308
  86.0 1.6 %copy-start.2 = (f32[256,64,32]{0,1,2:T(8,128)S(1)}, f32[256,64,32]{0,1,2:T(8,128)}, u32[]{:S(2)}) copy-start(f32[256,64,32]{0,1,2:T(8,128)} %fusion.16) | copy-start | bytes 6291460
  86.0 2.2 %copy-start.3 = (f32[256,64,32]{0,1,2:T(8,128)S(1)}, f32[256,64,32]{0,1,2:T(8,128)}, u32[]{:S(2)}) copy-start(f32[256,64,32]{0,1,2:T(8,128)} %fusion.8) | copy-start | bytes 6291460
  95.5 0.8 copy-start.6
  95.5 0.8 copy-start.8
  124.8 1.4 %copy-start.1 = (bf16[128,6144]{0,1:T(8,128)(2,1)S(1)}, bf16[128,6144]{0,1:T(8,128)(2,1)}, u32[]{:S(2)}) copy-start(bf16[128,6144]{0,1:T(8,128)(2,1)} %copy-done) | copy-start | bytes 4718596
  124.8 1.4 %copy-start.9 = (f32[2048]{0:T(1024)S(1)}, f32[2048]{0:T(1024)}, u32[]{:S(2)}) copy-start(f32[2048]{0:T(1024)} %param.7) | copy-start | bytes 24580

commit v11 on v10

--- a/solution.py
+++ b/solution.py
@@ -199,7 +199,9 @@
     spectra_imag = times(within_cos, twisted_imag) - times(within_sin, twisted_real)
     product_real = spectra_real * filter_real - spectra_imag * filter_imag
     product_imag = spectra_real * filter_imag + spectra_imag * filter_real
-    product = jnp.stack([product_real, product_imag]).reshape(2 * block_len, lanes)
+    product = jnp.concatenate(
+        [product_real.reshape(block_len, lanes), product_imag.reshape(block_len, lanes)], axis=0
+    ).astype(jnp.bfloat16)
 
     def inverse_part(left, right):
         return lax.dot_general(

time: 128 us -> 126 us (0.984)
  local copies, waits for them, and re-layouts: 20.9 us -> 19.1 us
    unnamed x24 -> x17, local copies, waits for them, and re-layouts: 10.1 us -> 9.49 us
  transfers between devices with their start and end apart: 3 -> 3, of which waited for: 2 -> 2; matrix products, arithmetic and copies ran while one was open for 21% -> 22% of each run, Pallas kernels for 0% -> 0%
where the time goes in v11:
time: 126 us
  waiting for transfers between devices  32 us (25%)
  blocking collectives  26.4 us (21%)
  matrix products  20.8 us (17%)
  local copies, waits for them, and re-layouts  19.1 us (15%)
  starting transfers between devices  14.1 us (11%)
  other arithmetic  12.7 us (10%)
    all_to_all x1, blocking collectives, channel_parallel(): lax.all_to_all(long_blocks, everyone, split_axis=0, concat_axis=0, tiled=...  26.4 us
    all_to_all x1, waiting for transfers between devices, channel_parallel(): lax.all_to_all(spectrum, 'ctx', split_axis=3, concat_axis=1, tiled=True)  23.7 us
    dot_general x4, matrix products, times(): lax.dot_general(table_part, data.reshape(block_len, lanes), (((1,), (0,))...  15.1 us
    unnamed x17, local copies, waits for them, and re-layouts  9.49 us
    all_to_all x1, waiting for transfers between devices, channel_parallel(): lax.all_to_all(outgoing, everyone, split_axis=1, concat_axis=0, tiled=True)  8.32 us
    all_to_all x1, starting transfers between devices, channel_parallel(): lax.all_to_all(outgoing, everyone, split_axis=1, concat_axis=0, tiled=True)  5.79 us
    convert_element_type x1, other arithmetic, short_convolution(): short = short.astype(jnp.bfloat16)  4.37 us
    all_to_all x1, starting transfers between devices, channel_parallel(): lax.all_to_all(spectrum, 'ctx', split_axis=3, concat_axis=1, tiled=True)  4.36 us
  transfers between devices with their start and end apart: 3, of which 2 were waited for; matrix products, arithmetic and copies ran while one was open for 22% of the time, Pallas kernels for 0%

profile of v11, /device:TPU:1, one launch (start us, length us, event | category | flops | bytes accessed | tf_op | source)
XLA Modules:
  0.0 125.5 jit_solution(15649562526108819712)
XLA Ops:
  0.0 0.9 slice.35
  0.9 3.9 %collective-permute-start = (bf16[2,6144]{1,0:T(2,128)(2,1)S(1)}, bf16[2,6144]{1,0:T(2,128)(2,1)S(1)}, u32[]{:S(2)}, u32[]{:S(2)}) collective-permute-start(bf16[2,6144]{1,0:T(2,128)(2,1)S(1)} %slice.35), channel_id=1, source_target_pairs={{0,1},{1,2},{2,3},{3,4},{4,5},{5,6},{6,7},{7,8},{8,9},{9,10},{10,1... | collective-permute-start | bytes 73736 | tf_op jit(solution)/shard_map/ppermute | solution.py:14
  4.9 1.1 fusion.126
  6.0 1.9 %copy.45 = bf16[128,6144]{0,1:T(8,128)(2,1)S(1)} copy(bf16[128,6144]{1,0:T(8,128)(2,1)} %param.5) | data formatting | bytes 3145728 | tf_op args[0]
  7.9 0.0 collective-permute-done
  7.9 0.9 copy.46
  8.8 4.4 %add_convert_fusion = bf16[128,6144]{0,1:T(8,128)(2,1)S(1)} fusion(bf16[128,6144]{0,1:T(8,128)(2,1)S(1)} %copy.45, bf16[2,6144]{0,1:T(8,128)(2,1)S(1)} %copy.46, f32[6144]{0:T(1024)S(1)} %bitcast.106, f32[6144]{0:T(1024)S(1)} %bitcast.107, f32[6144]{0:T(1024)S(1)} %bitcast.105), kind=kLoop, calls=%fused_computation.3 | loop fusion | flops 11796480 | bytes 3244032 | tf_op jit(solution)/shard_map/convert_element_type | solution.py:134
  13.2 0.0 copy-start
  13.2 1.2 copy-done
  14.4 0.0 copy-start.4
  14.4 0.1 fusion.40
  14.5 0.8 copy.48
  15.4 5.8 %all-to-all-start = ((bf16[128,32,64]{0,2,1:T(8,128)(2,1)}), bf16[128,32,64]{0,2,1:T(8,128)(2,1)S(1)}, u32[]{:S(2)}, u32[]{:S(2)}) async-start(bf16[128,32,64]{0,2,1:T(8,128)(2,1)} %bitcast.7), calls=%async_computation | async-start | bytes 1048576 | tf_op jit(solution)/shard_map/all_to_all | solution.py:163
  21.2 0.0 copy-done.4
  21.2 0.9 copy.50
  22.1 2.5 %copy.51 = bf16[2,256,1024]{1,0,2:T(2,128)(2,1)S(1)} copy(bf16[2,256,1024]{2,1,0:T(8,128)(2,1)} %param.9) | data formatting | bytes 2097152 | tf_op args[4]
  24.6 4.1 %pad_maximum_fusion = bf16[2,2,256,1024]{2,1,0,3:T(2,128)(2,1)} fusion(bf16[1,2,256,1024]{2,1,0,3:T(2,128)(2,1)S(1)} %bitcast.98, bf16[1,2,256,1024]{2,1,0,3:T(2,128)(2,1)S(1)} %bitcast.97), kind=kLoop, calls=%fused_computation.6 | loop fusion | flops 1048576 | bytes 4194304 | tf_op jit(solution)/shard_map/stack | solution.py:166
  28.7 8.3 %all-to-all-done = bf16[128,32,64]{0,2,1:T(8,128)(2,1)S(1)} async-done(((bf16[128,32,64]{0,2,1:T(8,128)(2,1)}), bf16[128,32,64]{0,2,1:T(8,128)(2,1)S(1)}, u32[]{:S(2)}, u32[]{:S(2)}) %all-to-all-start) | async-done | bytes 524320 | tf_op jit(solution)/shard_map/all_to_all | solution.py:163
  37.0 0.1 convert_bitcast_fusion.2
  37.1 0.6 copy.49
  37.7 0.3 reshape.100
  38.0 4.4 %all-to-all-start.1 = ((bf16[2,2,256,1024]{2,1,0,3:T(2,128)(2,1)}), bf16[2,2,256,1024]{2,1,0,3:T(2,128)(2,1)}, u32[]{:S(2)}, u32[]{:S(2)}) async-start(bf16[2,2,256,1024]{2,1,0,3:T(2,128)(2,1)} %pad_maximum_fusion), calls=%async_computation.1 | async-start | bytes 4194304 | tf_op jit(solution)/shard_map/all_to_all | solution.py:167
  42.4 0.1 fusion.70
  42.6 1.0 fusion.61
  43.6 1.7 %fusion.57 = (bf16[256,256]{1,0:T(8,128)(2,1)}, bf16[256,256]{1,0:T(8,128)(2,1)S(1)}) fusion(), kind=kLoop, calls=%fused_computation.67 | loop fusion | flops 1048576 | bytes 262144 | tf_op jit(solution)/shard_map/sin | solution.py:145
  45.3 1.1 fusion.76
  46.4 1.5 %add_bitcast_fusion = (f32[64,32,256]{2,1,0:T(8,128)S(1)}, f32[64,32,256]{2,1,0:T(8,128)S(1)}) fusion(f32[256,64,32]{0,2,1:T(8,128)S(1)} %fusion.76, f32[256,32]{0,1:T(8,128)S(1)} %get-tuple-element.16, f32[256,32]{0,1:T(8,128)S(1)} %get-tuple-element.17, f32[16,256,64]{1,0,2:T(8,128)S(1)} %reshape.100), kind=kOutput, calls=%fused_computation.19 | convolution fusion | flops 54008832 | bytes 7405568 | tf_op jit(solution)/shard_map/jpc,ja->pca/dot_general | solution.py:28
  47.9 4.3 %fusion.8 = f32[256,64,32]{0,1,2:T(8,128)} fusion(f32[64,32,256]{2,1,0:T(8,128)S(1)} %get-tuple-element.12), kind=kOutput, calls=%fused_computation.20 | convolution fusion | flops 806223872 | bytes 4194304 | tf_op jit(solution)/shard_map/dot_general | solution.py:187
  52.2 3.0 %fusion.10 = f32[256,64,32]{0,1,2:T(8,128)S(1)} fusion(f32[64,32,256]{2,1,0:T(8,128)S(1)} %get-tuple-element.12), kind=kOutput, calls=%fused_computation.22 | convolution fusion | flops 806223872 | bytes 4194304 | tf_op jit(solution)/shard_map/dot_general | solution.py:187
  55.2 4.4 %fusion.16 = f32[256,64,32]{0,1,2:T(8,128)} fusion(f32[256,64,32]{0,1,2:T(8,128)S(1)} %fusion.10, f32[64,32,256]{2,1,0:T(8,128)S(1)} %get-tuple-element.11), kind=kOutput, calls=%fused_computation.28 | convolution fusion | flops 806748160 | bytes 6291456 | tf_op jit(solution)/shard_map/dot_general | solution.py:187
  59.6 23.7 %all-to-all-done.1 = bf16[2,2,256,1024]{2,1,0,3:T(2,128)(2,1)} async-done(((bf16[2,2,256,1024]{2,1,0,3:T(2,128)(2,1)}), bf16[2,2,256,1024]{2,1,0,3:T(2,128)(2,1)}, u32[]{:S(2)}, u32[]{:S(2)}) %all-to-all-start.1) | async-done | bytes 2097184 | tf_op jit(solution)/shard_map/all_to_all | solution.py:167
  83.3 1.9 %copy.54 = bf16[2,2,256,1024]{2,3,1,0:T(8,128)(2,1)S(1)} copy(bf16[2,2,256,1024]{2,1,0,3:T(2,128)(2,1)} %all-to-all-done.1) | data formatting | bytes 4194304 | tf_op jit(solution)/shard_map/all_to_all | solution.py:167
  85.2 0.8 convert_bitcast_fusion
  85.9 0.0 copy-start.2
  85.9 0.0 copy-start.3
  86.0 0.5 copy.55
  86.5 1.1 copy-done.2
  87.5 0.6 copy-done.3
  88.2 3.3 %subtract_convert_fusion = (bf16[256,64,32]{0,1,2:T(8,128)(2,1)S(1)}, bf16[256,64,32]{0,1,2:T(8,128)(2,1)S(1)}) fusion(f32[256,64,32]{0,1,2:T(8,128)S(1)} %copy-done.2, f32[2,256,64,32]{1,2,3,0:T(8,128)S(1)} %bitcast.91, f32[256,64,32]{0,1,2:T(8,128)S(1)} %copy-done.3, f32[64,32,256]{2,1,0:T(8,128)S(1)} %get-tuple-element.11), kind=kOutput, calls=%fused_computation.17 | convolution fusion | flops 810942464 | bytes 12582912 | tf_op jit(solution)/shard_map/dot_general | solution.py:187
  91.5 0.0 copy-start.5
  91.5 0.6 copy.58
  92.1 0.6 copy.59
  92.7 0.0 copy-done.5
  92.7 0.7 fusion.29
  93.5 0.7 fusion.30
  94.2 0.8 fusion
  95.1 0.9 fusion.31
  95.9 0.2 convert_element_type.145
  96.1 0.2 copy.62
  96.3 26.4 %all_to_all.23 = bf16[32,128,64]{1,2,0:T(8,128)(2,1)S(1)} all-to-all(bf16[32,128,64]{1,2,0:T(8,128)(2,1)S(1)} %copy.62), channel_id=1, replica_groups=mesh['ctx'=16,'grp'=2] {'ctx','grp'}, dimensions={0} | all-to-all | bytes 1048576 | tf_op jit(solution)/shard_map/all_to_all | solution.py:224
  122.8 0.0 copy-start.1
  122.8 0.0 copy-start.6
  122.8 0.1 convert_bitcast_fusion.1
  122.9 0.1 copy.63
  123.0 1.2 copy-done.1
  124.2 0.0 copy-done.6
  124.2 0.3 fusion.35
  124.5 1.0 copy.64
Async XLA Ops:
  0.9 7.0 %collective-permute-start = (bf16[2,6144]{1,0:T(2,128)(2,1)S(1)}, bf16[2,6144]{1,0:T(2,128)(2,1)S(1)}, u32[]{:S(2)}, u32[]{:S(2)}) collective-permute-start(bf16[2,6144]{1,0:T(2,128)(2,1)S(1)} %slice.35), channel_id=1, source_target_pairs={{0,1},{1,2},{2,3},{3,4},{4,5},{5,6},{6,7},{7,8},{8,9},{9,10},{10,1... | collective-permute-start | bytes 73736 | tf_op jit(solution)/shard_map/ppermute | solution.py:14
  13.2 1.2 copy-start
  14.4 6.8 %copy-start.4 = (bf16[2,256,1024]{2,1,0:T(8,128)(2,1)S(1)}, bf16[2,256,1024]{2,1,0:T(8,128)(2,1)}, u32[]{:S(2)}) copy-start(bf16[2,256,1024]{2,1,0:T(8,128)(2,1)} %param.8) | copy-start | bytes 3145732
  15.4 21.6 %all-to-all-start = ((bf16[128,32,64]{0,2,1:T(8,128)(2,1)}), bf16[128,32,64]{0,2,1:T(8,128)(2,1)S(1)}, u32[]{:S(2)}, u32[]{:S(2)}) async-start(bf16[128,32,64]{0,2,1:T(8,128)(2,1)} %bitcast.7), calls=%async_computation | async-start | bytes 1048576 | tf_op jit(solution)/shard_map/all_to_all | solution.py:163
  38.0 45.2 %all-to-all-start.1 = ((bf16[2,2,256,1024]{2,1,0,3:T(2,128)(2,1)}), bf16[2,2,256,1024]{2,1,0,3:T(2,128)(2,1)}, u32[]{:S(2)}, u32[]{:S(2)}) async-start(bf16[2,2,256,1024]{2,1,0,3:T(2,128)(2,1)} %pad_maximum_fusion), calls=%async_computation.1 | async-start | bytes 4194304 | tf_op jit(solution)/shard_map/all_to_all | solution.py:167
  85.9 1.6 %copy-start.2 = (f32[256,64,32]{0,1,2:T(8,128)S(1)}, f32[256,64,32]{0,1,2:T(8,128)}, u32[]{:S(2)}) copy-start(f32[256,64,32]{0,1,2:T(8,128)} %fusion.16) | copy-start | bytes 6291460
  85.9 2.2 %copy-start.3 = (f32[256,64,32]{0,1,2:T(8,128)S(1)}, f32[256,64,32]{0,1,2:T(8,128)}, u32[]{:S(2)}) copy-start(f32[256,64,32]{0,1,2:T(8,128)} %fusion.8) | copy-start | bytes 6291460
  91.5 1.2 copy-start.5
  122.8 1.4 %copy-start.1 = (bf16[128,6144]{0,1:T(8,128)(2,1)S(1)}, bf16[128,6144]{0,1:T(8,128)(2,1)}, u32[]{:S(2)}) copy-start(bf16[128,6144]{0,1:T(8,128)(2,1)} %copy-done) | copy-start | bytes 4718596
  122.8 1.4 %copy-start.6 = (f32[2048]{0:T(1024)S(1)}, f32[2048]{0:T(1024)}, u32[]{:S(2)}) copy-start(f32[2048]{0:T(1024)} %param.7) | copy-start | bytes 24580

commit v12 on v11

--- a/solution.py
+++ b/solution.py
@@ -165,7 +165,7 @@
 
     tokens, spectrum = lax.optimization_barrier((tokens, jnp.stack([spectrum_real, spectrum_imag])))
     spectrum = lax.all_to_all(spectrum, "ctx", split_axis=3, concat_axis=1, tiled=True)
-    spectrum = spectrum.transpose(0, 2, 3, 1).astype(jnp.float32)
+    spectrum = spectrum.transpose(0, 2, 3, 1)
     filter_real, filter_imag = spectrum[0], spectrum[1]
 
     residue = jnp.arange(residues, dtype=jnp.int32)
@@ -197,6 +197,7 @@
 
     spectra_real = times(within_cos, twisted_real) + times(within_sin, twisted_imag)
     spectra_imag = times(within_cos, twisted_imag) - times(within_sin, twisted_real)
+    filter_real, filter_imag = filter_real.astype(jnp.float32), filter_imag.astype(jnp.float32)
     product_real = spectra_real * filter_real - spectra_imag * filter_imag
     product_imag = spectra_real * filter_imag + spectra_imag * filter_real
     product = jnp.concatenate(

time: 126 us -> 126 us (level)
  no operation moved by 1% of the time
where the time goes in v12:
time: 126 us; the launch traced here: 125 us
  waiting for transfers between devices  31.8 us (25%)
  blocking collectives  26.4 us (21%)
  matrix products  21.1 us (17%)
  local copies, waits for them, and re-layouts  19.4 us (15%)
  starting transfers between devices  14.1 us (11%)
  other arithmetic  12.2 us (10%)
    all_to_all x1, blocking collectives, channel_parallel(): lax.all_to_all(long_blocks, everyone, split_axis=0, concat_axis=0, tiled=...  26.4 us
    all_to_all x1, waiting for transfers between devices, channel_parallel(): lax.all_to_all(spectrum, 'ctx', split_axis=3, concat_axis=1, tiled=True)  23.5 us
    dot_general x4, matrix products, times(): lax.dot_general(table_part, data.reshape(block_len, lanes), (((1,), (0,))...  15.4 us
    unnamed x17, local copies, waits for them, and re-layouts  10.1 us
    all_to_all x1, waiting for transfers between devices, channel_parallel(): lax.all_to_all(outgoing, everyone, split_axis=1, concat_axis=0, tiled=True)  8.32 us
    all_to_all x1, starting transfers between devices, channel_parallel(): lax.all_to_all(outgoing, everyone, split_axis=1, concat_axis=0, tiled=True)  5.79 us
    convert_element_type x1, other arithmetic, short_convolution(): short = short.astype(jnp.bfloat16)  4.37 us
    all_to_all x1, starting transfers between devices, channel_parallel(): lax.all_to_all(spectrum, 'ctx', split_axis=3, concat_axis=1, tiled=True)  4.36 us
  transfers between devices with their start and end apart: 3, of which 2 were waited for; matrix products, arithmetic and copies ran while one was open for 22% of the time, Pallas kernels for 0%

profile of v12, /device:TPU:1, one launch (start us, length us, event | category | flops | bytes accessed | tf_op | source)
XLA Modules:
  0.0 125.2 jit_solution(9151838597723843794)
XLA Ops:
  0.0 0.9 slice.35
  0.9 3.9 %collective-permute-start = (bf16[2,6144]{1,0:T(2,128)(2,1)S(1)}, bf16[2,6144]{1,0:T(2,128)(2,1)S(1)}, u32[]{:S(2)}, u32[]{:S(2)}) collective-permute-start(bf16[2,6144]{1,0:T(2,128)(2,1)S(1)} %slice.35), channel_id=1, source_target_pairs={{0,1},{1,2},{2,3},{3,4},{4,5},{5,6},{6,7},{7,8},{8,9},{9,10},{10,1... | collective-permute-start | bytes 73736 | tf_op jit(solution)/shard_map/ppermute | solution.py:14
  4.9 1.1 fusion.130
  6.0 1.9 %copy.45 = bf16[128,6144]{0,1:T(8,128)(2,1)S(1)} copy(bf16[128,6144]{1,0:T(8,128)(2,1)} %param.5) | data formatting | bytes 3145728 | tf_op args[0]
  7.9 0.0 collective-permute-done
  7.9 0.9 copy.46
  8.8 4.4 %add_convert_fusion = bf16[128,6144]{0,1:T(8,128)(2,1)S(1)} fusion(bf16[128,6144]{0,1:T(8,128)(2,1)S(1)} %copy.45, bf16[2,6144]{0,1:T(8,128)(2,1)S(1)} %copy.46, f32[6144]{0:T(1024)S(1)} %bitcast.107, f32[6144]{0:T(1024)S(1)} %bitcast.108, f32[6144]{0:T(1024)S(1)} %bitcast.106), kind=kLoop, calls=%fused_computation.2 | loop fusion | flops 11796480 | bytes 3244032 | tf_op jit(solution)/shard_map/convert_element_type | solution.py:134
  13.2 0.0 copy-start
  13.2 1.2 copy-done
  14.4 0.0 copy-start.4
  14.4 0.1 fusion.44
  14.5 0.8 copy.48
  15.4 5.8 %all-to-all-start = ((bf16[128,32,64]{0,2,1:T(8,128)(2,1)}), bf16[128,32,64]{0,2,1:T(8,128)(2,1)S(1)}, u32[]{:S(2)}, u32[]{:S(2)}) async-start(bf16[128,32,64]{0,2,1:T(8,128)(2,1)} %bitcast.7), calls=%async_computation | async-start | bytes 1048576 | tf_op jit(solution)/shard_map/all_to_all | solution.py:163
  21.2 0.0 copy-done.4
  21.2 0.9 copy.50
  22.1 2.5 %copy.51 = bf16[2,256,1024]{1,0,2:T(2,128)(2,1)S(1)} copy(bf16[2,256,1024]{2,1,0:T(8,128)(2,1)} %param.9) | data formatting | bytes 2097152 | tf_op args[4]
  24.6 4.1 %pad_maximum_fusion = bf16[2,2,256,1024]{2,1,0,3:T(2,128)(2,1)} fusion(bf16[1,2,256,1024]{2,1,0,3:T(2,128)(2,1)S(1)} %bitcast.99, bf16[1,2,256,1024]{2,1,0,3:T(2,128)(2,1)S(1)} %bitcast.98), kind=kLoop, calls=%fused_computation.11 | loop fusion | flops 1048576 | bytes 4194304 | tf_op jit(solution)/shard_map/stack | solution.py:166
  28.7 8.3 %all-to-all-done = bf16[128,32,64]{0,2,1:T(8,128)(2,1)S(1)} async-done(((bf16[128,32,64]{0,2,1:T(8,128)(2,1)}), bf16[128,32,64]{0,2,1:T(8,128)(2,1)S(1)}, u32[]{:S(2)}, u32[]{:S(2)}) %all-to-all-start) | async-done | bytes 524320 | tf_op jit(solution)/shard_map/all_to_all | solution.py:163
  37.0 0.1 convert_bitcast_fusion.1
  37.1 0.6 copy.49
  37.7 0.3 reshape.100
  38.0 4.4 %all-to-all-start.1 = ((bf16[2,2,256,1024]{2,1,0,3:T(2,128)(2,1)}), bf16[2,2,256,1024]{2,1,0,3:T(2,128)(2,1)}, u32[]{:S(2)}, u32[]{:S(2)}) async-start(bf16[2,2,256,1024]{2,1,0,3:T(2,128)(2,1)} %pad_maximum_fusion), calls=%async_computation.1 | async-start | bytes 4194304 | tf_op jit(solution)/shard_map/all_to_all | solution.py:167
  42.4 0.1 fusion.74
  42.6 1.7 %fusion.65 = bf16[256,256]{1,0:T(8,128)(2,1)} fusion(), kind=kLoop, calls=%fused_computation.74 | loop fusion | flops 1048576 | bytes 131072 | tf_op jit(solution)/shard_map/neg | solution.py:216
  44.2 1.3 %fusion.61 = (bf16[256,256]{1,0:T(8,128)(2,1)S(1)}, bf16[256,256]{1,0:T(8,128)(2,1)S(1)}) fusion(), kind=kLoop, calls=%fused_computation.72 | loop fusion | flops 1048576 | bytes 262144 | tf_op jit(solution)/shard_map/sin | solution.py:145
  45.5 1.1 fusion.80
  46.6 1.5 %add_bitcast_fusion = (f32[64,32,256]{2,1,0:T(8,128)S(1)}, f32[64,32,256]{2,1,0:T(8,128)S(1)}) fusion(f32[256,64,32]{0,2,1:T(8,128)S(1)} %fusion.80, f32[256,32]{0,1:T(8,128)S(1)} %get-tuple-element.16, f32[256,32]{0,1:T(8,128)S(1)} %get-tuple-element.17, f32[16,256,64]{1,0,2:T(8,128)S(1)} %reshape.100), kind=kOutput, calls=%fused_computation.22 | convolution fusion | flops 54008832 | bytes 7405568 | tf_op jit(solution)/shard_map/jpc,ja->pca/dot_general | solution.py:28
  48.1 3.0 %fusion.14 = f32[256,64,32]{0,1,2:T(8,128)S(1)} fusion(f32[64,32,256]{2,1,0:T(8,128)S(1)} %get-tuple-element.12), kind=kOutput, calls=%fused_computation.25 | convolution fusion | flops 806223872 | bytes 4194304 | tf_op jit(solution)/shard_map/dot_general | solution.py:187
  51.1 4.3 %fusion.12 = f32[256,64,32]{0,1,2:T(8,128)} fusion(f32[64,32,256]{2,1,0:T(8,128)S(1)} %get-tuple-element.12), kind=kOutput, calls=%fused_computation.23 | convolution fusion | flops 806223872 | bytes 4194304 | tf_op jit(solution)/shard_map/dot_general | solution.py:187
  55.4 4.4 %fusion.20 = f32[256,64,32]{0,1,2:T(8,128)} fusion(f32[256,64,32]{0,1,2:T(8,128)S(1)} %fusion.14, f32[64,32,256]{2,1,0:T(8,128)S(1)} %get-tuple-element.11), kind=kOutput, calls=%fused_computation.31 | convolution fusion | flops 806748160 | bytes 6291456 | tf_op jit(solution)/shard_map/dot_general | solution.py:187
  59.8 23.5 %all-to-all-done.1 = bf16[2,2,256,1024]{2,1,0,3:T(2,128)(2,1)} async-done(((bf16[2,2,256,1024]{2,1,0,3:T(2,128)(2,1)}), bf16[2,2,256,1024]{2,1,0,3:T(2,128)(2,1)}, u32[]{:S(2)}, u32[]{:S(2)}) %all-to-all-start.1) | async-done | bytes 2097184 | tf_op jit(solution)/shard_map/all_to_all | solution.py:167
  83.3 1.9 %copy.54 = bf16[2,2,256,1024]{2,3,1,0:T(8,128)(2,1)S(1)} copy(bf16[2,2,256,1024]{2,1,0,3:T(2,128)(2,1)} %all-to-all-done.1) | data formatting | bytes 4194304 | tf_op jit(solution)/shard_map/all_to_all | solution.py:167
  85.2 0.2 copy-start.2
  85.4 0.0 copy-start.3
  85.4 0.1 copy.55
  85.5 1.4 %copy-done.2 = f32[256,64,32]{0,1,2:T(8,128)S(1)} copy-done((f32[256,64,32]{0,1,2:T(8,128)S(1)}, f32[256,64,32]{0,1,2:T(8,128)}, u32[]{:S(2)}) %copy-start.2) | copy-done | bytes 2097176
  87.0 0.6 copy-done.3
  87.6 3.6 %fusion.1 = (bf16[256,64,32]{0,1,2:T(8,128)(2,1)S(1)}, bf16[256,64,32]{0,1,2:T(8,128)(2,1)S(1)}) fusion(f32[256,64,32]{0,1,2:T(8,128)S(1)} %copy-done.2, bf16[2,256,64,32]{1,2,3,0:T(8,128)(2,1)S(1)} %bitcast.97, f32[256,64,32]{0,1,2:T(8,128)S(1)} %copy-done.3, f32[64,32,256]{2,1,0:T(8,128)S(1)} %get-tuple-element.11), kind=kOutput, calls=%fused_computation.8 | convolution fusion | flops 811991040 | bytes 10485760 | tf_op jit(solution)/shard_map/dot_general | solution.py:187
  91.2 0.0 copy-start.5
  91.2 0.6 copy.58
  91.8 0.6 copy.59
  92.4 0.0 copy-done.5
  92.4 0.7 fusion.34
  93.2 0.7 fusion.33
  93.9 0.8 fusion.4
  94.8 0.9 fusion.35
  95.7 0.2 convert_element_type.141
  95.9 0.2 copy.62
  96.1 26.4 %all_to_all.32 = bf16[32,128,64]{1,2,0:T(8,128)(2,1)S(1)} all-to-all(bf16[32,128,64]{1,2,0:T(8,128)(2,1)S(1)} %copy.62), channel_id=1, replica_groups=mesh['ctx'=16,'grp'=2] {'ctx','grp'}, dimensions={0} | all-to-all | bytes 1048576 | tf_op jit(solution)/shard_map/all_to_all | solution.py:225
  122.5 0.0 copy-start.1
  122.5 0.0 copy-start.6
  122.5 0.1 convert_bitcast_fusion
  122.6 0.1 copy.63
  122.7 1.2 copy-done.1
  123.9 0.0 copy-done.6
  123.9 0.3 fusion.39
  124.2 1.0 copy.64
Async XLA Ops:
  0.9 7.0 %collective-permute-start = (bf16[2,6144]{1,0:T(2,128)(2,1)S(1)}, bf16[2,6144]{1,0:T(2,128)(2,1)S(1)}, u32[]{:S(2)}, u32[]{:S(2)}) collective-permute-start(bf16[2,6144]{1,0:T(2,128)(2,1)S(1)} %slice.35), channel_id=1, source_target_pairs={{0,1},{1,2},{2,3},{3,4},{4,5},{5,6},{6,7},{7,8},{8,9},{9,10},{10,1... | collective-permute-start | bytes 73736 | tf_op jit(solution)/shard_map/ppermute | solution.py:14
  13.2 1.2 copy-start
  14.4 6.8 %copy-start.4 = (bf16[2,256,1024]{2,1,0:T(8,128)(2,1)S(1)}, bf16[2,256,1024]{2,1,0:T(8,128)(2,1)}, u32[]{:S(2)}) copy-start(bf16[2,256,1024]{2,1,0:T(8,128)(2,1)} %param.8) | copy-start | bytes 3145732
  15.4 21.6 %all-to-all-start = ((bf16[128,32,64]{0,2,1:T(8,128)(2,1)}), bf16[128,32,64]{0,2,1:T(8,128)(2,1)S(1)}, u32[]{:S(2)}, u32[]{:S(2)}) async-start(bf16[128,32,64]{0,2,1:T(8,128)(2,1)} %bitcast.7), calls=%async_computation | async-start | bytes 1048576 | tf_op jit(solution)/shard_map/all_to_all | solution.py:163
  38.0 45.2 %all-to-all-start.1 = ((bf16[2,2,256,1024]{2,1,0,3:T(2,128)(2,1)}), bf16[2,2,256,1024]{2,1,0,3:T(2,128)(2,1)}, u32[]{:S(2)}, u32[]{:S(2)}) async-start(bf16[2,2,256,1024]{2,1,0,3:T(2,128)(2,1)} %pad_maximum_fusion), calls=%async_computation.1 | async-start | bytes 4194304 | tf_op jit(solution)/shard_map/all_to_all | solution.py:167
  85.2 1.8 %copy-start.2 = (f32[256,64,32]{0,1,2:T(8,128)S(1)}, f32[256,64,32]{0,1,2:T(8,128)}, u32[]{:S(2)}) copy-start(f32[256,64,32]{0,1,2:T(8,128)} %fusion.20) | copy-start | bytes 6291460
  85.4 2.2 %copy-start.3 = (f32[256,64,32]{0,1,2:T(8,128)S(1)}, f32[256,64,32]{0,1,2:T(8,128)}, u32[]{:S(2)}) copy-start(f32[256,64,32]{0,1,2:T(8,128)} %fusion.12) | copy-start | bytes 6291460
  91.2 1.2 copy-start.5
  122.5 1.4 %copy-start.1 = (bf16[128,6144]{0,1:T(8,128)(2,1)S(1)}, bf16[128,6144]{0,1:T(8,128)(2,1)}, u32[]{:S(2)}) copy-start(bf16[128,6144]{0,1:T(8,128)(2,1)} %copy-done) | copy-start | bytes 4718596
  122.5 1.4 %copy-start.6 = (f32[2048]{0:T(1024)S(1)}, f32[2048]{0:T(1024)}, u32[]{:S(2)}) copy-start(f32[2048]{0:T(1024)} %param.7) | copy-start | bytes 24580

commit v13 on v11

--- a/solution.py
+++ b/solution.py
@@ -216,8 +216,8 @@
     restored_imag = inverse_part(within_sin, within_cos)
     unturned_real = restored_real * turn_cos - restored_imag * turn_sin
     unturned_imag = restored_real * turn_sin + restored_imag * turn_cos
-    long_blocks = contract_high("ja,pca->jpc", across_cos, unturned_real) - contract_high(
-        "ja,pca->jpc", across_sin, unturned_imag
+    long_blocks = contract("ja,pca->jpc", across_cos, unturned_real, lax.Precision.DEFAULT) - contract(
+        "ja,pca->jpc", across_sin, unturned_imag, lax.Precision.DEFAULT
     )
     long_blocks = (long_blocks * (1.0 / fft_len)).reshape(devices, row_count, width)
     long_blocks = long_blocks.astype(jnp.bfloat16)

time: 126 us -> 125 us (level)
  no operation moved by 1% of the time
where the time goes in v13:
time: 125 us
  waiting for transfers between devices  32 us (26%)
  blocking collectives  26.4 us (21%)
  matrix products  20.1 us (16%)
  local copies, waits for them, and re-layouts  19.1 us (15%)
  starting transfers between devices  14.1 us (11%)
  other arithmetic  12.7 us (10%)
    all_to_all x1, blocking collectives, channel_parallel(): lax.all_to_all(long_blocks, everyone, split_axis=0, concat_axis=0, tiled=...  26.4 us
    all_to_all x1, waiting for transfers between devices, channel_parallel(): lax.all_to_all(spectrum, 'ctx', split_axis=3, concat_axis=1, tiled=True)  23.7 us
    dot_general x4, matrix products, times(): lax.dot_general(table_part, data.reshape(block_len, lanes), (((1,), (0,))...  15.1 us
    unnamed x17, local copies, waits for them, and re-layouts  9.49 us
    all_to_all x1, waiting for transfers between devices, channel_parallel(): lax.all_to_all(outgoing, everyone, split_axis=1, concat_axis=0, tiled=True)  8.32 us
    all_to_all x1, starting transfers between devices, channel_parallel(): lax.all_to_all(outgoing, everyone, split_axis=1, concat_axis=0, tiled=True)  5.79 us
    convert_element_type x1, other arithmetic, short_convolution(): short = short.astype(jnp.bfloat16)  4.37 us
    all_to_all x1, starting transfers between devices, channel_parallel(): lax.all_to_all(spectrum, 'ctx', split_axis=3, concat_axis=1, tiled=True)  4.36 us
  transfers between devices with their start and end apart: 3, of which 2 were waited for; matrix products, arithmetic and copies ran while one was open for 22% of the time, Pallas kernels for 0%

profile of v13, /device:TPU:1, one launch (start us, length us, event | category | flops | bytes accessed | tf_op | source)
XLA Modules:
  0.0 124.7 jit_solution(11158492230343737274)
XLA Ops:
  0.0 0.9 slice.35
  0.9 3.9 %collective-permute-start = (bf16[2,6144]{1,0:T(2,128)(2,1)S(1)}, bf16[2,6144]{1,0:T(2,128)(2,1)S(1)}, u32[]{:S(2)}, u32[]{:S(2)}) collective-permute-start(bf16[2,6144]{1,0:T(2,128)(2,1)S(1)} %slice.35), channel_id=1, source_target_pairs={{0,1},{1,2},{2,3},{3,4},{4,5},{5,6},{6,7},{7,8},{8,9},{9,10},{10,1... | collective-permute-start | bytes 73736 | tf_op jit(solution)/shard_map/ppermute | solution.py:14
  4.9 1.1 fusion.126
  6.0 1.9 %copy.45 = bf16[128,6144]{0,1:T(8,128)(2,1)S(1)} copy(bf16[128,6144]{1,0:T(8,128)(2,1)} %param.5) | data formatting | bytes 3145728 | tf_op args[0]
  7.9 0.0 collective-permute-done
  7.9 0.9 copy.46
  8.8 4.4 %add_convert_fusion = bf16[128,6144]{0,1:T(8,128)(2,1)S(1)} fusion(bf16[128,6144]{0,1:T(8,128)(2,1)S(1)} %copy.45, bf16[2,6144]{0,1:T(8,128)(2,1)S(1)} %copy.46, f32[6144]{0:T(1024)S(1)} %bitcast.106, f32[6144]{0:T(1024)S(1)} %bitcast.107, f32[6144]{0:T(1024)S(1)} %bitcast.105), kind=kLoop, calls=%fused_computation.3 | loop fusion | flops 11796480 | bytes 3244032 | tf_op jit(solution)/shard_map/convert_element_type | solution.py:134
  13.2 0.0 copy-start
  13.2 1.2 copy-done
  14.4 0.0 copy-start.4
  14.4 0.1 fusion.40
  14.5 0.8 copy.48
  15.4 5.8 %all-to-all-start = ((bf16[128,32,64]{0,2,1:T(8,128)(2,1)}), bf16[128,32,64]{0,2,1:T(8,128)(2,1)S(1)}, u32[]{:S(2)}, u32[]{:S(2)}) async-start(bf16[128,32,64]{0,2,1:T(8,128)(2,1)} %bitcast.7), calls=%async_computation | async-start | bytes 1048576 | tf_op jit(solution)/shard_map/all_to_all | solution.py:163
  21.2 0.0 copy-done.4
  21.2 0.9 copy.50
  22.1 2.5 %copy.51 = bf16[2,256,1024]{1,0,2:T(2,128)(2,1)S(1)} copy(bf16[2,256,1024]{2,1,0:T(8,128)(2,1)} %param.9) | data formatting | bytes 2097152 | tf_op args[4]
  24.6 4.1 %pad_maximum_fusion = bf16[2,2,256,1024]{2,1,0,3:T(2,128)(2,1)} fusion(bf16[1,2,256,1024]{2,1,0,3:T(2,128)(2,1)S(1)} %bitcast.98, bf16[1,2,256,1024]{2,1,0,3:T(2,128)(2,1)S(1)} %bitcast.97), kind=kLoop, calls=%fused_computation.6 | loop fusion | flops 1048576 | bytes 4194304 | tf_op jit(solution)/shard_map/stack | solution.py:166
  28.7 8.3 %all-to-all-done = bf16[128,32,64]{0,2,1:T(8,128)(2,1)S(1)} async-done(((bf16[128,32,64]{0,2,1:T(8,128)(2,1)}), bf16[128,32,64]{0,2,1:T(8,128)(2,1)S(1)}, u32[]{:S(2)}, u32[]{:S(2)}) %all-to-all-start) | async-done | bytes 524320 | tf_op jit(solution)/shard_map/all_to_all | solution.py:163
  37.0 0.1 convert_bitcast_fusion.2
  37.1 0.6 copy.49
  37.7 0.3 reshape.100
  38.0 4.4 %all-to-all-start.1 = ((bf16[2,2,256,1024]{2,1,0,3:T(2,128)(2,1)}), bf16[2,2,256,1024]{2,1,0,3:T(2,128)(2,1)}, u32[]{:S(2)}, u32[]{:S(2)}) async-start(bf16[2,2,256,1024]{2,1,0,3:T(2,128)(2,1)} %pad_maximum_fusion), calls=%async_computation.1 | async-start | bytes 4194304 | tf_op jit(solution)/shard_map/all_to_all | solution.py:167
  42.4 0.1 fusion.70
  42.6 1.0 fusion.61
  43.6 1.7 %fusion.57 = (bf16[256,256]{1,0:T(8,128)(2,1)}, bf16[256,256]{1,0:T(8,128)(2,1)S(1)}) fusion(), kind=kLoop, calls=%fused_computation.67 | loop fusion | flops 1048576 | bytes 262144 | tf_op jit(solution)/shard_map/sin | solution.py:145
  45.3 1.1 fusion.76
  46.4 1.5 %add_bitcast_fusion = (f32[64,32,256]{2,1,0:T(8,128)S(1)}, f32[64,32,256]{2,1,0:T(8,128)S(1)}) fusion(f32[256,64,32]{0,2,1:T(8,128)S(1)} %fusion.76, f32[256,32]{0,1:T(8,128)S(1)} %get-tuple-element.16, f32[256,32]{0,1:T(8,128)S(1)} %get-tuple-element.17, f32[16,256,64]{1,0,2:T(8,128)S(1)} %reshape.100), kind=kOutput, calls=%fused_computation.19 | convolution fusion | flops 54008832 | bytes 7405568 | tf_op jit(solution)/shard_map/jpc,ja->pca/dot_general | solution.py:28
  47.9 4.3 %fusion.8 = f32[256,64,32]{0,1,2:T(8,128)} fusion(f32[64,32,256]{2,1,0:T(8,128)S(1)} %get-tuple-element.12), kind=kOutput, calls=%fused_computation.20 | convolution fusion | flops 806223872 | bytes 4194304 | tf_op jit(solution)/shard_map/dot_general | solution.py:187
  52.2 3.0 %fusion.10 = f32[256,64,32]{0,1,2:T(8,128)S(1)} fusion(f32[64,32,256]{2,1,0:T(8,128)S(1)} %get-tuple-element.12), kind=kOutput, calls=%fused_computation.22 | convolution fusion | flops 806223872 | bytes 4194304 | tf_op jit(solution)/shard_map/dot_general | solution.py:187
  55.2 4.4 %fusion.16 = f32[256,64,32]{0,1,2:T(8,128)} fusion(f32[256,64,32]{0,1,2:T(8,128)S(1)} %fusion.10, f32[64,32,256]{2,1,0:T(8,128)S(1)} %get-tuple-element.11), kind=kOutput, calls=%fused_computation.28 | convolution fusion | flops 806748160 | bytes 6291456 | tf_op jit(solution)/shard_map/dot_general | solution.py:187
  59.6 23.7 %all-to-all-done.1 = bf16[2,2,256,1024]{2,1,0,3:T(2,128)(2,1)} async-done(((bf16[2,2,256,1024]{2,1,0,3:T(2,128)(2,1)}), bf16[2,2,256,1024]{2,1,0,3:T(2,128)(2,1)}, u32[]{:S(2)}, u32[]{:S(2)}) %all-to-all-start.1) | async-done | bytes 2097184 | tf_op jit(solution)/shard_map/all_to_all | solution.py:167
  83.3 1.9 %copy.54 = bf16[2,2,256,1024]{2,3,1,0:T(8,128)(2,1)S(1)} copy(bf16[2,2,256,1024]{2,1,0,3:T(2,128)(2,1)} %all-to-all-done.1) | data formatting | bytes 4194304 | tf_op jit(solution)/shard_map/all_to_all | solution.py:167
  85.2 0.8 convert_bitcast_fusion
  85.9 0.0 copy-start.2
  85.9 0.0 copy-start.3
  86.0 0.5 copy.55
  86.5 1.1 copy-done.2
  87.5 0.6 copy-done.3
  88.2 3.3 %subtract_convert_fusion = (bf16[256,64,32]{0,1,2:T(8,128)(2,1)S(1)}, bf16[256,64,32]{0,1,2:T(8,128)(2,1)S(1)}) fusion(f32[256,64,32]{0,1,2:T(8,128)S(1)} %copy-done.2, f32[2,256,64,32]{1,2,3,0:T(8,128)S(1)} %bitcast.91, f32[256,64,32]{0,1,2:T(8,128)S(1)} %copy-done.3, f32[64,32,256]{2,1,0:T(8,128)S(1)} %get-tuple-element.11), kind=kOutput, calls=%fused_computation.17 | convolution fusion | flops 810942464 | bytes 12582912 | tf_op jit(solution)/shard_map/dot_general | solution.py:187
  91.5 0.0 copy-start.5
  91.5 0.6 copy.58
  92.1 0.6 copy.59
  92.7 0.0 copy-done.5
  92.7 0.7 fusion.29
  93.5 0.7 fusion.30
  94.2 0.4 fusion
  94.7 0.5 fusion.31
  95.1 0.2 convert_element_type.145
  95.3 0.2 copy.62
  95.5 26.4 %all_to_all.23 = bf16[32,128,64]{1,2,0:T(8,128)(2,1)S(1)} all-to-all(bf16[32,128,64]{1,2,0:T(8,128)(2,1)S(1)} %copy.62), channel_id=1, replica_groups=mesh['ctx'=16,'grp'=2] {'ctx','grp'}, dimensions={0} | all-to-all | bytes 1048576 | tf_op jit(solution)/shard_map/all_to_all | solution.py:224
  122.0 0.0 copy-start.1
  122.0 0.0 copy-start.6
  122.0 0.1 convert_bitcast_fusion.1
  122.1 0.1 copy.63
  122.2 1.2 copy-done.1
  123.4 0.0 copy-done.6
  123.4 0.3 fusion.35
  123.7 1.0 copy.64
Async XLA Ops:
  0.9 7.0 %collective-permute-start = (bf16[2,6144]{1,0:T(2,128)(2,1)S(1)}, bf16[2,6144]{1,0:T(2,128)(2,1)S(1)}, u32[]{:S(2)}, u32[]{:S(2)}) collective-permute-start(bf16[2,6144]{1,0:T(2,128)(2,1)S(1)} %slice.35), channel_id=1, source_target_pairs={{0,1},{1,2},{2,3},{3,4},{4,5},{5,6},{6,7},{7,8},{8,9},{9,10},{10,1... | collective-permute-start | bytes 73736 | tf_op jit(solution)/shard_map/ppermute | solution.py:14
  13.2 1.2 copy-start
  14.4 6.8 %copy-start.4 = (bf16[2,256,1024]{2,1,0:T(8,128)(2,1)S(1)}, bf16[2,256,1024]{2,1,0:T(8,128)(2,1)}, u32[]{:S(2)}) copy-start(bf16[2,256,1024]{2,1,0:T(8,128)(2,1)} %param.8) | copy-start | bytes 3145732
  15.4 21.6 %all-to-all-start = ((bf16[128,32,64]{0,2,1:T(8,128)(2,1)}), bf16[128,32,64]{0,2,1:T(8,128)(2,1)S(1)}, u32[]{:S(2)}, u32[]{:S(2)}) async-start(bf16[128,32,64]{0,2,1:T(8,128)(2,1)} %bitcast.7), calls=%async_computation | async-start | bytes 1048576 | tf_op jit(solution)/shard_map/all_to_all | solution.py:163
  38.0 45.2 %all-to-all-start.1 = ((bf16[2,2,256,1024]{2,1,0,3:T(2,128)(2,1)}), bf16[2,2,256,1024]{2,1,0,3:T(2,128)(2,1)}, u32[]{:S(2)}, u32[]{:S(2)}) async-start(bf16[2,2,256,1024]{2,1,0,3:T(2,128)(2,1)} %pad_maximum_fusion), calls=%async_computation.1 | async-start | bytes 4194304 | tf_op jit(solution)/shard_map/all_to_all | solution.py:167
  85.9 1.6 %copy-start.2 = (f32[256,64,32]{0,1,2:T(8,128)S(1)}, f32[256,64,32]{0,1,2:T(8,128)}, u32[]{:S(2)}) copy-start(f32[256,64,32]{0,1,2:T(8,128)} %fusion.16) | copy-start | bytes 6291460
  85.9 2.2 %copy-start.3 = (f32[256,64,32]{0,1,2:T(8,128)S(1)}, f32[256,64,32]{0,1,2:T(8,128)}, u32[]{:S(2)}) copy-start(f32[256,64,32]{0,1,2:T(8,128)} %fusion.8) | copy-start | bytes 6291460
  91.5 1.2 copy-start.5
  122.0 1.4 %copy-start.1 = (bf16[128,6144]{0,1:T(8,128)(2,1)S(1)}, bf16[128,6144]{0,1:T(8,128)(2,1)}, u32[]{:S(2)}) copy-start(bf16[128,6144]{0,1:T(8,128)(2,1)} %copy-done) | copy-start | bytes 4718596
  122.0 1.4 %copy-start.6 = (f32[2048]{0:T(1024)S(1)}, f32[2048]{0:T(1024)}, u32[]{:S(2)}) copy-start(f32[2048]{0:T(1024)} %param.7) | copy-start | bytes 24580
